TPU v7x, 256 devices: a whole 4x4x8 slice. The times are simulated.
256 devices in a mesh: rows: 16 (over x, y), sub: 16 (over z, core).
Axes of the slice: x: 4, y: 4, z: 8, core: 2. Of those that a mesh axis runs over, the one named last changes fastest.
Arguments:
- embeddings: bfloat16 [65536, 1024], P(('rows', 'sub'))
- codes: int32 [64, 65536], P(None, ('rows', 'sub')), may hold values from 0 to 255
- codebook: bfloat16 [256, 1024], P(None, 'sub'), may hold values from -6 to 6
Outputs:
- rotation: float32 [1024, 1024], P('sub')
- rotated: bfloat16 [65536, 1024], P(('rows', 'sub'))
- new_codebook: float32 [256, 1024], P(None, 'sub')
All inputs are finite; a program needn't handle non-finite values.
Results may differ from a plain program's by a relative error of at most 0.0095.
Values may be sent and summed in bfloat16 or wider, within the bound.
No kernel may reach another device: no remote copies, remote signals or barrier semaphores. Data moves between devices by JAX's collectives and lax.ppermute only.
A program may use at most 64 MiB of HBM per device.

v0:
```python
import math

import jax
import jax.numpy as jnp
from jax import lax
from jax.sharding import PartitionSpec as P

NS_STEPS = 3


coef_a = 3.4445
coef_b = -4.775
coef_c = 2.0315
frob_eps = 1e-07
highest = lax.Precision.HIGHEST


def rows_dot(left, right):
    return lax.dot_general(
        left, right, (((1,), (1,)), ((), ())), precision=highest, preferred_element_type=jnp.float32
    )


def one_hot_codes(code_block, count_codes):
    levels = lax.broadcasted_iota(jnp.int32, code_block.shape + (count_codes,), 2)
    return (code_block[:, :, None] == levels).astype(jnp.bfloat16)


def decode_rows(codes, table):
    subspaces, local_rows = codes.shape
    count_codes, row_width = table.shape
    sub_width = row_width // subspaces
    block_rows = math.gcd(local_rows, 32768 // subspaces)
    blocks = local_rows // block_rows
    codewords = table.reshape(count_codes, subspaces, sub_width)
    code_blocks = codes.reshape(subspaces, blocks, block_rows).transpose(1, 0, 2)

    def decode_block(unused, code_block):
        one_hot = one_hot_codes(code_block, count_codes)
        picked = jnp.einsum("mnk,kmj->nmj", one_hot, codewords, preferred_element_type=jnp.float32)
        return (unused, picked.reshape(block_rows, row_width).astype(jnp.bfloat16))

    unused, decoded = lax.scan(decode_block, jnp.zeros((), jnp.float32), code_blocks)
    return decoded.reshape(local_rows, row_width)


def codeword_totals(codes, row_values, count_codes):
    subspaces, total_rows = codes.shape
    row_width = row_values.shape[1]
    sub_width = row_width // subspaces
    block_rows = math.gcd(total_rows, 32768 // subspaces)
    blocks = total_rows // block_rows
    code_blocks = codes.reshape(subspaces, blocks, block_rows).transpose(1, 0, 2)
    row_blocks = row_values.reshape(blocks, block_rows, subspaces, sub_width)

    def accumulate(running, pieces):
        one_hot = one_hot_codes(pieces[0], count_codes)
        block_sums = jnp.einsum(
            "mnk,nmj->kmj", one_hot, pieces[1], preferred_element_type=jnp.float32
        )
        block_counts = jnp.sum(one_hot, axis=1, dtype=jnp.float32).T
        return ((running[0] + block_sums, running[1] + block_counts), None)

    initial = (
        jnp.zeros((count_codes, subspaces, sub_width), jnp.float32),
        jnp.zeros((count_codes, subspaces), jnp.float32),
    )
    (code_sums, counts), unused = lax.scan(accumulate, initial, (code_blocks, row_blocks))
    return (code_sums.reshape(count_codes, row_width), counts)


def newton_panel(panel, whole):
    gram_rows = rows_dot(panel, whole)
    quartic = rows_dot(
        jnp.dot(gram_rows, whole, precision=highest, preferred_element_type=jnp.float32), whole
    )
    mixer = coef_b * gram_rows + coef_c * quartic
    return coef_a * panel + jnp.dot(
        mixer, whole, precision=highest, preferred_element_type=jnp.float32
    )


def collect(panel):
    return lax.all_gather(panel, "sub", axis=0, tiled=True)


def body(embeddings, codes, codebook):
    table = lax.all_gather(codebook, "sub", axis=1, tiled=True)
    decoded = decode_rows(codes, table)
    partial_panel = lax.psum_scatter(
        lax.dot_general(
            embeddings, decoded, (((0,), (0,)), ((), ())), preferred_element_type=jnp.float32
        ),
        "sub",
        scatter_dimension=0,
        tiled=True,
    )
    cross_panel = lax.psum(partial_panel, "rows")
    squares = lax.psum(jnp.sum(cross_panel * cross_panel), "sub")
    frob_scale = jnp.sqrt(squares) + frob_eps
    panel = cross_panel / frob_scale
    whole = collect(panel)
    for newton_step in range(NS_STEPS):
        if newton_step > 0:
            whole = collect(panel)
        panel = newton_panel(panel, whole)
    rotation_full = lax.all_gather(panel.astype(jnp.bfloat16), "sub", axis=0, tiled=True)
    rotated = jnp.dot(embeddings, rotation_full, preferred_element_type=jnp.float32).astype(
        jnp.bfloat16
    )
    moved_rows = lax.all_to_all(rotated, "sub", split_axis=1, concat_axis=0, tiled=True)
    moved_codes = lax.all_to_all(codes, "sub", split_axis=0, concat_axis=1, tiled=True)
    code_sums, counts = codeword_totals(moved_codes, moved_rows, table.shape[0])
    code_sums, counts = (
        lax.psum(code_sums.astype(jnp.bfloat16), "rows").astype(jnp.float32),
        lax.psum(counts.astype(jnp.bfloat16), "rows").astype(jnp.float32),
    )
    own_codebook = codebook.astype(jnp.float32)
    spread = jnp.repeat(counts, own_codebook.shape[1] // counts.shape[1], axis=1)
    new_codebook = (code_sums + own_codebook) / (spread + 1.0)
    return (panel, rotated, new_codebook)


def solution(mesh):
    in_specs = (P(("rows", "sub"), None), P(None, ("rows", "sub")), P(None, "sub"))
    out_specs = (P("sub", None), P(("rows", "sub"), None), P(None, "sub"))
    return jax.shard_map(body, mesh=mesh, in_specs=in_specs, out_specs=out_specs, check_vma=False)
```

profile of v0, /device:TPU:64, one launch (start us, length us, event | category | flops | bytes accessed | tf_op | source)
XLA Modules:
  0.0 547.7 jit_solution(3402713358330620616)
XLA Ops:
  7.2 0.0 reduce-scatter.4.cloned.1.call-start
  7.2 18.8 %all_gather.15 = bf16[256,1024]{0,1:T(8,128)(2,1)S(1)} all-gather(bf16[256,64]{0,1:T(8,128)(2,1)} %param.5), channel_id=1, replica_groups=mesh['rows'=16,'sub'=16] {'sub'}, dimensions={1}, use_global_device_ids=true | all-gather | bytes 557056 | tf_op jit(solution)/shard_map/all_gather | solution.py:88
  26.0 5.3 fusion.6
  31.3 2.7 convolution_bitcast_fusion
  34.0 5.4 copy.15
  39.3 0.0 reduce-scatter.4.cloned.1.call-update
  39.4 0.0 all-reduce.3.cloned.1.call-start
  39.4 58.3 %reduce-scatter.4.cloned.1.call-done = f32[64,1024]{1,0:T(8,128)} async-done(((f32[1024,1024]{1,0:T(8,128)}), f32[64,1024]{1,0:T(8,128)}) %reduce-scatter.4.cloned.1.call-update) | async-done | bytes 262160 | tf_op jit(solution)/shard_map/reduce_scatter | solution.py:90
  97.7 0.0 all-reduce.3.cloned.1.call-update
  97.7 0.0 all-gather.5.cloned.1.call-start
  97.8 102.1 %all-reduce.3.cloned.1.call-done = f32[64,1024]{1,0:T(8,128)} async-done(((f32[64,1024]{1,0:T(8,128)}), f32[64,1024]{1,0:T(8,128)}) %all-reduce.3.cloned.1.call-update) | async-done | bytes 262160 | tf_op jit(solution)/shard_map/psum | solution.py:98
  199.9 1.6 multiply_reduce_fusion
  201.5 21.1 %psum.29 = f32[]{:T(128)} all-reduce(f32[]{:T(128)} %multiply_reduce_fusion), channel_id=1, replica_groups=mesh['rows'=16,'sub'=16] {'sub'}, use_global_device_ids=true, to_apply=%region_3.4 | all-reduce | flops 1 | bytes 8 | tf_op jit(solution)/shard_map/psum | solution.py:99
  223.3 1.7 broadcast_divide_fusion
  224.9 0.0 all-gather.5.cloned.1.call-update
  225.0 0.0 all-gather.7.cloned.1.call-start
  225.0 43.2 %all-gather.5.cloned.1.call-done = f32[1024,1024]{1,0:T(8,128)} async-done(((f32[64,1024]{1,0:T(8,128)}), f32[1024,1024]{1,0:T(8,128)}) %all-gather.5.cloned.1.call-update) | async-done | bytes 4194320 | tf_op jit(solution)/shard_map/all_gather | solution.py:84
  268.2 6.5 %fusion.12 = f32[64,1024]{1,0:T(8,128)S(1)} fusion(f32[64,1024]{1,0:T(8,128)} %broadcast_divide_fusion, f32[1024,1024]{1,0:T(8,128)} %all-gather.5.cloned.1.call-done), kind=kOutput, calls=%fused_computation.26 | convolution fusion | flops 805306368 | bytes 4718592 | tf_op jit(solution)/shard_map/dot_general | solution.py:19
  274.8 2.6 fusion.13
  277.4 4.2 fusion.9
  281.6 3.4 convolution_add_fusion.2
  284.9 0.0 all-gather.7.cloned.1.call-update
  285.0 0.5 all-gather.9.cloned.1.call-start
  285.5 40.1 %all-gather.7.cloned.1.call-done = f32[1024,1024]{1,0:T(8,128)} async-done(((f32[64,1024]{1,0:T(8,128)}), f32[1024,1024]{1,0:T(8,128)}) %all-gather.7.cloned.1.call-update) | async-done | bytes 4194320 | tf_op jit(solution)/shard_map/all_gather | solution.py:84
  325.5 6.5 %fusion.14 = f32[64,1024]{1,0:T(8,128)S(1)} fusion(f32[64,1024]{1,0:T(8,128)} %convolution_add_fusion.2, f32[1024,1024]{1,0:T(8,128)} %all-gather.7.cloned.1.call-done), kind=kOutput, calls=%fused_computation.28 | convolution fusion | flops 805306368 | bytes 4718592 | tf_op jit(solution)/shard_map/dot_general | solution.py:19
  332.0 2.6 fusion.15
  334.7 4.2 fusion.8
  338.9 3.4 convolution_add_fusion.1
  342.2 0.2 all-gather.11.cloned.1.call-start
  342.5 40.4 %all-gather.9.cloned.1.call-done = f32[1024,1024]{1,0:T(8,128)} async-done(((f32[64,1024]{1,0:T(8,128)}), f32[1024,1024]{1,0:T(8,128)}) %all-gather.9.cloned.1.call-update) | async-done | bytes 4194320 | tf_op jit(solution)/shard_map/all_gather | solution.py:84
  382.8 6.5 %fusion.16 = f32[64,1024]{1,0:T(8,128)S(1)} fusion(f32[64,1024]{1,0:T(8,128)} %convolution_add_fusion.1, f32[1024,1024]{1,0:T(8,128)} %all-gather.9.cloned.1.call-done), kind=kOutput, calls=%fused_computation.30 | convolution fusion | flops 805306368 | bytes 4718592 | tf_op jit(solution)/shard_map/dot_general | solution.py:19
  389.3 2.7 fusion.17
  392.0 4.2 fusion.7
  396.2 3.4 fusion.11
  399.6 0.0 all-gather.11.cloned.1.call-update
  399.6 0.7 all_to_all.27
  400.3 6.0 %all-to-all-start.1 = ((s32[16,4,256]{2,1,0:T(4,128)}), s32[16,4,256]{2,1,0:T(4,128)S(1)}, u32[]{:S(2)}, u32[]{:S(2)}) async-start(s32[16,4,256]{2,1,0:T(4,128)} %all_to_all.27), calls=%async_computation.1 | async-start | bytes 131072 | tf_op jit(solution)/shard_map/all_to_all | solution.py:112
  406.3 31.3 %all-gather.11.cloned.1.call-done = bf16[1024,1024]{1,0:T(8,128)(2,1)} async-done(((bf16[64,1024]{1,0:T(8,128)(2,1)}), bf16[1024,1024]{1,0:T(8,128)(2,1)}) %all-gather.11.cloned.1.call-update) | async-done | bytes 2097168 | tf_op jit(solution)/shard_map/all_gather | solution.py:107
  437.6 3.2 convolution_convert_fusion
  440.8 6.4 %all-to-all-start = ((bf16[256,16,64]{0,2,1:T(8,128)(2,1)}), bf16[256,16,64]{0,2,1:T(8,128)(2,1)S(1)}, u32[]{:S(2)}, u32[]{:S(2)}) async-start(bf16[256,16,64]{0,2,1:T(8,128)(2,1)} %bitcast.5), calls=%async_computation | async-start | bytes 1048576 | tf_op jit(solution)/shard_map/all_to_all | solution.py:111
  447.1 6.9 %fusion.3 = bf16[4,256]{1,0:T(4,128)(2,1)S(1)} fusion(s32[4,4096]{1,0:T(4,128)S(1)} %bitcast.55), kind=kLoop, calls=%fused_computation.5 | loop fusion | flops 12581888 | bytes 67584 | tf_op jit(solution)/shard_map/while/body/eval_jaxpr/reduce_sum | solution.py:61
  454.1 2.0 copy.14
  456.1 5.9 %all-to-all-done = bf16[256,16,64]{0,2,1:T(8,128)(2,1)S(1)} async-done(((bf16[256,16,64]{0,2,1:T(8,128)(2,1)}), bf16[256,16,64]{0,2,1:T(8,128)(2,1)S(1)}, u32[]{:S(2)}, u32[]{:S(2)}) %all-to-all-start) | async-done | bytes 524320 | tf_op jit(solution)/shard_map/all_to_all | solution.py:111
  462.0 0.3 copy.13
  462.3 0.2 squeeze.11
  462.5 3.2 fusion.10
  465.8 74.2 %all-reduce = (bf16[256,64]{0,1:T(8,128)(2,1)S(1)}, bf16[256,4]{0,1:T(4,128)(2,1)S(1)}) all-reduce(bf16[256,64]{0,1:T(8,128)(2,1)S(1)} %bitcast.57, bf16[256,4]{0,1:T(4,128)(2,1)S(1)} %bitcast.58), channel_id=1, replica_groups=mesh['rows'=16,'sub'=16] {'rows'}, use_global_device_ids=true, to_apply=%region_4.5 | all-reduce | flops 17408 | bytes 69632 | tf_op jit(solution)/shard_map/psum | solution.py:115
  540.0 0.6 bitcast_divide_fusion
  (21 shorter events, 0.1 us)
Async XLA Ops:
  7.2 24.1 %copy-start = (bf16[256,1024]{1,0:T(8,128)(2,1)S(1)}, bf16[256,1024]{1,0:T(8,128)(2,1)}, u32[]{:S(2)}) copy-start(bf16[256,1024]{1,0:T(8,128)(2,1)} %param.3) | copy-start | bytes 1572868
  7.2 90.5 %reduce-scatter.4.cloned.1.call-start = ((), (), s32[]{:S(2)}) async-start(), calls=%async_computation.8 | async-start | bytes 4456448 | tf_op jit(solution)/shard_map/reduce_scatter | solution.py:90
  39.4 160.5 %all-reduce.3.cloned.1.call-start = ((), (), s32[]{:S(2)}) async-start(), calls=%async_computation.3 | async-start | bytes 524288 | tf_op jit(solution)/shard_map/psum | solution.py:98
  97.7 170.5 %all-gather.5.cloned.1.call-start = ((), (), s32[]{:S(2)}) async-start(), calls=%async_computation.4 | async-start | bytes 4456448 | tf_op jit(solution)/shard_map/all_gather | solution.py:84
  225.0 100.6 %all-gather.7.cloned.1.call-start = ((), (), s32[]{:S(2)}) async-start(), calls=%async_computation.5 | async-start | bytes 4456448 | tf_op jit(solution)/shard_map/all_gather | solution.py:84
  268.2 6.5 %copy-start.2 = (f32[1024,1024]{1,0:T(8,128)S(1)}, f32[1024,1024]{1,0:T(8,128)}, u32[]{:S(2)}) copy-start(f32[1024,1024]{1,0:T(8,128)} %all-gather.5.cloned.1.call-done) | copy-start | bytes 12582916
  274.7 6.8 %copy-start.6 = (f32[64,1024]{1,0:T(8,128)S(1)}, f32[64,1024]{1,0:T(8,128)}, u32[]{:S(2)}) copy-start(f32[64,1024]{1,0:T(8,128)} %broadcast_divide_fusion) | copy-start | bytes 786436
  285.0 97.9 %all-gather.9.cloned.1.call-start = ((), (), s32[]{:S(2)}) async-start(), calls=%async_computation.6 | async-start | bytes 4456448 | tf_op jit(solution)/shard_map/all_gather | solution.py:84
  325.5 6.5 %copy-start.3 = (f32[1024,1024]{1,0:T(8,128)S(1)}, f32[1024,1024]{1,0:T(8,128)}, u32[]{:S(2)}) copy-start(f32[1024,1024]{1,0:T(8,128)} %all-gather.7.cloned.1.call-done) | copy-start | bytes 12582916
  332.0 6.8 %copy-start.5 = (f32[64,1024]{1,0:T(8,128)S(1)}, f32[64,1024]{1,0:T(8,128)}, u32[]{:S(2)}) copy-start(f32[64,1024]{1,0:T(8,128)} %convolution_add_fusion.2) | copy-start | bytes 786436
  342.2 95.4 %all-gather.11.cloned.1.call-start = ((), (), s32[]{:S(2)}) async-start(), calls=%async_computation.7 | async-start | bytes 2228224 | tf_op jit(solution)/shard_map/all_gather | solution.py:107
  382.8 6.5 %copy-start.1 = (f32[1024,1024]{1,0:T(8,128)S(1)}, f32[1024,1024]{1,0:T(8,128)}, u32[]{:S(2)}) copy-start(f32[1024,1024]{1,0:T(8,128)} %all-gather.9.cloned.1.call-done) | copy-start | bytes 12582916
  389.3 6.9 %copy-start.4 = (f32[64,1024]{1,0:T(8,128)S(1)}, f32[64,1024]{1,0:T(8,128)}, u32[]{:S(2)}) copy-start(f32[64,1024]{1,0:T(8,128)} %convolution_add_fusion.1) | copy-start | bytes 786436
  392.0 7.6 %copy-start.8 = (s32[64,256]{1,0:T(8,128)S(1)}, s32[64,256]{1,0:T(8,128)}, u32[]{:S(2)}) copy-start(s32[64,256]{1,0:T(8,128)} %param.4) | copy-start | bytes 196612
  400.3 40.5 %all-to-all-start.1 = ((s32[16,4,256]{2,1,0:T(4,128)}), s32[16,4,256]{2,1,0:T(4,128)S(1)}, u32[]{:S(2)}, u32[]{:S(2)}) async-start(s32[16,4,256]{2,1,0:T(4,128)} %all_to_all.27), calls=%async_computation.1 | async-start | bytes 131072 | tf_op jit(solution)/shard_map/all_to_all | solution.py:112
  440.8 21.2 %all-to-all-start = ((bf16[256,16,64]{0,2,1:T(8,128)(2,1)}), bf16[256,16,64]{0,2,1:T(8,128)(2,1)S(1)}, u32[]{:S(2)}, u32[]{:S(2)}) async-start(bf16[256,16,64]{0,2,1:T(8,128)(2,1)} %bitcast.5), calls=%async_computation | async-start | bytes 1048576 | tf_op jit(solution)/shard_map/all_to_all | solution.py:111
  456.1 83.9 %copy-start.7 = (bf16[256,64]{0,1:T(8,128)(2,1)S(1)}, bf16[256,64]{0,1:T(8,128)(2,1)}, u32[]{:S(2)}) copy-start(bf16[256,64]{0,1:T(8,128)(2,1)} %param.5) | copy-start | bytes 98308
Sparse Core Ops, SparseCore 0:
  39.5 58.1 reduce-scatter.3
  100.9 98.9 all-reduce.2
  225.1 43.1 all-gather.4
  285.1 40.4 all-gather.6
  342.4 40.4 all-gather.8
  399.7 37.8 all-gather.10
where the time goes:
time: 557 us; the launch traced here: 548 us
  waiting for transfers between devices  321 us (58%)
  blocking collectives  114 us (20%)
  matrix products  64.3 us (12%)
  between operations  15.2 us (3%)
  starting transfers between devices  13.3 us (2%)
  other arithmetic  10.9 us (2%)
  local copies, waits for them, and re-layouts  8.64 us (2%)
    all_gather x3, waiting for transfers between devices, collect(): return lax.all_gather(panel, 'sub', axis=0, tiled=True)  124 us
    psum x1, waiting for transfers between devices, body(): cross_panel = lax.psum(partial_panel, 'rows')  102 us
    psum x1, blocking collectives, body(): lax.psum(code_sums.astype(jnp.bfloat16), 'rows').astype(jnp.float32)  74.2 us
    reduce_scatter x1, waiting for transfers between devices, body(): lax.psum_scatter(lax.dot_general(embeddings, decoded, (((0,), (0,)), ((),...  58.3 us
    dot_general x6, matrix products, rows_dot(): lax.dot_general(left, right, (((1,), (1,)), ((), ())), precision=highest,...  31.9 us
    all_gather x1, waiting for transfers between devices, body(): lax.all_gather(panel.astype(jnp.bfloat16), 'sub', axis=0, tiled=True)  31.3 us
    psum x1, blocking collectives, body(): squares = lax.psum(jnp.sum(cross_panel * cross_panel), 'sub')  21.1 us
    all_gather x1, blocking collectives, body(): table = lax.all_gather(codebook, 'sub', axis=1, tiled=True)  18.8 us
  transfers between devices with their start and end apart: 8, of which 7 were waited for; matrix products, arithmetic and copies ran while one was open for 2% of the time, Pallas kernels for 0%

commit v1 on v0

v1 whole, which is shorter than its diff:
```python
import math

import jax
import jax.numpy as jnp
from jax import lax
from jax.sharding import PartitionSpec as P

NS_STEPS = 3


coef_a = 3.4445
coef_b = -4.775
coef_c = 2.0315
frob_eps = 1e-07


def one_hot_codes(code_block, count_codes):
    levels = lax.broadcasted_iota(jnp.int32, code_block.shape + (count_codes,), 2)
    return (code_block[:, :, None] == levels).astype(jnp.bfloat16)


def decode_rows(codes, table):
    subspaces, local_rows = codes.shape
    count_codes, row_width = table.shape
    sub_width = row_width // subspaces
    codewords = table.reshape(count_codes, subspaces, sub_width)
    one_hot = one_hot_codes(codes, count_codes)
    picked = jnp.einsum("mnk,kmj->nmj", one_hot, codewords, preferred_element_type=jnp.float32)
    return picked.reshape(local_rows, row_width).astype(jnp.bfloat16)


def codeword_totals(codes, row_values, count_codes):
    subspaces, local_rows = codes.shape
    row_width = row_values.shape[1]
    sub_width = row_width // subspaces
    one_hot = one_hot_codes(codes, count_codes)
    pieces = row_values.reshape(local_rows, subspaces, sub_width)
    code_sums = jnp.einsum("mnk,nmj->kmj", one_hot, pieces, preferred_element_type=jnp.float32)
    counts = jnp.sum(one_hot, axis=1, dtype=jnp.float32).T
    return code_sums.reshape(count_codes, row_width), counts


def bdot(left, right, dims):
    return lax.dot_general(
        left.astype(jnp.bfloat16), right.astype(jnp.bfloat16), (dims, ((), ())),
        preferred_element_type=jnp.float32,
    )


def newton_step(z):
    z_half = z.astype(jnp.bfloat16)
    gram = bdot(z_half, z_half, ((1,), (1,)))
    quartic = bdot(gram, gram, ((1,), (0,)))
    mixer = coef_b * gram + coef_c * quartic
    return coef_a * z + bdot(mixer, z_half, ((1,), (0,)))


def body(embeddings, codes, codebook):
    table = lax.all_gather(codebook, "sub", axis=1, tiled=True)
    decoded = decode_rows(codes, table)
    partial = lax.dot_general(
        embeddings, decoded, (((0,), (0,)), ((), ())), preferred_element_type=jnp.float32
    )
    cross = lax.psum(partial, ("rows", "sub"))
    frob_scale = jnp.sqrt(jnp.sum(cross * cross)) + frob_eps
    z = cross / frob_scale
    for newton_step_index in range(NS_STEPS):
        z = newton_step(z)
    rotation_half = z.astype(jnp.bfloat16)
    rotated = jnp.dot(embeddings, rotation_half, preferred_element_type=jnp.float32).astype(
        jnp.bfloat16
    )
    code_sums, counts = codeword_totals(codes, rotated, table.shape[0])
    code_sums = lax.psum(code_sums, ("rows", "sub"))
    counts = lax.psum(counts, ("rows", "sub"))
    me = lax.axis_index("sub")
    cols = codebook.shape[1]
    own_subspaces = counts.shape[1] * cols // code_sums.shape[1]
    own_sums = lax.dynamic_slice_in_dim(code_sums, me * cols, cols, axis=1)
    own_counts = lax.dynamic_slice_in_dim(counts, me * own_subspaces, own_subspaces, axis=1)
    own_codebook = codebook.astype(jnp.float32)
    spread = jnp.repeat(own_counts, cols // own_subspaces, axis=1)
    new_codebook = (own_sums + own_codebook) / (spread + 1.0)
    panel_rows = z.shape[0] // lax.axis_size("sub")
    panel = lax.dynamic_slice_in_dim(z, me * panel_rows, panel_rows, axis=0)
    return (panel, rotated, new_codebook)


def solution(mesh):
    in_specs = (P(("rows", "sub"), None), P(None, ("rows", "sub")), P(None, "sub"))
    out_specs = (P("sub", None), P(("rows", "sub"), None), P(None, "sub"))
    return jax.shard_map(body, mesh=mesh, in_specs=in_specs, out_specs=out_specs, check_vma=False)
```

time: 557 us -> 652 us (1.17)
  waiting for transfers between devices: 321 us -> 517 us
  blocking collectives: 114 us -> 18.8 us
  matrix products: 64.3 us -> 81.1 us
  starting transfers between devices: 13.3 us -> 0.08 us
    psum x1 -> x2, waiting for transfers between devices: 102 us -> 517 us  [the longest x1 264 us: body(): cross = lax.psum(partial, ('rows', 'sub'))]
    all_gather x4 -> x0, waiting for transfers between devices: 155 us -> none  [the longest x3 124 us: collect(): return lax.all_gather(panel, 'sub', axis=0, tiled=True)]
    psum x2 -> x0, blocking collectives: 95.3 us -> none  [the longest x1 74.2 us: body(): lax.psum(code_sums.astype(jnp.bfloat16), 'rows').astype(jnp.float32)]
    reduce_scatter x1 -> x0, waiting for transfers between devices: 58.3 us -> none  [body(): lax.psum_scatter(lax.dot_general(embeddings, decoded, (((0,), (0,)), ((),...]
    dot_general x15 -> x9, matrix products: 61.6 us -> 78.5 us  [the longest x6 65.2 us: bdot(): lax.dot_general(left.astype(jnp.bfloat16), right.astype(jnp.bfloat16), (d...]
    all_to_all x2 -> x0, starting transfers between devices: 12.4 us -> none  [the longest x1 6.37 us: body(): lax.all_to_all(rotated, 'sub', split_axis=1, concat_axis=0, tiled=True)]
  transfers between devices with their start and end apart: 8 -> 2, of which waited for: 7 -> 2; matrix products, arithmetic and copies ran while one was open for 2% -> 1% of each run, Pallas kernels for 0% -> 0%
where the time goes in v1:
time: 652 us; the launch traced here: 645 us
  waiting for transfers between devices  517 us (79%)
  matrix products  81.1 us (12%)
  blocking collectives  18.8 us (3%)
  between operations  14.8 us (2%)
  other arithmetic  9.48 us (1%)
    psum x1, waiting for transfers between devices, body(): cross = lax.psum(partial, ('rows', 'sub'))  264 us
    psum x1, waiting for transfers between devices, body(): code_sums = lax.psum(code_sums, ('rows', 'sub'))  254 us
    dot_general x6, matrix products, bdot(): lax.dot_general(left.astype(jnp.bfloat16), right.astype(jnp.bfloat16), (d...  65.2 us
    all_gather x1, blocking collectives, body(): table = lax.all_gather(codebook, 'sub', axis=1, tiled=True)  18.8 us
  transfers between devices with their start and end apart: 2, of which 2 were waited for; matrix products, arithmetic and copies ran while one was open for 1% of the time, Pallas kernels for 0%

profile of v1, /device:TPU:64, one launch (start us, length us, event | category | flops | bytes accessed | tf_op | source)
XLA Modules:
  0.0 645.3 jit_solution(6691471587485620089)
XLA Ops:
  7.2 0.0 copy-start
  7.2 0.0 all-reduce.4.cloned.1.call-start
  7.2 18.8 %all_gather.3 = bf16[256,1024]{0,1:T(8,128)(2,1)S(1)} all-gather(bf16[256,64]{0,1:T(8,128)(2,1)} %param.5), channel_id=1, replica_groups=mesh['rows'=16,'sub'=16] {'sub'}, dimensions={1}, use_global_device_ids=true | all-gather | bytes 557056 | tf_op jit(solution)/shard_map/all_gather | solution.py:59
  26.0 5.3 fusion.14
  31.3 0.0 copy-done
  31.3 2.7 convolution_bitcast_fusion
  33.9 0.0 copy-start.2
  33.9 0.0 all-reduce.4.cloned.1.call-update
  33.9 0.0 all-reduce.6.cloned.1.call-start
  34.0 0.8 copy-done.2
  34.8 3.4 convert_reduce_fusion
  38.2 263.5 %all-reduce.4.cloned.1.call-done = f32[1024,1024]{0,1:T(8,128)} async-done(((f32[1024,1024]{0,1:T(8,128)}), f32[1024,1024]{0,1:T(8,128)}) %all-reduce.4.cloned.1.call-update) | async-done | bytes 4194320 | tf_op jit(solution)/shard_map/psum | solution.py:64
  301.7 3.9 multiply_reduce_fusion
  306.3 7.8 %fusion.28 = f32[1024,1024]{1,0:T(8,128)} fusion(f32[1024,1024]{0,1:T(8,128)} %all-reduce.4.cloned.1.call-done, f32[]{:T(128)S(6)} %add.47), kind=kOutput, calls=%fused_computation.30 | convolution fusion | flops 2149580800 | bytes 8388612 | tf_op jit(solution)/shard_map/dot_general | solution.py:44
  314.1 13.9 %multiply_add_fusion.2 = f32[1024,1024]{0,1:T(8,128)} fusion(f32[1024,1024]{0,1:T(8,128)} %all-reduce.4.cloned.1.call-done, f32[]{:T(128)S(6)} %add.47, f32[1024,1024]{1,0:T(8,128)} %fusion.28), kind=kOutput, calls=%fused_computation.12 | convolution fusion | flops 4305453056 | bytes 12582916 | tf_op jit(solution)/shard_map/dot_general | solution.py:44
  328.0 7.8 %fusion.21 = f32[1024,1024]{1,0:T(8,128)} fusion(f32[1024,1024]{0,1:T(8,128)} %multiply_add_fusion.2), kind=kOutput, calls=%fused_computation.28 | convolution fusion | flops 2148532224 | bytes 8388608 | tf_op jit(solution)/shard_map/dot_general | solution.py:44
  335.8 13.7 %multiply_add_fusion.1 = f32[1024,1024]{0,1:T(8,128)} fusion(f32[1024,1024]{0,1:T(8,128)} %multiply_add_fusion.2, f32[1024,1024]{1,0:T(8,128)} %fusion.21), kind=kOutput, calls=%fused_computation.10 | convolution fusion | flops 4303355904 | bytes 12582912 | tf_op jit(solution)/shard_map/dot_general | solution.py:44
  349.5 8.0 %fusion.18 = f32[1024,1024]{1,0:T(8,128)} fusion(f32[1024,1024]{0,1:T(8,128)} %multiply_add_fusion.1), kind=kOutput, calls=%fused_computation.25 | convolution fusion | flops 2148532224 | bytes 8388608 | tf_op jit(solution)/shard_map/dot_general | solution.py:44
  357.6 13.9 %multiply_add_fusion = f32[1024,1024]{0,1:T(8,128)} fusion(f32[1024,1024]{0,1:T(8,128)} %multiply_add_fusion.1, f32[1024,1024]{1,0:T(8,128)} %fusion.18), kind=kOutput, calls=%fused_computation.8 | convolution fusion | flops 4303355904 | bytes 12582912 | tf_op jit(solution)/shard_map/dot_general | solution.py:44
  371.4 2.9 fusion.11
  374.4 0.0 copy-start.1
  374.4 5.1 fusion.1
  379.5 0.0 all-reduce.6.cloned.1.call-update
  379.5 1.2 constant_dynamic-slice_fusion
  380.8 0.9 copy.9
  381.7 1.0 copy.10
  382.7 253.6 %all-reduce.6.cloned.1.call-done = (f32[256,1024]{0,1:T(8,128)}, f32[256,64]{0,1:T(8,128)}) async-done(((f32[256,1024]{0,1:T(8,128)}, f32[256,64]{0,1:T(8,128)}), (f32[256,1024]{0,1:T(8,128)}, f32[256,64]{0,1:T(8,128)})) %all-reduce.6.cloned.1.call-update) | async-done | bytes 1114128 | tf_op jit(solution)/shard_map/psum | solution.py:74
  636.3 0.7 dynamic-slice_add_fusion
  637.0 0.0 copy-done.1
  637.0 1.5 bitcast_divide_fusion
Async XLA Ops:
  7.2 24.1 %copy-start = (bf16[256,1024]{1,0:T(8,128)(2,1)S(1)}, bf16[256,1024]{1,0:T(8,128)(2,1)}, u32[]{:S(2)}) copy-start(bf16[256,1024]{1,0:T(8,128)(2,1)} %param.3) | copy-start | bytes 1572868
  7.2 294.5 %all-reduce.4.cloned.1.call-start = ((), (), s32[]{:S(2)}) async-start(), calls=%async_computation | async-start | bytes 8388608 | tf_op jit(solution)/shard_map/psum | solution.py:64
  33.9 0.8 copy-start.2
  33.9 602.3 %all-reduce.6.cloned.1.call-start = ((), (), s32[]{:S(2)}) async-start(), calls=%async_computation.1 | async-start | bytes 2228224 | tf_op jit(solution)/shard_map/psum | solution.py:74
  374.4 262.6 %copy-start.1 = (bf16[256,64]{0,1:T(8,128)(2,1)S(1)}, bf16[256,64]{0,1:T(8,128)(2,1)}, u32[]{:S(2)}) copy-start(bf16[256,64]{0,1:T(8,128)(2,1)} %param.5) | copy-start | bytes 98308
Sparse Core Ops, SparseCore 0:
  34.1 267.6 all-reduce.3
  379.6 256.5 all-reduce.5

commit v2 on v1

--- a/solution.py
+++ b/solution.py
@@ -1,5 +1,3 @@
-import math
-
 import jax
 import jax.numpy as jnp
 from jax import lax
@@ -40,6 +38,15 @@
     return code_sums.reshape(count_codes, row_width), counts
 
 
+def rows_sum(x):
+    groups = lax.axis_size("rows")
+    chunk = x.shape[0] // groups
+    scattered = lax.all_to_all(x, "rows", split_axis=0, concat_axis=0, tiled=True)
+    own = jnp.sum(scattered.reshape((groups, chunk) + x.shape[1:]), axis=0)
+    spread = jnp.broadcast_to(own[None], (groups,) + own.shape).reshape(x.shape)
+    return lax.all_to_all(spread, "rows", split_axis=0, concat_axis=0, tiled=True)
+
+
 def bdot(left, right, dims):
     return lax.dot_general(
         left.astype(jnp.bfloat16), right.astype(jnp.bfloat16), (dims, ((), ())),
@@ -56,12 +63,15 @@
 
 
 def body(embeddings, codes, codebook):
+    moved_codes = lax.all_to_all(codes, "sub", split_axis=0, concat_axis=1, tiled=True)
     table = lax.all_gather(codebook, "sub", axis=1, tiled=True)
     decoded = decode_rows(codes, table)
     partial = lax.dot_general(
         embeddings, decoded, (((0,), (0,)), ((), ())), preferred_element_type=jnp.float32
     )
-    cross = lax.psum(partial, ("rows", "sub"))
+    partial_panel = lax.psum_scatter(partial, "sub", scatter_dimension=0, tiled=True)
+    cross_panel = rows_sum(partial_panel)
+    cross = lax.all_gather(cross_panel, "sub", axis=0, tiled=True)
     frob_scale = jnp.sqrt(jnp.sum(cross * cross)) + frob_eps
     z = cross / frob_scale
     for newton_step_index in range(NS_STEPS):
@@ -70,17 +80,15 @@
     rotated = jnp.dot(embeddings, rotation_half, preferred_element_type=jnp.float32).astype(
         jnp.bfloat16
     )
-    code_sums, counts = codeword_totals(codes, rotated, table.shape[0])
-    code_sums = lax.psum(code_sums, ("rows", "sub"))
-    counts = lax.psum(counts, ("rows", "sub"))
+    moved_rows = lax.all_to_all(rotated, "sub", split_axis=1, concat_axis=0, tiled=True)
+    code_sums, counts = codeword_totals(moved_codes, moved_rows, table.shape[0])
+    sums_width = code_sums.shape[1]
+    totals = rows_sum(jnp.concatenate([code_sums, counts], axis=1))
+    code_sums, counts = totals[:, :sums_width], totals[:, sums_width:]
+    own_codebook = codebook.astype(jnp.float32)
+    spread = jnp.repeat(counts, own_codebook.shape[1] // counts.shape[1], axis=1)
+    new_codebook = (code_sums + own_codebook) / (spread + 1.0)
     me = lax.axis_index("sub")
-    cols = codebook.shape[1]
-    own_subspaces = counts.shape[1] * cols // code_sums.shape[1]
-    own_sums = lax.dynamic_slice_in_dim(code_sums, me * cols, cols, axis=1)
-    own_counts = lax.dynamic_slice_in_dim(counts, me * own_subspaces, own_subspaces, axis=1)
-    own_codebook = codebook.astype(jnp.float32)
-    spread = jnp.repeat(own_counts, cols // own_subspaces, axis=1)
-    new_codebook = (own_sums + own_codebook) / (spread + 1.0)
     panel_rows = z.shape[0] // lax.axis_size("sub")
     panel = lax.dynamic_slice_in_dim(z, me * panel_rows, panel_rows, axis=0)
     return (panel, rotated, new_codebook)

time: 652 us -> 305 us (0.47)
  waiting for transfers between devices: 517 us -> 109 us
  blocking collectives: 18.8 us -> 46.3 us
  starting transfers between devices: 0.08 us -> 25.6 us
  local copies, waits for them, and re-layouts: 3.92 us -> 14.5 us
    psum x2 -> x0, waiting for transfers between devices: 517 us -> none  [the longest x1 264 us: body(): cross = lax.psum(partial, ('rows', 'sub'))]
    reduce_scatter x0 -> x1, waiting for transfers between devices: none -> 58.1 us  [body(): lax.psum_scatter(partial, 'sub', scatter_dimension=0, tiled=True)]
    all_gather x0 -> x1, waiting for transfers between devices: none -> 31.4 us  [body(): cross = lax.all_gather(cross_panel, 'sub', axis=0, tiled=True)]
    all_to_all x0 -> x2, blocking collectives: none -> 27.5 us  [the longest x1 15.1 us: rows_sum(): lax.all_to_all(x, 'rows', split_axis=0, concat_axis=0, tiled=True)]
    all_to_all x0 -> x4, starting transfers between devices: none -> 25.5 us  [the longest x1 9.71 us: body(): lax.all_to_all(codes, 'sub', split_axis=0, concat_axis=1, tiled=True)]
    all_to_all x0 -> x4, waiting for transfers between devices: none -> 19.7 us  [the longest x1 7.84 us: body(): lax.all_to_all(rotated, 'sub', split_axis=1, concat_axis=0, tiled=True)]
  transfers between devices with their start and end apart: 2 -> 6, of which waited for: 2 -> 5; matrix products, arithmetic and copies ran while one was open for 1% -> 28% of each run, Pallas kernels for 0% -> 0%
where the time goes in v2:
time: 305 us; the launch traced here: 302 us
  waiting for transfers between devices  109 us (36%)
  matrix products  80.1 us (26%)
  blocking collectives  46.3 us (15%)
  starting transfers between devices  25.6 us (8%)
  between operations  14.9 us (5%)
  local copies, waits for them, and re-layouts  14.5 us (5%)
  other arithmetic  11.7 us (4%)
    dot_general x6, matrix products, bdot(): lax.dot_general(left.astype(jnp.bfloat16), right.astype(jnp.bfloat16), (d...  65.2 us
    reduce_scatter x1, waiting for transfers between devices, body(): lax.psum_scatter(partial, 'sub', scatter_dimension=0, tiled=True)  58.1 us
    all_gather x1, waiting for transfers between devices, body(): cross = lax.all_gather(cross_panel, 'sub', axis=0, tiled=True)  31.4 us
    all_gather x1, blocking collectives, body(): table = lax.all_gather(codebook, 'sub', axis=1, tiled=True)  18.8 us
    all_to_all x1, blocking collectives, rows_sum(): lax.all_to_all(x, 'rows', split_axis=0, concat_axis=0, tiled=True)  15.1 us
    all_to_all x1, blocking collectives, rows_sum(): lax.all_to_all(spread, 'rows', split_axis=0, concat_axis=0, tiled=True)  12.5 us
    all_to_all x1, starting transfers between devices, body(): lax.all_to_all(codes, 'sub', split_axis=0, concat_axis=1, tiled=True)  9.71 us
    unnamed x11, local copies, waits for them, and re-layouts  8.31 us
  transfers between devices with their start and end apart: 6, of which 5 were waited for; matrix products, arithmetic and copies ran while one was open for 28% of the time, Pallas kernels for 0%

profile of v2, /device:TPU:64, one launch (start us, length us, event | category | flops | bytes accessed | tf_op | source)
XLA Modules:
  0.0 302.3 jit_solution(14414597527904808225)
XLA Ops:
  7.2 0.0 copy-start
  7.2 0.0 reduce-scatter.4.cloned.1.call-start
  7.2 18.8 %all_gather.6 = bf16[256,1024]{0,1:T(8,128)(2,1)S(1)} all-gather(bf16[256,64]{0,1:T(8,128)(2,1)} %param.5), channel_id=1, replica_groups=mesh['rows'=16,'sub'=16] {'sub'}, dimensions={1}, use_global_device_ids=true | all-gather | bytes 557056 | tf_op jit(solution)/shard_map/all_gather | solution.py:67
  26.0 5.3 %fusion.14 = bf16[64,256,16]{1,2,0:T(8,128)(2,1)S(1)} fusion(bf16[256,64,16]{0,2,1:T(8,128)(2,1)S(1)} %bitcast.34, s32[64,256]{1,0:T(8,128)} %param.4), kind=kOutput, calls=%fused_computation.24 | convolution fusion | flops 138674176 | bytes 1114112 | tf_op jit(solution)/shard_map/mnk,kmj->nmj/dot_general | solution.py:26
  31.3 2.7 convolution_bitcast_fusion
  34.0 5.3 %copy.53 = f32[1024,1024]{1,0:T(8,128)} copy(f32[1024,1024]{0,1:T(8,128)} %convolution_bitcast_fusion) | data formatting | bytes 8388608
  39.3 0.0 reduce-scatter.4.cloned.1.call-update
  39.3 0.0 all-gather.2.cloned.1.call-start
  39.4 58.1 %reduce-scatter.4.cloned.1.call-done = f32[64,1024]{1,0:T(8,128)} async-done(((f32[1024,1024]{1,0:T(8,128)}), f32[64,1024]{1,0:T(8,128)}) %reduce-scatter.4.cloned.1.call-update) | async-done | bytes 262160 | tf_op jit(solution)/shard_map/reduce_scatter | solution.py:72
  97.5 1.0 all_to_all.46
  98.6 15.1 %all_to_all.65 = f32[16,4,1024]{2,1,0:T(4,128)S(1)} all-to-all(f32[16,4,1024]{2,1,0:T(4,128)S(1)} %all_to_all.46), channel_id=1, replica_groups=mesh['rows'=16,'sub'=16] {'rows'}, dimensions={0} | all-to-all | bytes 524288 | tf_op jit(solution)/shard_map/all_to_all | solution.py:44
  113.6 0.1 reduce_sum.36
  113.7 12.5 %all_to_all.66 = f32[16,4,1024]{2,1,0:T(4,128)S(1)} all-to-all(f32[16,4,1024]{2,1,0:T(4,128)S(1)} %broadcast_in_dim.6), channel_id=1, replica_groups=mesh['rows'=16,'sub'=16] {'rows'}, dimensions={0} | all-to-all | bytes 524288 | tf_op jit(solution)/shard_map/all_to_all | solution.py:47
  126.2 0.8 all_to_all.49
  127.0 0.0 all-gather.2.cloned.1.call-update
  127.0 0.7 all_to_all.53
  127.7 9.7 %all-to-all-start.3 = ((s32[16,4,256]{2,1,0:T(4,128)}), s32[16,4,256]{2,1,0:T(4,128)S(1)}, u32[]{:S(2)}, u32[]{:S(2)}) async-start(s32[16,4,256]{2,1,0:T(4,128)} %all_to_all.53), calls=%async_computation.3 | async-start | bytes 131072 | tf_op jit(solution)/shard_map/all_to_all | solution.py:66
  137.4 31.4 %all-gather.2.cloned.1.call-done = f32[1024,1024]{1,0:T(8,128)} async-done(((f32[64,1024]{1,0:T(8,128)}), f32[1024,1024]{1,0:T(8,128)}) %all-gather.2.cloned.1.call-update) | async-done | bytes 4194320 | tf_op jit(solution)/shard_map/all_gather | solution.py:74
  168.8 3.9 %multiply_reduce_fusion = f32[]{:T(128)} fusion(f32[1024,1024]{1,0:T(8,128)} %all-gather.2.cloned.1.call-done), kind=kLoop, calls=%fused_computation.14 | loop fusion | flops 2097151 | bytes 4194308 | tf_op jit(solution)/shard_map/reduce_sum | solution.py:75
  173.4 7.8 %fusion.29 = f32[1024,1024]{1,0:T(8,128)} fusion(f32[1024,1024]{1,0:T(8,128)} %all-gather.2.cloned.1.call-done, f32[]{:T(128)S(6)} %add.39), kind=kOutput, calls=%fused_computation.32 | convolution fusion | flops 2149580800 | bytes 8388612 | tf_op jit(solution)/shard_map/dot_general | solution.py:51
  181.2 13.9 %multiply_add_fusion.2 = f32[1024,1024]{1,0:T(8,128)} fusion(f32[1024,1024]{1,0:T(8,128)} %all-gather.2.cloned.1.call-done, f32[]{:T(128)S(6)} %add.39, f32[1024,1024]{1,0:T(8,128)} %fusion.29), kind=kOutput, calls=%fused_computation.13 | convolution fusion | flops 4305453056 | bytes 12582916 | tf_op jit(solution)/shard_map/dot_general | solution.py:51
  195.1 7.8 %fusion.22 = f32[1024,1024]{1,0:T(8,128)} fusion(f32[1024,1024]{1,0:T(8,128)} %multiply_add_fusion.2), kind=kOutput, calls=%fused_computation.30 | convolution fusion | flops 2148532224 | bytes 8388608 | tf_op jit(solution)/shard_map/dot_general | solution.py:51
  202.9 13.8 %multiply_add_fusion.1 = f32[1024,1024]{1,0:T(8,128)} fusion(f32[1024,1024]{1,0:T(8,128)} %multiply_add_fusion.2, f32[1024,1024]{1,0:T(8,128)} %fusion.22), kind=kOutput, calls=%fused_computation.11 | convolution fusion | flops 4303355904 | bytes 12582912 | tf_op jit(solution)/shard_map/dot_general | solution.py:51
  216.6 8.0 %fusion.19 = f32[1024,1024]{1,0:T(8,128)} fusion(f32[1024,1024]{1,0:T(8,128)} %multiply_add_fusion.1), kind=kOutput, calls=%fused_computation.27 | convolution fusion | flops 2148532224 | bytes 8388608 | tf_op jit(solution)/shard_map/dot_general | solution.py:51
  224.6 13.9 %multiply_add_fusion = f32[1024,1024]{1,0:T(8,128)} fusion(f32[1024,1024]{1,0:T(8,128)} %multiply_add_fusion.1, f32[1024,1024]{1,0:T(8,128)} %fusion.19), kind=kOutput, calls=%fused_computation.9 | convolution fusion | flops 4303355904 | bytes 12582912 | tf_op jit(solution)/shard_map/dot_general | solution.py:51
  238.5 3.7 %fusion.11 = bf16[1024,256]{1,0:T(8,128)(2,1)} fusion(bf16[256,1024]{1,0:T(8,128)(2,1)S(1)} %copy-done, f32[1024,1024]{1,0:T(8,128)} %multiply_add_fusion), kind=kOutput, calls=%fused_computation.23 | convolution fusion | flops 538181632 | bytes 5242880 | tf_op jit(solution)/shard_map/dot_general | solution.py:80
  242.3 5.8 %all-to-all-start.2 = ((bf16[256,16,64]{0,2,1:T(8,128)(2,1)}), bf16[256,16,64]{0,2,1:T(8,128)(2,1)S(1)}, u32[]{:S(2)}, u32[]{:S(2)}) async-start(bf16[256,16,64]{0,2,1:T(8,128)(2,1)} %bitcast.5), calls=%async_computation.2 | async-start | bytes 1048576 | tf_op jit(solution)/shard_map/all_to_all | solution.py:83
  248.1 6.9 %convert_reduce_fusion = f32[4,256]{1,0:T(4,128)S(1)} fusion(s32[4,4096]{1,0:T(4,128)S(1)} %bitcast.36), kind=kLoop, calls=%fused_computation | loop fusion | flops 16776192 | bytes 69632 | tf_op jit(solution)/shard_map/reduce_sum | solution.py:37
  255.0 0.1 copy.52
  255.1 7.8 %all-to-all-done.2 = bf16[256,16,64]{0,2,1:T(8,128)(2,1)S(1)} async-done(((bf16[256,16,64]{0,2,1:T(8,128)(2,1)}), bf16[256,16,64]{0,2,1:T(8,128)(2,1)S(1)}, u32[]{:S(2)}, u32[]{:S(2)}) %all-to-all-start.2) | async-done | bytes 524320 | tf_op jit(solution)/shard_map/all_to_all | solution.py:83
  263.0 0.3 copy.42
  263.3 0.2 reshape.50
  263.5 3.2 %fusion.17 = f32[256,4,16]{0,2,1:T(8,128)S(1)} fusion(bf16[4096,4,16]{0,2,1:T(8,128)(2,1)S(1)} %reshape.50, s32[4,4096]{1,0:T(4,128)S(1)} %bitcast.37), kind=kOutput, calls=%fused_computation.25 | convolution fusion | flops 138412032 | bytes 655360 | tf_op jit(solution)/shard_map/mnk,nmj->kmj/dot_general | solution.py:36
  266.7 0.2 concatenate.8
  266.9 0.2 copy.43
  267.2 0.8 pad_maximum_fusion
  267.9 6.4 %all-to-all-start.4 = ((f32[16,16,68]{2,1,0:T(8,128)}), f32[16,16,68]{2,1,0:T(8,128)S(1)}, u32[]{:S(2)}, u32[]{:S(2)}) async-start(f32[16,16,68]{2,1,0:T(8,128)} %pad_maximum_fusion), calls=%async_computation.4 | async-start | bytes 262144 | tf_op jit(solution)/shard_map/all_to_all | solution.py:44
  274.4 0.1 copy.47
  274.5 2.0 copy.50
  276.6 5.7 %all-to-all-done.4 = f32[16,16,68]{2,1,0:T(8,128)S(1)} async-done(((f32[16,16,68]{2,1,0:T(8,128)}), f32[16,16,68]{2,1,0:T(8,128)S(1)}, u32[]{:S(2)}, u32[]{:S(2)}) %all-to-all-start.4) | async-done | bytes 69664 | tf_op jit(solution)/shard_map/all_to_all | solution.py:44
  282.3 0.7 broadcast_in_dim.7
  282.9 3.6 %all-to-all-start.5 = ((f32[16,16,68]{2,1,0:T(8,128)}), f32[16,16,68]{2,1,0:T(8,128)S(1)}, u32[]{:S(2)}, u32[]{:S(2)}) async-start(f32[16,16,68]{2,1,0:T(8,128)} %broadcast_in_dim.7), calls=%async_computation.5 | async-start | bytes 262144 | tf_op jit(solution)/shard_map/all_to_all | solution.py:47
  286.5 1.7 constant_dynamic-slice_fusion
  288.2 6.2 %all-to-all-done.5 = f32[16,16,68]{2,1,0:T(8,128)S(1)} async-done(((f32[16,16,68]{2,1,0:T(8,128)}), f32[16,16,68]{2,1,0:T(8,128)S(1)}, u32[]{:S(2)}, u32[]{:S(2)}) %all-to-all-start.5) | async-done | bytes 69664 | tf_op jit(solution)/shard_map/all_to_all | solution.py:47
  294.4 0.1 slice.9
  294.5 0.1 copy.56
  294.6 0.1 copy.49
  294.7 0.7 copy.51
  (11 shorter events, 0.1 us)
Async XLA Ops:
  7.2 24.1 %copy-start = (bf16[256,1024]{1,0:T(8,128)(2,1)S(1)}, bf16[256,1024]{1,0:T(8,128)(2,1)}, u32[]{:S(2)}) copy-start(bf16[256,1024]{1,0:T(8,128)(2,1)} %param.3) | copy-start | bytes 1572868
  7.2 90.4 %reduce-scatter.4.cloned.1.call-start = ((), (), s32[]{:S(2)}) async-start(), calls=%async_computation.8 | async-start | bytes 4456448 | tf_op jit(solution)/shard_map/reduce_scatter | solution.py:72
  39.3 87.7 %copy-start.2 = (s32[64,256]{1,0:T(8,128)S(1)}, s32[64,256]{1,0:T(8,128)}, u32[]{:S(2)}) copy-start(s32[64,256]{1,0:T(8,128)} %param.4) | copy-start | bytes 196612
  39.3 129.5 %all-gather.2.cloned.1.call-start = ((), (), s32[]{:S(2)}) async-start(), calls=%async_computation.7 | async-start | bytes 4456448 | tf_op jit(solution)/shard_map/all_gather | solution.py:74
  127.7 114.6 %all-to-all-start.3 = ((s32[16,4,256]{2,1,0:T(4,128)}), s32[16,4,256]{2,1,0:T(4,128)S(1)}, u32[]{:S(2)}, u32[]{:S(2)}) async-start(s32[16,4,256]{2,1,0:T(4,128)} %all_to_all.53), calls=%async_computation.3 | async-start | bytes 131072 | tf_op jit(solution)/shard_map/all_to_all | solution.py:66
  242.3 20.7 %all-to-all-start.2 = ((bf16[256,16,64]{0,2,1:T(8,128)(2,1)}), bf16[256,16,64]{0,2,1:T(8,128)(2,1)S(1)}, u32[]{:S(2)}, u32[]{:S(2)}) async-start(bf16[256,16,64]{0,2,1:T(8,128)(2,1)} %bitcast.5), calls=%async_computation.2 | async-start | bytes 1048576 | tf_op jit(solution)/shard_map/all_to_all | solution.py:83
  263.2 11.2 %copy-start.1 = (bf16[256,64]{0,1:T(8,128)(2,1)S(1)}, bf16[256,64]{0,1:T(8,128)(2,1)}, u32[]{:S(2)}) copy-start(bf16[256,64]{0,1:T(8,128)(2,1)} %param.5) | copy-start | bytes 98308
  267.9 14.3 %all-to-all-start.4 = ((f32[16,16,68]{2,1,0:T(8,128)}), f32[16,16,68]{2,1,0:T(8,128)S(1)}, u32[]{:S(2)}, u32[]{:S(2)}) async-start(f32[16,16,68]{2,1,0:T(8,128)} %pad_maximum_fusion), calls=%async_computation.4 | async-start | bytes 262144 | tf_op jit(solution)/shard_map/all_to_all | solution.py:44
  282.9 11.4 %all-to-all-start.5 = ((f32[16,16,68]{2,1,0:T(8,128)}), f32[16,16,68]{2,1,0:T(8,128)S(1)}, u32[]{:S(2)}, u32[]{:S(2)}) async-start(f32[16,16,68]{2,1,0:T(8,128)} %broadcast_in_dim.7), calls=%async_computation.5 | async-start | bytes 262144 | tf_op jit(solution)/shard_map/all_to_all | solution.py:47
Sparse Core Ops, SparseCore 0:
  39.5 58.0 reduce-scatter.3
  127.2 41.5 all-gather.1

commit v3 on v2

--- a/solution.py
+++ b/solution.py
@@ -54,17 +54,34 @@
     )
 
 
-def newton_step(z):
-    z_half = z.astype(jnp.bfloat16)
-    gram = bdot(z_half, z_half, ((1,), (1,)))
-    quartic = bdot(gram, gram, ((1,), (0,)))
-    mixer = coef_b * gram + coef_c * quartic
-    return coef_a * z + bdot(mixer, z_half, ((1,), (0,)))
+def partner(x):
+    count = lax.axis_size("sub")
+    return lax.ppermute(x, "sub", [(i, i ^ 1) for i in range(count)])
+
+
+def newton_half(z_own, z_other_half):
+    own_half = z_own.astype(jnp.bfloat16)
+    gram_own = bdot(own_half, own_half, ((1,), (1,)))
+    gram_cross = bdot(own_half, z_other_half, ((1,), (1,)))
+    gram_other = partner(gram_own.astype(jnp.bfloat16))
+    own_block, cross_block = gram_own.astype(jnp.bfloat16), gram_cross.astype(jnp.bfloat16)
+    quartic_left = bdot(own_block, own_block, ((1,), (0,))) + bdot(cross_block, cross_block, ((1,), (1,)))
+    quartic_right = bdot(own_block, cross_block, ((1,), (0,))) + bdot(cross_block, gram_other, ((1,), (0,)))
+    mixer_left = coef_b * gram_own + coef_c * quartic_left
+    mixer_right = coef_b * gram_cross + coef_c * quartic_right
+    return (
+        coef_a * z_own
+        + bdot(mixer_left, own_half, ((1,), (0,)))
+        + bdot(mixer_right, z_other_half, ((1,), (0,)))
+    )
 
 
 def body(embeddings, codes, codebook):
     moved_codes = lax.all_to_all(codes, "sub", split_axis=0, concat_axis=1, tiled=True)
-    table = lax.all_gather(codebook, "sub", axis=1, tiled=True)
+    groups = lax.axis_size("sub")
+    copies = jnp.broadcast_to(codebook[None], (groups,) + codebook.shape)
+    shards = lax.all_to_all(copies, "sub", split_axis=0, concat_axis=0, tiled=True)
+    table = jnp.transpose(shards, (1, 0, 2)).reshape(codebook.shape[0], groups * codebook.shape[1])
     decoded = decode_rows(codes, table)
     partial = lax.dot_general(
         embeddings, decoded, (((0,), (0,)), ((), ())), preferred_element_type=jnp.float32
@@ -74,9 +91,22 @@
     cross = lax.all_gather(cross_panel, "sub", axis=0, tiled=True)
     frob_scale = jnp.sqrt(jnp.sum(cross * cross)) + frob_eps
     z = cross / frob_scale
+    core = lax.axis_index("sub") % 2
+    panel_rows = z.shape[0] // lax.axis_size("sub")
+    by_parity = z.reshape(-1, 2, panel_rows, z.shape[1])
+    z_own = lax.dynamic_index_in_dim(by_parity, core, axis=1, keepdims=False).reshape(-1, z.shape[1])
+    z_other = lax.dynamic_index_in_dim(by_parity, 1 - core, axis=1, keepdims=False).reshape(-1, z.shape[1])
+    z_other_half = z_other.astype(jnp.bfloat16)
     for newton_step_index in range(NS_STEPS):
-        z = newton_step(z)
-    rotation_half = z.astype(jnp.bfloat16)
+        z_own = newton_half(z_own, z_other_half)
+        z_other_half = partner(z_own.astype(jnp.bfloat16))
+    own_panels = z_own.astype(jnp.bfloat16).reshape(-1, panel_rows, z.shape[1])
+    other_panels = z_other_half.reshape(-1, panel_rows, z.shape[1])
+    rotation_half = jnp.where(
+        core == 0,
+        jnp.stack([own_panels, other_panels], axis=1),
+        jnp.stack([other_panels, own_panels], axis=1),
+    ).reshape(z.shape)
     rotated = jnp.dot(embeddings, rotation_half, preferred_element_type=jnp.float32).astype(
         jnp.bfloat16
     )
@@ -89,8 +119,7 @@
     spread = jnp.repeat(counts, own_codebook.shape[1] // counts.shape[1], axis=1)
     new_codebook = (code_sums + own_codebook) / (spread + 1.0)
     me = lax.axis_index("sub")
-    panel_rows = z.shape[0] // lax.axis_size("sub")
-    panel = lax.dynamic_slice_in_dim(z, me * panel_rows, panel_rows, axis=0)
+    panel = lax.dynamic_index_in_dim(z_own.reshape(-1, panel_rows, z.shape[1]), me // 2, axis=0, keepdims=False)
     return (panel, rotated, new_codebook)
 
 

time: 305 us -> 303 us (level)
  matrix products: 80.1 us -> 57.4 us
  waiting for transfers between devices: 109 us -> 122 us
  other arithmetic: 11.7 us -> 16 us
  blocking collectives: 46.3 us -> 50.3 us
    all_to_all x0 -> x1, blocking collectives: none -> 22.8 us  [body(): lax.all_to_all(copies, 'sub', split_axis=0, concat_axis=0, tiled=True)]
    dot_general x6 -> x18, matrix products: 65.2 us -> 44.6 us  [bdot(): lax.dot_general(left.astype(jnp.bfloat16), right.astype(jnp.bfloat16), (d...]
    all_gather x1 -> x0, blocking collectives: 18.8 us -> none  [body(): table = lax.all_gather(codebook, 'sub', axis=1, tiled=True)]
    all_gather x1, waiting for transfers between devices: 31.4 us -> 41.2 us  [body(): cross = lax.all_gather(cross_panel, 'sub', axis=0, tiled=True)]
    all_to_all x1, waiting for transfers between devices: 0.01 us -> 3.97 us  [body(): lax.all_to_all(codes, 'sub', split_axis=0, concat_axis=1, tiled=True)]
    all_to_all x1, starting transfers between devices: 9.71 us -> 6.02 us  [body(): lax.all_to_all(codes, 'sub', split_axis=0, concat_axis=1, tiled=True)]
    unnamed x11 -> x17, local copies, waits for them, and re-layouts: 8.31 us -> 8.35 us
  transfers between devices with their start and end apart: 6 -> 12, of which waited for: 5 -> 6; matrix products, arithmetic and copies ran while one was open for 28% -> 14% of each run, Pallas kernels for 0% -> 0%
where the time goes in v3:
time: 303 us; the launch traced here: 300 us
  waiting for transfers between devices  122 us (40%)
  matrix products  57.4 us (19%)
  blocking collectives  50.3 us (17%)
  starting transfers between devices  23.6 us (8%)
  other arithmetic  16 us (5%)
  local copies, waits for them, and re-layouts  15.7 us (5%)
  between operations  15 us (5%)
    reduce_scatter x1, waiting for transfers between devices, body(): lax.psum_scatter(partial, 'sub', scatter_dimension=0, tiled=True)  57.1 us
    dot_general x18, matrix products, bdot(): lax.dot_general(left.astype(jnp.bfloat16), right.astype(jnp.bfloat16), (d...  44.6 us
    all_gather x1, waiting for transfers between devices, body(): cross = lax.all_gather(cross_panel, 'sub', axis=0, tiled=True)  41.2 us
    all_to_all x1, blocking collectives, body(): lax.all_to_all(copies, 'sub', split_axis=0, concat_axis=0, tiled=True)  22.8 us
    all_to_all x1, blocking collectives, rows_sum(): lax.all_to_all(x, 'rows', split_axis=0, concat_axis=0, tiled=True)  15 us
    all_to_all x1, blocking collectives, rows_sum(): lax.all_to_all(spread, 'rows', split_axis=0, concat_axis=0, tiled=True)  12.5 us
    unnamed x17, local copies, waits for them, and re-layouts  8.35 us
    all_to_all x1, waiting for transfers between devices, body(): lax.all_to_all(rotated, 'sub', split_axis=1, concat_axis=0, tiled=True)  7.87 us
  transfers between devices with their start and end apart: 12, of which 6 were waited for; matrix products, arithmetic and copies ran while one was open for 14% of the time, Pallas kernels for 0%

profile of v3, /device:TPU:64, one launch (start us, length us, event | category | flops | bytes accessed | tf_op | source)
XLA Modules:
  0.0 299.9 jit_solution(8240723206419444688)
XLA Ops:
  7.2 0.9 broadcast_in_dim.8
  8.1 22.8 %all_to_all.70 = bf16[16,256,64]{1,2,0:T(8,128)(2,1)S(1)} all-to-all(bf16[16,256,64]{1,2,0:T(8,128)(2,1)S(1)} %broadcast_in_dim.8), channel_id=1, replica_groups=mesh['rows'=16,'sub'=16] {'sub'}, dimensions={0} | all-to-all | bytes 1048576 | tf_op jit(solution)/shard_map/all_to_all | solution.py:83
  30.9 5.3 %fusion.16 = bf16[64,256,16]{1,2,0:T(8,128)(2,1)S(1)} fusion(bf16[256,64,16]{0,2,1:T(8,128)(2,1)S(1)} %bitcast.97, s32[64,256]{1,0:T(8,128)} %param.4), kind=kOutput, calls=%fused_computation.35 | convolution fusion | flops 138674176 | bytes 1114112 | tf_op jit(solution)/shard_map/mnk,kmj->nmj/dot_general | solution.py:26
  36.2 2.7 convolution_bitcast_fusion
  38.9 5.4 %copy.73 = f32[1024,1024]{1,0:T(8,128)} copy(f32[1024,1024]{0,1:T(8,128)} %convolution_bitcast_fusion) | data formatting | bytes 8388608
  44.3 57.1 %reduce-scatter.4.cloned.1.call-done = f32[64,1024]{1,0:T(8,128)} async-done(((f32[1024,1024]{1,0:T(8,128)}), f32[64,1024]{1,0:T(8,128)}) %reduce-scatter.4.cloned.1.call-update) | async-done | bytes 262160 | tf_op jit(solution)/shard_map/reduce_scatter | solution.py:89
  101.5 1.0 all_to_all.50
  102.5 15.0 %all_to_all.71 = f32[16,4,1024]{2,1,0:T(4,128)S(1)} all-to-all(f32[16,4,1024]{2,1,0:T(4,128)S(1)} %all_to_all.50), channel_id=1, replica_groups=mesh['rows'=16,'sub'=16] {'rows'}, dimensions={0} | all-to-all | bytes 524288 | tf_op jit(solution)/shard_map/all_to_all | solution.py:44
  117.6 12.5 %all_to_all.72 = f32[16,4,1024]{2,1,0:T(4,128)S(1)} all-to-all(f32[16,4,1024]{2,1,0:T(4,128)S(1)} %broadcast_in_dim.9), channel_id=1, replica_groups=mesh['rows'=16,'sub'=16] {'rows'}, dimensions={0} | all-to-all | bytes 524288 | tf_op jit(solution)/shard_map/all_to_all | solution.py:47
  130.1 0.8 all_to_all.53
  130.9 41.2 %all-gather.2.cloned.1.call-done = f32[1024,1024]{1,0:T(8,128)} async-done(((f32[64,1024]{1,0:T(8,128)}), f32[1024,1024]{1,0:T(8,128)}) %all-gather.2.cloned.1.call-update) | async-done | bytes 4194320 | tf_op jit(solution)/shard_map/all_gather | solution.py:91
  172.1 3.9 %multiply_reduce_fusion = f32[]{:T(128)} fusion(f32[1024,1024]{1,0:T(8,128)} %all-gather.2.cloned.1.call-done), kind=kLoop, calls=%fused_computation.8 | loop fusion | flops 2097151 | bytes 4194308 | tf_op jit(solution)/shard_map/reduce_sum | solution.py:92
  176.7 2.6 broadcast_divide_fusion
  179.6 1.7 fusion.72
  181.6 1.5 fusion.84
  183.0 0.7 fusion.85
  183.8 1.5 fusion.62
  185.2 1.6 dynamic-slice_multiply_fusion
  186.8 4.0 %fusion.23 = f32[512,1024]{1,0:T(8,128)} fusion(bf16[512,1024]{1,0:T(8,128)(2,1)S(1)} %bitcast.83, f32[512,512]{1,0:T(8,128)} %fusion.84, f32[512,512]{1,0:T(8,128)} %get-tuple-element.24, f32[512,512]{1,0:T(8,128)S(1)} %fusion.85), kind=kOutput, calls=%fused_computation.43 | convolution fusion | flops 806879232 | bytes 6291456 | tf_op jit(solution)/shard_map/dot_general | solution.py:51
  190.8 5.5 %fusion.73 = (bf16[512,1024]{1,0:T(8,128)(2,1)S(1)}, f32[512,1024]{1,0:T(8,128)}) fusion(bf16[512,1024]{1,0:T(8,128)(2,1)} %bitcast.87, f32[512,512]{1,0:T(8,128)} %fusion.62, bf16[512,512]{1,0:T(8,128)(2,1)} %collective-permute-done, f32[512,512]{1,0:T(8,128)S(1)} %fusion.85, f32[512,1024]{1,0:T(8,128)} %fusion.23, ...), kind=kOutput, calls=%fused_computation.93 | convolution fusion | flops 808452096 | bytes 11010048 | tf_op jit(solution)/shard_map/dot_general | solution.py:51
  196.5 1.7 fusion.76
  198.5 1.5 fusion.86
  199.9 0.7 fusion.87
  200.7 1.5 fusion.50
  202.1 4.0 %fusion.22 = f32[512,1024]{1,0:T(8,128)} fusion(bf16[512,1024]{1,0:T(8,128)(2,1)S(1)} %get-tuple-element.25, f32[512,512]{1,0:T(8,128)} %fusion.86, f32[512,512]{1,0:T(8,128)} %get-tuple-element.28, f32[512,512]{1,0:T(8,128)S(1)} %fusion.87), kind=kOutput, calls=%fused_computation.42 | convolution fusion | flops 806879232 | bytes 6291456 | tf_op jit(solution)/shard_map/dot_general | solution.py:51
  206.2 5.5 %fusion.77 = (bf16[512,1024]{1,0:T(8,128)(2,1)S(1)}, f32[512,1024]{1,0:T(8,128)}) fusion(bf16[512,1024]{1,0:T(8,128)(2,1)} %copy-done.2, f32[512,512]{1,0:T(8,128)S(1)} %fusion.87, f32[512,512]{1,0:T(8,128)} %fusion.50, bf16[512,512]{1,0:T(8,128)(2,1)} %collective-permute-done.2, f32[512,1024]{1,0:T(8,128)} %fusion.22, f32[512,1024]{1,0:T(8,128)} %get-tuple-element.26), kind=kOutput, calls=%fused_computation.95 | convolution fusion | flops 808976384 | bytes 11010048 | tf_op jit(solution)/shard_map/dot_general | solution.py:51
  211.9 1.7 fusion.80
  213.9 1.5 fusion.88
  215.4 0.7 fusion.89
  216.1 1.5 fusion.44
  217.6 4.0 %fusion.21 = f32[512,1024]{1,0:T(8,128)} fusion(bf16[512,1024]{1,0:T(8,128)(2,1)S(1)} %get-tuple-element.29, f32[512,512]{1,0:T(8,128)} %fusion.88, f32[512,512]{1,0:T(8,128)} %get-tuple-element.32, f32[512,512]{1,0:T(8,128)S(1)} %fusion.89), kind=kOutput, calls=%fused_computation.41 | convolution fusion | flops 806879232 | bytes 6291456 | tf_op jit(solution)/shard_map/dot_general | solution.py:51
  221.5 5.5 %fusion.81 = (bf16[512,1024]{1,0:T(8,128)(2,1)S(1)}, f32[512,1024]{1,0:T(8,128)}) fusion(bf16[512,1024]{1,0:T(8,128)(2,1)} %copy-done.3, f32[512,512]{1,0:T(8,128)S(1)} %fusion.89, f32[512,512]{1,0:T(8,128)} %fusion.44, bf16[512,512]{1,0:T(8,128)(2,1)} %collective-permute-done.4, f32[512,1024]{1,0:T(8,128)} %fusion.21, f32[512,1024]{1,0:T(8,128)} %get-tuple-element.30), kind=kOutput, calls=%fused_computation.97 | convolution fusion | flops 808976384 | bytes 11010048 | tf_op jit(solution)/shard_map/dot_general | solution.py:51
  228.0 6.0 %all-to-all-start.4 = ((s32[16,4,256]{2,1,0:T(4,128)}), s32[16,4,256]{2,1,0:T(4,128)S(1)}, u32[]{:S(2)}, u32[]{:S(2)}) async-start(s32[16,4,256]{2,1,0:T(4,128)} %all_to_all.57), calls=%async_computation.4 | async-start | bytes 131072 | tf_op jit(solution)/shard_map/all_to_all | solution.py:80
  234.2 1.6 convolution_convert_fusion
  235.8 4.0 %all-to-all-done.4 = s32[16,4,256]{2,1,0:T(4,128)S(1)} async-done(((s32[16,4,256]{2,1,0:T(4,128)}), s32[16,4,256]{2,1,0:T(4,128)S(1)}, u32[]{:S(2)}, u32[]{:S(2)}) %all-to-all-start.4) | async-done | bytes 65568 | tf_op jit(solution)/shard_map/all_to_all | solution.py:80
  239.8 5.5 %all-to-all-start.3 = ((bf16[256,16,64]{0,2,1:T(8,128)(2,1)}), bf16[256,16,64]{0,2,1:T(8,128)(2,1)S(1)}, u32[]{:S(2)}, u32[]{:S(2)}) async-start(bf16[256,16,64]{0,2,1:T(8,128)(2,1)} %bitcast.19), calls=%async_computation.3 | async-start | bytes 1048576 | tf_op jit(solution)/shard_map/all_to_all | solution.py:113
  245.3 6.9 %convert_reduce_fusion = f32[4,256]{1,0:T(4,128)S(1)} fusion(s32[4,4096]{1,0:T(4,128)S(1)} %bitcast.99), kind=kLoop, calls=%fused_computation | loop fusion | flops 16776192 | bytes 69632 | tf_op jit(solution)/shard_map/reduce_sum | solution.py:37
  252.3 7.9 %all-to-all-done.3 = bf16[256,16,64]{0,2,1:T(8,128)(2,1)S(1)} async-done(((bf16[256,16,64]{0,2,1:T(8,128)(2,1)}), bf16[256,16,64]{0,2,1:T(8,128)(2,1)S(1)}, u32[]{:S(2)}, u32[]{:S(2)}) %all-to-all-start.3) | async-done | bytes 524320 | tf_op jit(solution)/shard_map/all_to_all | solution.py:113
  260.8 3.2 %fusion.24 = f32[256,4,16]{0,2,1:T(8,128)S(1)} fusion(bf16[4096,4,16]{0,2,1:T(8,128)(2,1)S(1)} %reshape.72, s32[4,4096]{1,0:T(4,128)S(1)} %bitcast.100), kind=kOutput, calls=%fused_computation.44 | convolution fusion | flops 138412032 | bytes 655360 | tf_op jit(solution)/shard_map/mnk,nmj->kmj/dot_general | solution.py:36
  264.4 0.8 pad_maximum_fusion
  265.2 6.8 %all-to-all-start.5 = ((f32[16,16,68]{2,1,0:T(8,128)}), f32[16,16,68]{2,1,0:T(8,128)S(1)}, u32[]{:S(2)}, u32[]{:S(2)}) async-start(f32[16,16,68]{2,1,0:T(8,128)} %pad_maximum_fusion), calls=%async_computation.5 | async-start | bytes 262144 | tf_op jit(solution)/shard_map/all_to_all | solution.py:44
  272.2 7.7 %all-to-all-done.5 = f32[16,16,68]{2,1,0:T(8,128)S(1)} async-done(((f32[16,16,68]{2,1,0:T(8,128)}), f32[16,16,68]{2,1,0:T(8,128)S(1)}, u32[]{:S(2)}, u32[]{:S(2)}) %all-to-all-start.5) | async-done | bytes 69664 | tf_op jit(solution)/shard_map/all_to_all | solution.py:44
  279.9 0.7 broadcast_in_dim.10
  280.6 3.6 %all-to-all-start.6 = ((f32[16,16,68]{2,1,0:T(8,128)}), f32[16,16,68]{2,1,0:T(8,128)S(1)}, u32[]{:S(2)}, u32[]{:S(2)}) async-start(f32[16,16,68]{2,1,0:T(8,128)} %broadcast_in_dim.10), calls=%async_computation.6 | async-start | bytes 262144 | tf_op jit(solution)/shard_map/all_to_all | solution.py:47
  284.2 1.7 dynamic-slice_bitcast_fusion
  285.8 2.0 copy.70
  287.9 4.1 %all-to-all-done.6 = f32[16,16,68]{2,1,0:T(8,128)S(1)} async-done(((f32[16,16,68]{2,1,0:T(8,128)}), f32[16,16,68]{2,1,0:T(8,128)S(1)}, u32[]{:S(2)}, u32[]{:S(2)}) %all-to-all-start.6) | async-done | bytes 69664 | tf_op jit(solution)/shard_map/all_to_all | solution.py:47
  292.3 0.7 copy.71
  (46 shorter events, 4.5 us)
Async XLA Ops:
  7.2 29.0 %copy-start = (bf16[256,1024]{1,0:T(8,128)(2,1)S(1)}, bf16[256,1024]{1,0:T(8,128)(2,1)}, u32[]{:S(2)}) copy-start(bf16[256,1024]{1,0:T(8,128)(2,1)} %param.3) | copy-start | bytes 1572868
  7.2 94.3 %reduce-scatter.4.cloned.1.call-start = ((), (), s32[]{:S(2)}) async-start(), calls=%async_computation.9 | async-start | bytes 4456448 | tf_op jit(solution)/shard_map/reduce_scatter | solution.py:89
  44.3 127.8 %all-gather.2.cloned.1.call-start = ((), (), s32[]{:S(2)}) async-start(), calls=%async_computation.8 | async-start | bytes 4456448 | tf_op jit(solution)/shard_map/all_gather | solution.py:91
  179.6 3.4 %copy-start.1 = (bf16[8,1,64,1024]{3,2,1,0:T(8,128)(2,1)}, bf16[8,1,64,1024]{3,2,1,0:T(8,128)(2,1)S(1)}, u32[]{:S(2)}) copy-start(bf16[8,1,64,1024]{3,2,1,0:T(8,128)(2,1)S(1)} %get-tuple-element.21) | copy-start | bytes 3145732
  181.3 9.4 %collective-permute-start = (bf16[512,512]{1,0:T(8,128)(2,1)S(1)}, bf16[512,512]{1,0:T(8,128)(2,1)}, u32[]{:S(2)}, u32[]{:S(2)}) collective-permute-start(bf16[512,512]{1,0:T(8,128)(2,1)S(1)} %get-tuple-element.23), channel_id=1, source_target_pairs={{0,1},{1,0},{2,3},{3,2},{4,5},{5,4},{6,7},{7,6},{8,9},{9,8},{10,11... | collective-permute-start | bytes 1572872 | tf_op jit(solution)/shard_map/ppermute | solution.py:59
  196.2 3.7 %collective-permute-start.1 = (bf16[512,1024]{1,0:T(8,128)(2,1)S(1)}, bf16[512,1024]{1,0:T(8,128)(2,1)S(1)}, u32[]{:S(2)}, u32[]{:S(2)}) collective-permute-start(bf16[512,1024]{1,0:T(8,128)(2,1)S(1)} %get-tuple-element.25), channel_id=1, source_target_pairs={{0,1},{1,0},{2,3},{3,2},{4,5},{5,4},{6,7},{7,6},{8,9},{9,8},{10,11... | collective-permute-start | bytes 3145736 | tf_op jit(solution)/shard_map/ppermute | solution.py:59
  198.2 7.9 %collective-permute-start.2 = (bf16[512,512]{1,0:T(8,128)(2,1)S(1)}, bf16[512,512]{1,0:T(8,128)(2,1)}, u32[]{:S(2)}, u32[]{:S(2)}) collective-permute-start(bf16[512,512]{1,0:T(8,128)(2,1)S(1)} %get-tuple-element.27), channel_id=1, source_target_pairs={{0,1},{1,0},{2,3},{3,2},{4,5},{5,4},{6,7},{7,6},{8,9},{9,8},{10,11... | collective-permute-start | bytes 1572872 | tf_op jit(solution)/shard_map/ppermute | solution.py:59
  199.9 2.2 copy-start.2
  211.6 3.7 %collective-permute-start.3 = (bf16[512,1024]{1,0:T(8,128)(2,1)S(1)}, bf16[512,1024]{1,0:T(8,128)(2,1)S(1)}, u32[]{:S(2)}, u32[]{:S(2)}) collective-permute-start(bf16[512,1024]{1,0:T(8,128)(2,1)S(1)} %get-tuple-element.29), channel_id=1, source_target_pairs={{0,1},{1,0},{2,3},{3,2},{4,5},{5,4},{6,7},{7,6},{8,9},{9,8},{10,11... | collective-permute-start | bytes 3145736 | tf_op jit(solution)/shard_map/ppermute | solution.py:59
  213.7 7.9 %collective-permute-start.4 = (bf16[512,512]{1,0:T(8,128)(2,1)S(1)}, bf16[512,512]{1,0:T(8,128)(2,1)}, u32[]{:S(2)}, u32[]{:S(2)}) collective-permute-start(bf16[512,512]{1,0:T(8,128)(2,1)S(1)} %get-tuple-element.31), channel_id=1, source_target_pairs={{0,1},{1,0},{2,3},{3,2},{4,5},{5,4},{6,7},{7,6},{8,9},{9,8},{10,11... | collective-permute-start | bytes 1572872 | tf_op jit(solution)/shard_map/ppermute | solution.py:59
  215.4 2.2 copy-start.3
  221.5 5.8 %copy-start.5 = (s32[64,256]{1,0:T(8,128)S(1)}, s32[64,256]{1,0:T(8,128)}, u32[]{:S(2)}) copy-start(s32[64,256]{1,0:T(8,128)} %param.4) | copy-start | bytes 196612
  227.0 7.0 %collective-permute-start.5 = (bf16[512,1024]{1,0:T(8,128)(2,1)S(1)}, bf16[512,1024]{1,0:T(8,128)(2,1)S(1)}, u32[]{:S(2)}, u32[]{:S(2)}) collective-permute-start(bf16[512,1024]{1,0:T(8,128)(2,1)S(1)} %get-tuple-element.33), channel_id=1, source_target_pairs={{0,1},{1,0},{2,3},{3,2},{4,5},{5,4},{6,7},{7,6},{8,9},{9,8},{10,11... | collective-permute-start | bytes 3145736 | tf_op jit(solution)/shard_map/ppermute | solution.py:59
  228.0 11.8 %all-to-all-start.4 = ((s32[16,4,256]{2,1,0:T(4,128)}), s32[16,4,256]{2,1,0:T(4,128)S(1)}, u32[]{:S(2)}, u32[]{:S(2)}) async-start(s32[16,4,256]{2,1,0:T(4,128)} %all_to_all.57), calls=%async_computation.4 | async-start | bytes 131072 | tf_op jit(solution)/shard_map/all_to_all | solution.py:80
  239.8 20.5 %all-to-all-start.3 = ((bf16[256,16,64]{0,2,1:T(8,128)(2,1)}), bf16[256,16,64]{0,2,1:T(8,128)(2,1)S(1)}, u32[]{:S(2)}, u32[]{:S(2)}) async-start(bf16[256,16,64]{0,2,1:T(8,128)(2,1)} %bitcast.19), calls=%async_computation.3 | async-start | bytes 1048576 | tf_op jit(solution)/shard_map/all_to_all | solution.py:113
  260.8 11.3 %copy-start.4 = (bf16[256,64]{0,1:T(8,128)(2,1)S(1)}, bf16[256,64]{0,1:T(8,128)(2,1)}, u32[]{:S(2)}) copy-start(bf16[256,64]{0,1:T(8,128)(2,1)} %param.5) | copy-start | bytes 98308
  265.2 14.7 %all-to-all-start.5 = ((f32[16,16,68]{2,1,0:T(8,128)}), f32[16,16,68]{2,1,0:T(8,128)S(1)}, u32[]{:S(2)}, u32[]{:S(2)}) async-start(f32[16,16,68]{2,1,0:T(8,128)} %pad_maximum_fusion), calls=%async_computation.5 | async-start | bytes 262144 | tf_op jit(solution)/shard_map/all_to_all | solution.py:44
  280.6 11.4 %all-to-all-start.6 = ((f32[16,16,68]{2,1,0:T(8,128)}), f32[16,16,68]{2,1,0:T(8,128)S(1)}, u32[]{:S(2)}, u32[]{:S(2)}) async-start(f32[16,16,68]{2,1,0:T(8,128)} %broadcast_in_dim.10), calls=%async_computation.6 | async-start | bytes 262144 | tf_op jit(solution)/shard_map/all_to_all | solution.py:47
Sparse Core Ops, SparseCore 0:
  44.4 56.9 reduce-scatter.3
  131.0 41.0 all-gather.1

commit v4 on v3

--- a/solution.py
+++ b/solution.py
@@ -27,15 +27,14 @@
     return picked.reshape(local_rows, row_width).astype(jnp.bfloat16)
 
 
-def codeword_totals(codes, row_values, count_codes):
+def codeword_sums(codes, row_values, count_codes):
     subspaces, local_rows = codes.shape
     row_width = row_values.shape[1]
     sub_width = row_width // subspaces
     one_hot = one_hot_codes(codes, count_codes)
     pieces = row_values.reshape(local_rows, subspaces, sub_width)
     code_sums = jnp.einsum("mnk,nmj->kmj", one_hot, pieces, preferred_element_type=jnp.float32)
-    counts = jnp.sum(one_hot, axis=1, dtype=jnp.float32).T
-    return code_sums.reshape(count_codes, row_width), counts
+    return code_sums.reshape(count_codes, row_width)
 
 
 def rows_sum(x):
@@ -78,15 +77,15 @@
 
 def body(embeddings, codes, codebook):
     moved_codes = lax.all_to_all(codes, "sub", split_axis=0, concat_axis=1, tiled=True)
-    groups = lax.axis_size("sub")
-    copies = jnp.broadcast_to(codebook[None], (groups,) + codebook.shape)
-    shards = lax.all_to_all(copies, "sub", split_axis=0, concat_axis=0, tiled=True)
-    table = jnp.transpose(shards, (1, 0, 2)).reshape(codebook.shape[0], groups * codebook.shape[1])
+    table = lax.all_gather(codebook, "sub", axis=1, tiled=True)
     decoded = decode_rows(codes, table)
-    partial = lax.dot_general(
-        embeddings, decoded, (((0,), (0,)), ((), ())), preferred_element_type=jnp.float32
+    partial_t = lax.dot_general(
+        decoded, embeddings, (((0,), (0,)), ((), ())), preferred_element_type=jnp.float32
     )
-    partial_panel = lax.psum_scatter(partial, "sub", scatter_dimension=0, tiled=True)
+    partial_panel = lax.psum_scatter(partial_t, "sub", scatter_dimension=1, tiled=True).T
+    code_one_hot = one_hot_codes(moved_codes, table.shape[0])
+    counts = jnp.sum(code_one_hot, axis=1, dtype=jnp.float32).T
+    partial_panel, moved_codes, counts = lax.optimization_barrier((partial_panel, moved_codes, counts))
     cross_panel = rows_sum(partial_panel)
     cross = lax.all_gather(cross_panel, "sub", axis=0, tiled=True)
     frob_scale = jnp.sqrt(jnp.sum(cross * cross)) + frob_eps
@@ -111,7 +110,7 @@
         jnp.bfloat16
     )
     moved_rows = lax.all_to_all(rotated, "sub", split_axis=1, concat_axis=0, tiled=True)
-    code_sums, counts = codeword_totals(moved_codes, moved_rows, table.shape[0])
+    code_sums = codeword_sums(moved_codes, moved_rows, table.shape[0])
     sums_width = code_sums.shape[1]
     totals = rows_sum(jnp.concatenate([code_sums, counts], axis=1))
     code_sums, counts = totals[:, :sums_width], totals[:, sums_width:]

time: 303 us -> 286 us (0.944)
  waiting for transfers between devices: 122 us -> 109 us
  blocking collectives: 50.3 us -> 58.2 us
  local copies, waits for them, and re-layouts: 15.7 us -> 9.58 us
  starting transfers between devices: 23.6 us -> 18.1 us
    all_gather x0 -> x1, blocking collectives: none -> 18.8 us  [body(): table = lax.all_gather(codebook, 'sub', axis=1, tiled=True)]
    reduce_scatter x1, waiting for transfers between devices: 57.1 us -> 38.6 us  [body(): lax.psum_scatter(partial_t, 'sub', scatter_dimension=1, tiled=True)]
    all_to_all x1, blocking collectives: 22.8 us -> 11.9 us  [body(): lax.all_to_all(codes, 'sub', split_axis=0, concat_axis=1, tiled=True)]
    all_to_all x1, waiting for transfers between devices: 7.87 us -> 14.8 us  [body(): lax.all_to_all(rotated, 'sub', split_axis=1, concat_axis=0, tiled=True)]
    all_to_all x1 -> x0, starting transfers between devices: 6.02 us -> none  [body(): lax.all_to_all(codes, 'sub', split_axis=0, concat_axis=1, tiled=True)]
    unnamed x17 -> x16, local copies, waits for them, and re-layouts: 8.35 us -> 3.74 us
    all_to_all x1 -> x0, waiting for transfers between devices: 3.97 us -> none  [body(): lax.all_to_all(codes, 'sub', split_axis=0, concat_axis=1, tiled=True)]
  transfers between devices with their start and end apart: 12 -> 11, of which waited for: 6 -> 6; matrix products, arithmetic and copies ran while one was open for 14% -> 14% of each run, Pallas kernels for 0% -> 0%
where the time goes in v4:
time: 286 us; the launch traced here: 283 us
  waiting for transfers between devices  109 us (38%)
  blocking collectives  58.2 us (20%)
  matrix products  57.4 us (20%)
  starting transfers between devices  18.1 us (6%)
  other arithmetic  16 us (6%)
  between operations  15 us (5%)
  local copies, waits for them, and re-layouts  9.58 us (3%)
    dot_general x18, matrix products, bdot(): lax.dot_general(left.astype(jnp.bfloat16), right.astype(jnp.bfloat16), (d...  44.6 us
    all_gather x1, waiting for transfers between devices, body(): cross = lax.all_gather(cross_panel, 'sub', axis=0, tiled=True)  41.1 us
    reduce_scatter x1, waiting for transfers between devices, body(): lax.psum_scatter(partial_t, 'sub', scatter_dimension=1, tiled=True)  38.6 us
    all_gather x1, blocking collectives, body(): table = lax.all_gather(codebook, 'sub', axis=1, tiled=True)  18.8 us
    all_to_all x1, blocking collectives, rows_sum(): lax.all_to_all(x, 'rows', split_axis=0, concat_axis=0, tiled=True)  15.1 us
    all_to_all x1, waiting for transfers between devices, body(): lax.all_to_all(rotated, 'sub', split_axis=1, concat_axis=0, tiled=True)  14.8 us
    all_to_all x1, blocking collectives, rows_sum(): lax.all_to_all(spread, 'rows', split_axis=0, concat_axis=0, tiled=True)  12.4 us
    all_to_all x1, blocking collectives, body(): lax.all_to_all(codes, 'sub', split_axis=0, concat_axis=1, tiled=True)  11.9 us
  transfers between devices with their start and end apart: 11, of which 6 were waited for; matrix products, arithmetic and copies ran while one was open for 14% of the time, Pallas kernels for 0%

profile of v4, /device:TPU:64, one launch (start us, length us, event | category | flops | bytes accessed | tf_op | source)
XLA Modules:
  0.0 282.9 jit_solution(4938832556385207143)
XLA Ops:
  7.2 18.8 %all_gather.6 = bf16[256,1024]{0,1:T(8,128)(2,1)S(1)} all-gather(bf16[256,64]{0,1:T(8,128)(2,1)} %param.5), channel_id=1, replica_groups=mesh['rows'=16,'sub'=16] {'sub'}, dimensions={1}, use_global_device_ids=true | all-gather | bytes 557056 | tf_op jit(solution)/shard_map/all_gather | solution.py:80
  26.0 5.3 %fusion.16 = bf16[64,256,16]{1,2,0:T(8,128)(2,1)S(1)} fusion(bf16[256,64,16]{0,2,1:T(8,128)(2,1)S(1)} %bitcast.93, s32[64,256]{1,0:T(8,128)} %param.4), kind=kOutput, calls=%fused_computation.35 | convolution fusion | flops 138674176 | bytes 1114112 | tf_op jit(solution)/shard_map/mnk,kmj->nmj/dot_general | solution.py:26
  31.3 2.7 fusion.84
  34.1 0.8 copy-done.5
  34.9 11.9 %all_to_all.68 = s32[16,4,256]{2,1,0:T(4,128)S(1)} all-to-all(s32[16,4,256]{2,1,0:T(4,128)S(1)} %all_to_all.48), channel_id=1, replica_groups=mesh['rows'=16,'sub'=16] {'sub'}, dimensions={0} | all-to-all | bytes 131072 | tf_op jit(solution)/shard_map/all_to_all | solution.py:79
  46.7 6.9 %convert_reduce_fusion = f32[4,256]{1,0:T(4,128)S(1)} fusion(s32[4,4096]{1,0:T(4,128)S(1)} %bitcast.96), kind=kLoop, calls=%fused_computation.1 | loop fusion | flops 16776192 | bytes 69632 | tf_op jit(solution)/shard_map/reduce_sum | solution.py:87
  53.6 38.6 %reduce-scatter.2.cloned.1.call-done = f32[1024,64]{0,1:T(8,128)} async-done(((f32[1024,1024]{0,1:T(8,128)}), f32[1024,64]{0,1:T(8,128)}) %reduce-scatter.2.cloned.1.call-update) | async-done | bytes 262160 | tf_op jit(solution)/shard_map/reduce_scatter | solution.py:85
  92.2 1.0 all_to_all.52
  93.3 15.1 %all_to_all.69 = f32[16,4,1024]{2,1,0:T(4,128)S(1)} all-to-all(f32[16,4,1024]{2,1,0:T(4,128)S(1)} %all_to_all.52), channel_id=1, replica_groups=mesh['rows'=16,'sub'=16] {'rows'}, dimensions={0} | all-to-all | bytes 524288 | tf_op jit(solution)/shard_map/all_to_all | solution.py:43
  108.5 12.4 %all_to_all.70 = f32[16,4,1024]{2,1,0:T(4,128)S(1)} all-to-all(f32[16,4,1024]{2,1,0:T(4,128)S(1)} %broadcast_in_dim.6), channel_id=1, replica_groups=mesh['rows'=16,'sub'=16] {'rows'}, dimensions={0} | all-to-all | bytes 524288 | tf_op jit(solution)/shard_map/all_to_all | solution.py:46
  120.9 0.8 all_to_all.55
  121.7 41.1 %all-gather.2.cloned.1.call-done = f32[1024,1024]{1,0:T(8,128)} async-done(((f32[64,1024]{1,0:T(8,128)}), f32[1024,1024]{1,0:T(8,128)}) %all-gather.2.cloned.1.call-update) | async-done | bytes 4194320 | tf_op jit(solution)/shard_map/all_gather | solution.py:90
  162.9 3.9 %multiply_reduce_fusion = f32[]{:T(128)} fusion(f32[1024,1024]{1,0:T(8,128)} %all-gather.2.cloned.1.call-done), kind=kLoop, calls=%fused_computation.9 | loop fusion | flops 2097151 | bytes 4194308 | tf_op jit(solution)/shard_map/reduce_sum | solution.py:91
  167.4 2.6 broadcast_divide_fusion
  170.1 0.3 dynamic-slice_convert_fusion
  170.4 1.7 fusion.72
  172.4 1.5 fusion.85
  173.8 0.7 fusion.86
  174.6 1.5 fusion.62
  176.0 1.5 dynamic-slice_multiply_fusion
  177.6 4.0 %fusion.23 = f32[512,1024]{1,0:T(8,128)} fusion(bf16[512,1024]{1,0:T(8,128)(2,1)S(1)} %bitcast.79, f32[512,512]{1,0:T(8,128)} %fusion.85, f32[512,512]{1,0:T(8,128)} %get-tuple-element.30, f32[512,512]{1,0:T(8,128)S(1)} %fusion.86), kind=kOutput, calls=%fused_computation.43 | convolution fusion | flops 806879232 | bytes 6291456 | tf_op jit(solution)/shard_map/dot_general | solution.py:50
  181.6 5.5 %fusion.73 = (bf16[512,1024]{1,0:T(8,128)(2,1)S(1)}, f32[512,1024]{1,0:T(8,128)}) fusion(bf16[512,1024]{1,0:T(8,128)(2,1)} %bitcast.83, f32[512,512]{1,0:T(8,128)} %fusion.62, bf16[512,512]{1,0:T(8,128)(2,1)} %collective-permute-done, f32[512,512]{1,0:T(8,128)S(1)} %fusion.86, f32[512,1024]{1,0:T(8,128)} %fusion.23, ...), kind=kOutput, calls=%fused_computation.93 | convolution fusion | flops 808452096 | bytes 11010048 | tf_op jit(solution)/shard_map/dot_general | solution.py:50
  187.3 1.7 fusion.76
  189.3 1.5 fusion.87
  190.8 0.7 fusion.88
  191.5 1.5 fusion.50
  193.0 4.0 %fusion.22 = f32[512,1024]{1,0:T(8,128)} fusion(bf16[512,1024]{1,0:T(8,128)(2,1)S(1)} %get-tuple-element.31, f32[512,512]{1,0:T(8,128)} %fusion.87, f32[512,512]{1,0:T(8,128)} %get-tuple-element.34, f32[512,512]{1,0:T(8,128)S(1)} %fusion.88), kind=kOutput, calls=%fused_computation.42 | convolution fusion | flops 806879232 | bytes 6291456 | tf_op jit(solution)/shard_map/dot_general | solution.py:50
  197.0 5.5 %fusion.77 = (bf16[512,1024]{1,0:T(8,128)(2,1)S(1)}, f32[512,1024]{1,0:T(8,128)}) fusion(bf16[512,1024]{1,0:T(8,128)(2,1)} %copy-done.2, f32[512,512]{1,0:T(8,128)S(1)} %fusion.88, f32[512,512]{1,0:T(8,128)} %fusion.50, bf16[512,512]{1,0:T(8,128)(2,1)} %collective-permute-done.2, f32[512,1024]{1,0:T(8,128)} %fusion.22, f32[512,1024]{1,0:T(8,128)} %get-tuple-element.32), kind=kOutput, calls=%fused_computation.95 | convolution fusion | flops 808976384 | bytes 11010048 | tf_op jit(solution)/shard_map/dot_general | solution.py:50
  202.8 1.7 fusion.80
  204.7 1.5 fusion.89
  206.2 0.7 fusion.90
  206.9 1.5 fusion.44
  208.4 4.0 %fusion.21 = f32[512,1024]{1,0:T(8,128)} fusion(bf16[512,1024]{1,0:T(8,128)(2,1)S(1)} %get-tuple-element.35, f32[512,512]{1,0:T(8,128)} %fusion.89, f32[512,512]{1,0:T(8,128)} %get-tuple-element.38, f32[512,512]{1,0:T(8,128)S(1)} %fusion.90), kind=kOutput, calls=%fused_computation.41 | convolution fusion | flops 806879232 | bytes 6291456 | tf_op jit(solution)/shard_map/dot_general | solution.py:50
  212.4 5.5 %fusion.81 = (bf16[512,1024]{1,0:T(8,128)(2,1)S(1)}, f32[512,1024]{1,0:T(8,128)}) fusion(bf16[512,1024]{1,0:T(8,128)(2,1)} %copy-done.3, f32[512,512]{1,0:T(8,128)S(1)} %fusion.90, f32[512,512]{1,0:T(8,128)} %fusion.44, bf16[512,512]{1,0:T(8,128)(2,1)} %collective-permute-done.4, f32[512,1024]{1,0:T(8,128)} %fusion.21, f32[512,1024]{1,0:T(8,128)} %get-tuple-element.36), kind=kOutput, calls=%fused_computation.97 | convolution fusion | flops 808976384 | bytes 11010048 | tf_op jit(solution)/shard_map/dot_general | solution.py:50
  218.2 2.4 collective-permute-done.5
  220.7 1.6 convolution_convert_fusion
  222.3 6.0 %all-to-all-start.3 = ((bf16[256,16,64]{0,2,1:T(8,128)(2,1)}), bf16[256,16,64]{0,2,1:T(8,128)(2,1)S(1)}, u32[]{:S(2)}, u32[]{:S(2)}) async-start(bf16[256,16,64]{0,2,1:T(8,128)(2,1)} %bitcast.22), calls=%async_computation.4 | async-start | bytes 1048576 | tf_op jit(solution)/shard_map/all_to_all | solution.py:112
  228.5 14.8 %all-to-all-done.3 = bf16[256,16,64]{0,2,1:T(8,128)(2,1)S(1)} async-done(((bf16[256,16,64]{0,2,1:T(8,128)(2,1)}), bf16[256,16,64]{0,2,1:T(8,128)(2,1)S(1)}, u32[]{:S(2)}, u32[]{:S(2)}) %all-to-all-start.3) | async-done | bytes 524320 | tf_op jit(solution)/shard_map/all_to_all | solution.py:112
  243.8 3.2 %fusion.24 = f32[256,4,16]{0,2,1:T(8,128)S(1)} fusion(bf16[4096,4,16]{0,2,1:T(8,128)(2,1)S(1)} %reshape.76, s32[4,4096]{1,0:T(4,128)S(1)} %bitcast.97), kind=kOutput, calls=%fused_computation.44 | convolution fusion | flops 138412032 | bytes 655360 | tf_op jit(solution)/shard_map/mnk,nmj->kmj/dot_general | solution.py:36
  247.4 0.8 pad_maximum_fusion
  248.2 6.8 %all-to-all-start.4 = ((f32[16,16,68]{2,1,0:T(8,128)}), f32[16,16,68]{2,1,0:T(8,128)S(1)}, u32[]{:S(2)}, u32[]{:S(2)}) async-start(f32[16,16,68]{2,1,0:T(8,128)} %pad_maximum_fusion), calls=%async_computation.5 | async-start | bytes 262144 | tf_op jit(solution)/shard_map/all_to_all | solution.py:43
  255.2 7.7 %all-to-all-done.4 = f32[16,16,68]{2,1,0:T(8,128)S(1)} async-done(((f32[16,16,68]{2,1,0:T(8,128)}), f32[16,16,68]{2,1,0:T(8,128)S(1)}, u32[]{:S(2)}, u32[]{:S(2)}) %all-to-all-start.4) | async-done | bytes 69664 | tf_op jit(solution)/shard_map/all_to_all | solution.py:43
  262.9 0.7 broadcast_in_dim.7
  263.6 3.6 %all-to-all-start.5 = ((f32[16,16,68]{2,1,0:T(8,128)}), f32[16,16,68]{2,1,0:T(8,128)S(1)}, u32[]{:S(2)}, u32[]{:S(2)}) async-start(f32[16,16,68]{2,1,0:T(8,128)} %broadcast_in_dim.7), calls=%async_computation.6 | async-start | bytes 262144 | tf_op jit(solution)/shard_map/all_to_all | solution.py:46
  267.2 1.7 dynamic-slice_bitcast_fusion
  268.8 2.0 copy.65
  270.9 4.1 %all-to-all-done.5 = f32[16,16,68]{2,1,0:T(8,128)S(1)} async-done(((f32[16,16,68]{2,1,0:T(8,128)}), f32[16,16,68]{2,1,0:T(8,128)S(1)}, u32[]{:S(2)}, u32[]{:S(2)}) %all-to-all-start.5) | async-done | bytes 69664 | tf_op jit(solution)/shard_map/all_to_all | solution.py:46
  275.4 0.7 copy.66
  (43 shorter events, 3.6 us)
Async XLA Ops:
  7.2 24.1 %copy-start = (bf16[256,1024]{1,0:T(8,128)(2,1)S(1)}, bf16[256,1024]{1,0:T(8,128)(2,1)}, u32[]{:S(2)}) copy-start(bf16[256,1024]{1,0:T(8,128)(2,1)} %param.3) | copy-start | bytes 1572868
  7.2 85.1 %reduce-scatter.2.cloned.1.call-start = ((), (), s32[]{:S(2)}) async-start(), calls=%async_computation.7 | async-start | bytes 4456448 | tf_op jit(solution)/shard_map/reduce_scatter | solution.py:85
  34.0 0.8 copy-start.5
  34.0 128.8 %all-gather.2.cloned.1.call-start = ((), (), s32[]{:S(2)}) async-start(), calls=%async_computation.8 | async-start | bytes 4456448 | tf_op jit(solution)/shard_map/all_gather | solution.py:90
  170.4 3.5 %copy-start.1 = (bf16[8,1,64,1024]{3,2,1,0:T(8,128)(2,1)}, bf16[8,1,64,1024]{3,2,1,0:T(8,128)(2,1)S(1)}, u32[]{:S(2)}) copy-start(bf16[8,1,64,1024]{3,2,1,0:T(8,128)(2,1)S(1)} %get-tuple-element.27) | copy-start | bytes 3145732
  172.1 9.4 %collective-permute-start = (bf16[512,512]{1,0:T(8,128)(2,1)S(1)}, bf16[512,512]{1,0:T(8,128)(2,1)}, u32[]{:S(2)}, u32[]{:S(2)}) collective-permute-start(bf16[512,512]{1,0:T(8,128)(2,1)S(1)} %get-tuple-element.29), channel_id=1, source_target_pairs={{0,1},{1,0},{2,3},{3,2},{4,5},{5,4},{6,7},{7,6},{8,9},{9,8},{10,11... | collective-permute-start | bytes 1572872 | tf_op jit(solution)/shard_map/ppermute | solution.py:58
  187.0 3.7 %collective-permute-start.1 = (bf16[512,1024]{1,0:T(8,128)(2,1)S(1)}, bf16[512,1024]{1,0:T(8,128)(2,1)S(1)}, u32[]{:S(2)}, u32[]{:S(2)}) collective-permute-start(bf16[512,1024]{1,0:T(8,128)(2,1)S(1)} %get-tuple-element.31), channel_id=1, source_target_pairs={{0,1},{1,0},{2,3},{3,2},{4,5},{5,4},{6,7},{7,6},{8,9},{9,8},{10,11... | collective-permute-start | bytes 3145736 | tf_op jit(solution)/shard_map/ppermute | solution.py:58
  189.1 7.9 %collective-permute-start.2 = (bf16[512,512]{1,0:T(8,128)(2,1)S(1)}, bf16[512,512]{1,0:T(8,128)(2,1)}, u32[]{:S(2)}, u32[]{:S(2)}) collective-permute-start(bf16[512,512]{1,0:T(8,128)(2,1)S(1)} %get-tuple-element.33), channel_id=1, source_target_pairs={{0,1},{1,0},{2,3},{3,2},{4,5},{5,4},{6,7},{7,6},{8,9},{9,8},{10,11... | collective-permute-start | bytes 1572872 | tf_op jit(solution)/shard_map/ppermute | solution.py:58
  190.8 2.2 copy-start.2
  202.5 3.7 %collective-permute-start.3 = (bf16[512,1024]{1,0:T(8,128)(2,1)S(1)}, bf16[512,1024]{1,0:T(8,128)(2,1)S(1)}, u32[]{:S(2)}, u32[]{:S(2)}) collective-permute-start(bf16[512,1024]{1,0:T(8,128)(2,1)S(1)} %get-tuple-element.35), channel_id=1, source_target_pairs={{0,1},{1,0},{2,3},{3,2},{4,5},{5,4},{6,7},{7,6},{8,9},{9,8},{10,11... | collective-permute-start | bytes 3145736 | tf_op jit(solution)/shard_map/ppermute | solution.py:58
  204.5 7.9 %collective-permute-start.4 = (bf16[512,512]{1,0:T(8,128)(2,1)S(1)}, bf16[512,512]{1,0:T(8,128)(2,1)}, u32[]{:S(2)}, u32[]{:S(2)}) collective-permute-start(bf16[512,512]{1,0:T(8,128)(2,1)S(1)} %get-tuple-element.37), channel_id=1, source_target_pairs={{0,1},{1,0},{2,3},{3,2},{4,5},{5,4},{6,7},{7,6},{8,9},{9,8},{10,11... | collective-permute-start | bytes 1572872 | tf_op jit(solution)/shard_map/ppermute | solution.py:58
  206.2 2.2 copy-start.3
  217.9 2.7 collective-permute-start.5
  222.3 20.9 %all-to-all-start.3 = ((bf16[256,16,64]{0,2,1:T(8,128)(2,1)}), bf16[256,16,64]{0,2,1:T(8,128)(2,1)S(1)}, u32[]{:S(2)}, u32[]{:S(2)}) async-start(bf16[256,16,64]{0,2,1:T(8,128)(2,1)} %bitcast.22), calls=%async_computation.4 | async-start | bytes 1048576 | tf_op jit(solution)/shard_map/all_to_all | solution.py:112
  243.8 11.3 %copy-start.4 = (bf16[256,64]{0,1:T(8,128)(2,1)S(1)}, bf16[256,64]{0,1:T(8,128)(2,1)}, u32[]{:S(2)}) copy-start(bf16[256,64]{0,1:T(8,128)(2,1)} %param.5) | copy-start | bytes 98308
  248.2 14.7 %all-to-all-start.4 = ((f32[16,16,68]{2,1,0:T(8,128)}), f32[16,16,68]{2,1,0:T(8,128)S(1)}, u32[]{:S(2)}, u32[]{:S(2)}) async-start(f32[16,16,68]{2,1,0:T(8,128)} %pad_maximum_fusion), calls=%async_computation.5 | async-start | bytes 262144 | tf_op jit(solution)/shard_map/all_to_all | solution.py:43
  263.6 11.4 %all-to-all-start.5 = ((f32[16,16,68]{2,1,0:T(8,128)}), f32[16,16,68]{2,1,0:T(8,128)S(1)}, u32[]{:S(2)}, u32[]{:S(2)}) async-start(f32[16,16,68]{2,1,0:T(8,128)} %broadcast_in_dim.7), calls=%async_computation.6 | async-start | bytes 262144 | tf_op jit(solution)/shard_map/all_to_all | solution.py:46
Sparse Core Ops, SparseCore 0:
  34.2 58.0 reduce-scatter.1
  121.8 41.0 all-gather.1

commit v5 on v4

--- a/solution.py
+++ b/solution.py
@@ -87,25 +87,28 @@
     counts = jnp.sum(code_one_hot, axis=1, dtype=jnp.float32).T
     partial_panel, moved_codes, counts = lax.optimization_barrier((partial_panel, moved_codes, counts))
     cross_panel = rows_sum(partial_panel)
-    cross = lax.all_gather(cross_panel, "sub", axis=0, tiled=True)
-    frob_scale = jnp.sqrt(jnp.sum(cross * cross)) + frob_eps
-    z = cross / frob_scale
+    panel_rows, width = cross_panel.shape
+    squares = jnp.broadcast_to(jnp.sum(cross_panel * cross_panel), (8, width))
+    gathered = lax.all_gather(jnp.concatenate([cross_panel, squares], axis=0), "sub", axis=0, tiled=True)
+    gathered = gathered.reshape(-1, panel_rows + 8, width)
+    frob_scale = jnp.sqrt(jnp.sum(gathered[:, panel_rows, 0])) + frob_eps
     core = lax.axis_index("sub") % 2
-    panel_rows = z.shape[0] // lax.axis_size("sub")
-    by_parity = z.reshape(-1, 2, panel_rows, z.shape[1])
-    z_own = lax.dynamic_index_in_dim(by_parity, core, axis=1, keepdims=False).reshape(-1, z.shape[1])
-    z_other = lax.dynamic_index_in_dim(by_parity, 1 - core, axis=1, keepdims=False).reshape(-1, z.shape[1])
+    by_parity = gathered.reshape(-1, 2, panel_rows + 8, width)
+    own_rows = lax.dynamic_index_in_dim(by_parity, core, axis=1, keepdims=False)
+    other_rows = lax.dynamic_index_in_dim(by_parity, 1 - core, axis=1, keepdims=False)
+    z_own = own_rows[:, :panel_rows, :].reshape(-1, width) / frob_scale
+    z_other = other_rows[:, :panel_rows, :].reshape(-1, width) / frob_scale
     z_other_half = z_other.astype(jnp.bfloat16)
     for newton_step_index in range(NS_STEPS):
         z_own = newton_half(z_own, z_other_half)
         z_other_half = partner(z_own.astype(jnp.bfloat16))
-    own_panels = z_own.astype(jnp.bfloat16).reshape(-1, panel_rows, z.shape[1])
-    other_panels = z_other_half.reshape(-1, panel_rows, z.shape[1])
+    own_panels = z_own.astype(jnp.bfloat16).reshape(-1, panel_rows, width)
+    other_panels = z_other_half.reshape(-1, panel_rows, width)
     rotation_half = jnp.where(
         core == 0,
         jnp.stack([own_panels, other_panels], axis=1),
         jnp.stack([other_panels, own_panels], axis=1),
-    ).reshape(z.shape)
+    ).reshape(-1, width)
     rotated = jnp.dot(embeddings, rotation_half, preferred_element_type=jnp.float32).astype(
         jnp.bfloat16
     )
@@ -118,7 +121,7 @@
     spread = jnp.repeat(counts, own_codebook.shape[1] // counts.shape[1], axis=1)
     new_codebook = (code_sums + own_codebook) / (spread + 1.0)
     me = lax.axis_index("sub")
-    panel = lax.dynamic_index_in_dim(z_own.reshape(-1, panel_rows, z.shape[1]), me // 2, axis=0, keepdims=False)
+    panel = lax.dynamic_index_in_dim(z_own.reshape(-1, panel_rows, width), me // 2, axis=0, keepdims=False)
     return (panel, rotated, new_codebook)
 
 

time: 286 us -> 286 us (level)
  other arithmetic: 16 us -> 12.2 us
  local copies, waits for them, and re-layouts: 9.58 us -> 13 us
    squeeze x1 -> x2, local copies, waits for them, and re-layouts: 1.68 us -> 4.78 us  [the longest x1 3.1 us: body(): lax.dynamic_index_in_dim(by_parity, 1 - core, axis=1, keepdims=False)]
  transfers between devices with their start and end apart: 11 -> 11, of which waited for: 6 -> 6; matrix products, arithmetic and copies ran while one was open for 14% -> 13% of each run, Pallas kernels for 0% -> 0%
where the time goes in v5:
time: 286 us; the launch traced here: 283 us
  waiting for transfers between devices  110 us (38%)
  blocking collectives  58.2 us (20%)
  matrix products  57.4 us (20%)
  starting transfers between devices  17.9 us (6%)
  between operations  15 us (5%)
  local copies, waits for them, and re-layouts  13 us (5%)
  other arithmetic  12.2 us (4%)
    dot_general x18, matrix products, bdot(): lax.dot_general(left.astype(jnp.bfloat16), right.astype(jnp.bfloat16), (d...  44.6 us
    all_gather x1, waiting for transfers between devices, body(): lax.all_gather(jnp.concatenate([cross_panel, squares], axis=0), 'sub', ax...  41.9 us
    reduce_scatter x1, waiting for transfers between devices, body(): lax.psum_scatter(partial_t, 'sub', scatter_dimension=1, tiled=True)  38.6 us
    all_gather x1, blocking collectives, body(): table = lax.all_gather(codebook, 'sub', axis=1, tiled=True)  18.8 us
    all_to_all x1, blocking collectives, rows_sum(): lax.all_to_all(x, 'rows', split_axis=0, concat_axis=0, tiled=True)  15.1 us
    all_to_all x1, waiting for transfers between devices, body(): lax.all_to_all(rotated, 'sub', split_axis=1, concat_axis=0, tiled=True)  14.8 us
    all_to_all x1, blocking collectives, rows_sum(): lax.all_to_all(spread, 'rows', split_axis=0, concat_axis=0, tiled=True)  12.4 us
    all_to_all x1, blocking collectives, body(): lax.all_to_all(codes, 'sub', split_axis=0, concat_axis=1, tiled=True)  11.9 us
  transfers between devices with their start and end apart: 11, of which 6 were waited for; matrix products, arithmetic and copies ran while one was open for 13% of the time, Pallas kernels for 0%

profile of v5, /device:TPU:64, one launch (start us, length us, event | category | flops | bytes accessed | tf_op | source)
XLA Modules:
  0.0 283.2 jit_solution(14009535849916423926)
XLA Ops:
  7.2 18.8 %all_gather.6 = bf16[256,1024]{0,1:T(8,128)(2,1)S(1)} all-gather(bf16[256,64]{0,1:T(8,128)(2,1)} %param.5), channel_id=1, replica_groups=mesh['rows'=16,'sub'=16] {'sub'}, dimensions={1}, use_global_device_ids=true | all-gather | bytes 557056 | tf_op jit(solution)/shard_map/all_gather | solution.py:80
  26.0 5.3 %fusion.17 = bf16[64,256,16]{1,2,0:T(8,128)(2,1)S(1)} fusion(bf16[256,64,16]{0,2,1:T(8,128)(2,1)S(1)} %bitcast.98, s32[64,256]{1,0:T(8,128)} %param.4), kind=kOutput, calls=%fused_computation.35 | convolution fusion | flops 138674176 | bytes 1114112 | tf_op jit(solution)/shard_map/mnk,kmj->nmj/dot_general | solution.py:26
  31.3 2.7 fusion.86
  34.1 0.8 copy-done.5
  34.9 11.9 %all_to_all.68 = s32[16,4,256]{2,1,0:T(4,128)S(1)} all-to-all(s32[16,4,256]{2,1,0:T(4,128)S(1)} %all_to_all.48), channel_id=1, replica_groups=mesh['rows'=16,'sub'=16] {'sub'}, dimensions={0} | all-to-all | bytes 131072 | tf_op jit(solution)/shard_map/all_to_all | solution.py:79
  46.7 6.9 %convert_reduce_fusion = f32[4,256]{1,0:T(4,128)S(1)} fusion(s32[4,4096]{1,0:T(4,128)S(1)} %bitcast.101), kind=kLoop, calls=%fused_computation.1 | loop fusion | flops 16776192 | bytes 69632 | tf_op jit(solution)/shard_map/reduce_sum | solution.py:87
  53.6 38.6 %reduce-scatter.2.cloned.1.call-done = f32[1024,64]{0,1:T(8,128)} async-done(((f32[1024,1024]{0,1:T(8,128)}), f32[1024,64]{0,1:T(8,128)}) %reduce-scatter.2.cloned.1.call-update) | async-done | bytes 262160 | tf_op jit(solution)/shard_map/reduce_scatter | solution.py:85
  92.2 1.0 all_to_all.52
  93.2 15.1 %all_to_all.69 = f32[16,4,1024]{2,1,0:T(4,128)S(1)} all-to-all(f32[16,4,1024]{2,1,0:T(4,128)S(1)} %all_to_all.52), channel_id=1, replica_groups=mesh['rows'=16,'sub'=16] {'rows'}, dimensions={0} | all-to-all | bytes 524288 | tf_op jit(solution)/shard_map/all_to_all | solution.py:43
  108.4 12.4 %all_to_all.70 = f32[16,4,1024]{2,1,0:T(4,128)S(1)} all-to-all(f32[16,4,1024]{2,1,0:T(4,128)S(1)} %broadcast_in_dim.6), channel_id=1, replica_groups=mesh['rows'=16,'sub'=16] {'rows'}, dimensions={0} | all-to-all | bytes 524288 | tf_op jit(solution)/shard_map/all_to_all | solution.py:46
  121.0 0.7 multiply_reduce_fusion
  121.7 1.4 concatenate.11
  123.1 41.9 %all-gather.2.cloned.1.call-done = f32[1152,1024]{1,0:T(8,128)} async-done(((f32[72,1024]{1,0:T(8,128)}), f32[1152,1024]{1,0:T(8,128)}) %all-gather.2.cloned.1.call-update) | async-done | bytes 4718608 | tf_op jit(solution)/shard_map/all_gather | solution.py:92
  165.1 1.5 slice_reduce_fusion
  167.2 3.1 %dynamic-slice_bitcast_fusion = (f32[8,72,1024]{2,1,0:T(8,128)S(1)}, f32[8,72,1024]{2,1,0:T(8,128)S(1)}) fusion(f32[8,2,72,1024]{3,2,1,0:T(8,128)} %bitcast.86, s32[]{:T(128)S(6)} %select_n.36, s32[]{:T(128)S(6)} %select_n.35), kind=kLoop, calls=%fused_computation.9 | loop fusion | bytes 9437192 | tf_op jit(solution)/shard_map/jit(dynamic_index_in_dim)/squeeze | solution.py:98
  170.3 1.8 broadcast_multiply_fusion
  172.2 1.8 fusion.74
  174.2 0.8 fusion.88
  175.3 1.5 fusion.64
  176.7 1.5 fusion.87
  178.2 4.0 %fusion.24 = f32[512,1024]{1,0:T(8,128)} fusion(bf16[512,1024]{1,0:T(8,128)(2,1)S(1)} %bitcast.84, f32[512,512]{1,0:T(8,128)} %fusion.87, f32[512,512]{1,0:T(8,128)} %get-tuple-element.32, f32[512,512]{1,0:T(8,128)S(1)} %fusion.88), kind=kOutput, calls=%fused_computation.43 | convolution fusion | flops 806879232 | bytes 6291456 | tf_op jit(solution)/shard_map/dot_general | solution.py:50
  182.2 5.5 %fusion.75 = (bf16[512,1024]{1,0:T(8,128)(2,1)S(1)}, f32[512,1024]{1,0:T(8,128)}) fusion(bf16[512,1024]{1,0:T(8,128)(2,1)} %bitcast.89, f32[512,512]{1,0:T(8,128)} %fusion.64, bf16[512,512]{1,0:T(8,128)(2,1)} %collective-permute-done, f32[512,512]{1,0:T(8,128)S(1)} %fusion.88, f32[512,1024]{1,0:T(8,128)} %fusion.24, f32[8,64,1024]{2,1,0:T(8,128)} %get-tuple-element.29), kind=kOutput, calls=%fused_computation.97 | convolution fusion | flops 808452096 | bytes 11010048 | tf_op jit(solution)/shard_map/dot_general | solution.py:50
  187.9 1.8 fusion.78
  189.9 1.5 fusion.89
  191.3 0.7 fusion.90
  192.1 1.5 fusion.52
  193.5 4.0 %fusion.23 = f32[512,1024]{1,0:T(8,128)} fusion(bf16[512,1024]{1,0:T(8,128)(2,1)S(1)} %get-tuple-element.33, f32[512,512]{1,0:T(8,128)} %fusion.89, f32[512,512]{1,0:T(8,128)} %get-tuple-element.36, f32[512,512]{1,0:T(8,128)S(1)} %fusion.90), kind=kOutput, calls=%fused_computation.42 | convolution fusion | flops 806879232 | bytes 6291456 | tf_op jit(solution)/shard_map/dot_general | solution.py:50
  197.5 5.5 %fusion.79 = (bf16[512,1024]{1,0:T(8,128)(2,1)S(1)}, f32[512,1024]{1,0:T(8,128)}) fusion(bf16[512,1024]{1,0:T(8,128)(2,1)} %copy-done.2, f32[512,512]{1,0:T(8,128)S(1)} %fusion.90, f32[512,512]{1,0:T(8,128)} %fusion.52, bf16[512,512]{1,0:T(8,128)(2,1)} %collective-permute-done.2, f32[512,1024]{1,0:T(8,128)} %fusion.23, f32[512,1024]{1,0:T(8,128)} %get-tuple-element.34), kind=kOutput, calls=%fused_computation.99 | convolution fusion | flops 808976384 | bytes 11010048 | tf_op jit(solution)/shard_map/dot_general | solution.py:50
  203.3 1.7 fusion.82
  205.3 1.5 fusion.91
  206.8 0.7 fusion.92
  207.5 1.5 fusion.46
  209.0 4.0 %fusion.22 = f32[512,1024]{1,0:T(8,128)} fusion(bf16[512,1024]{1,0:T(8,128)(2,1)S(1)} %get-tuple-element.37, f32[512,512]{1,0:T(8,128)} %fusion.91, f32[512,512]{1,0:T(8,128)} %get-tuple-element.40, f32[512,512]{1,0:T(8,128)S(1)} %fusion.92), kind=kOutput, calls=%fused_computation.41 | convolution fusion | flops 806879232 | bytes 6291456 | tf_op jit(solution)/shard_map/dot_general | solution.py:50
  212.9 5.5 %fusion.83 = (bf16[512,1024]{1,0:T(8,128)(2,1)S(1)}, f32[512,1024]{1,0:T(8,128)}) fusion(bf16[512,1024]{1,0:T(8,128)(2,1)} %copy-done.3, f32[512,512]{1,0:T(8,128)S(1)} %fusion.92, f32[512,512]{1,0:T(8,128)} %fusion.46, bf16[512,512]{1,0:T(8,128)(2,1)} %collective-permute-done.4, f32[512,1024]{1,0:T(8,128)} %fusion.22, f32[512,1024]{1,0:T(8,128)} %get-tuple-element.38), kind=kOutput, calls=%fused_computation.101 | convolution fusion | flops 808976384 | bytes 11010048 | tf_op jit(solution)/shard_map/dot_general | solution.py:50
  218.7 2.4 collective-permute-done.5
  221.3 1.6 convolution_convert_fusion
  222.8 5.8 %all-to-all-start.3 = ((bf16[256,16,64]{0,2,1:T(8,128)(2,1)}), bf16[256,16,64]{0,2,1:T(8,128)(2,1)S(1)}, u32[]{:S(2)}, u32[]{:S(2)}) async-start(bf16[256,16,64]{0,2,1:T(8,128)(2,1)} %bitcast.25), calls=%async_computation.4 | async-start | bytes 1048576 | tf_op jit(solution)/shard_map/all_to_all | solution.py:115
  228.8 14.8 %all-to-all-done.3 = bf16[256,16,64]{0,2,1:T(8,128)(2,1)S(1)} async-done(((bf16[256,16,64]{0,2,1:T(8,128)(2,1)}), bf16[256,16,64]{0,2,1:T(8,128)(2,1)S(1)}, u32[]{:S(2)}, u32[]{:S(2)}) %all-to-all-start.3) | async-done | bytes 524320 | tf_op jit(solution)/shard_map/all_to_all | solution.py:115
  244.1 3.2 %fusion.25 = f32[256,4,16]{0,2,1:T(8,128)S(1)} fusion(bf16[4096,4,16]{0,2,1:T(8,128)(2,1)S(1)} %reshape.78, s32[4,4096]{1,0:T(4,128)S(1)} %bitcast.102), kind=kOutput, calls=%fused_computation.44 | convolution fusion | flops 138412032 | bytes 655360 | tf_op jit(solution)/shard_map/mnk,nmj->kmj/dot_general | solution.py:36
  247.8 0.8 pad_maximum_fusion
  248.5 6.8 %all-to-all-start.4 = ((f32[16,16,68]{2,1,0:T(8,128)}), f32[16,16,68]{2,1,0:T(8,128)S(1)}, u32[]{:S(2)}, u32[]{:S(2)}) async-start(f32[16,16,68]{2,1,0:T(8,128)} %pad_maximum_fusion), calls=%async_computation.5 | async-start | bytes 262144 | tf_op jit(solution)/shard_map/all_to_all | solution.py:43
  255.5 7.7 %all-to-all-done.4 = f32[16,16,68]{2,1,0:T(8,128)S(1)} async-done(((f32[16,16,68]{2,1,0:T(8,128)}), f32[16,16,68]{2,1,0:T(8,128)S(1)}, u32[]{:S(2)}, u32[]{:S(2)}) %all-to-all-start.4) | async-done | bytes 69664 | tf_op jit(solution)/shard_map/all_to_all | solution.py:43
  263.2 0.7 broadcast_in_dim.7
  263.9 3.6 %all-to-all-start.5 = ((f32[16,16,68]{2,1,0:T(8,128)}), f32[16,16,68]{2,1,0:T(8,128)S(1)}, u32[]{:S(2)}, u32[]{:S(2)}) async-start(f32[16,16,68]{2,1,0:T(8,128)} %broadcast_in_dim.7), calls=%async_computation.6 | async-start | bytes 262144 | tf_op jit(solution)/shard_map/all_to_all | solution.py:46
  267.5 1.7 dynamic-slice_bitcast_fusion.2
  269.2 2.0 copy.65
  271.2 4.1 %all-to-all-done.5 = f32[16,16,68]{2,1,0:T(8,128)S(1)} async-done(((f32[16,16,68]{2,1,0:T(8,128)}), f32[16,16,68]{2,1,0:T(8,128)S(1)}, u32[]{:S(2)}, u32[]{:S(2)}) %all-to-all-start.5) | async-done | bytes 69664 | tf_op jit(solution)/shard_map/all_to_all | solution.py:46
  275.7 0.7 copy.66
  (45 shorter events, 4.0 us)
Async XLA Ops:
  7.2 24.1 %copy-start = (bf16[256,1024]{1,0:T(8,128)(2,1)S(1)}, bf16[256,1024]{1,0:T(8,128)(2,1)}, u32[]{:S(2)}) copy-start(bf16[256,1024]{1,0:T(8,128)(2,1)} %param.3) | copy-start | bytes 1572868
  7.2 85.0 %reduce-scatter.2.cloned.1.call-start = ((), (), s32[]{:S(2)}) async-start(), calls=%async_computation.7 | async-start | bytes 4456448 | tf_op jit(solution)/shard_map/reduce_scatter | solution.py:85
  34.0 0.8 copy-start.5
  34.0 131.0 %all-gather.2.cloned.1.call-start = ((), (), s32[]{:S(2)}) async-start(), calls=%async_computation.8 | async-start | bytes 5013504 | tf_op jit(solution)/shard_map/all_gather | solution.py:92
  174.2 2.6 copy-start.1
  174.9 7.2 %collective-permute-start = (bf16[512,512]{1,0:T(8,128)(2,1)S(1)}, bf16[512,512]{1,0:T(8,128)(2,1)}, u32[]{:S(2)}, u32[]{:S(2)}) collective-permute-start(bf16[512,512]{1,0:T(8,128)(2,1)S(1)} %get-tuple-element.31), channel_id=1, source_target_pairs={{0,1},{1,0},{2,3},{3,2},{4,5},{5,4},{6,7},{7,6},{8,9},{9,8},{10,11... | collective-permute-start | bytes 1572872 | tf_op jit(solution)/shard_map/ppermute | solution.py:58
  187.6 3.7 %collective-permute-start.1 = (bf16[512,1024]{1,0:T(8,128)(2,1)S(1)}, bf16[512,1024]{1,0:T(8,128)(2,1)S(1)}, u32[]{:S(2)}, u32[]{:S(2)}) collective-permute-start(bf16[512,1024]{1,0:T(8,128)(2,1)S(1)} %get-tuple-element.33), channel_id=1, source_target_pairs={{0,1},{1,0},{2,3},{3,2},{4,5},{5,4},{6,7},{7,6},{8,9},{9,8},{10,11... | collective-permute-start | bytes 3145736 | tf_op jit(solution)/shard_map/ppermute | solution.py:58
  189.7 7.9 %collective-permute-start.2 = (bf16[512,512]{1,0:T(8,128)(2,1)S(1)}, bf16[512,512]{1,0:T(8,128)(2,1)}, u32[]{:S(2)}, u32[]{:S(2)}) collective-permute-start(bf16[512,512]{1,0:T(8,128)(2,1)S(1)} %get-tuple-element.35), channel_id=1, source_target_pairs={{0,1},{1,0},{2,3},{3,2},{4,5},{5,4},{6,7},{7,6},{8,9},{9,8},{10,11... | collective-permute-start | bytes 1572872 | tf_op jit(solution)/shard_map/ppermute | solution.py:58
  191.3 2.2 copy-start.2
  203.0 3.7 %collective-permute-start.3 = (bf16[512,1024]{1,0:T(8,128)(2,1)S(1)}, bf16[512,1024]{1,0:T(8,128)(2,1)S(1)}, u32[]{:S(2)}, u32[]{:S(2)}) collective-permute-start(bf16[512,1024]{1,0:T(8,128)(2,1)S(1)} %get-tuple-element.37), channel_id=1, source_target_pairs={{0,1},{1,0},{2,3},{3,2},{4,5},{5,4},{6,7},{7,6},{8,9},{9,8},{10,11... | collective-permute-start | bytes 3145736 | tf_op jit(solution)/shard_map/ppermute | solution.py:58
  205.1 7.9 %collective-permute-start.4 = (bf16[512,512]{1,0:T(8,128)(2,1)S(1)}, bf16[512,512]{1,0:T(8,128)(2,1)}, u32[]{:S(2)}, u32[]{:S(2)}) collective-permute-start(bf16[512,512]{1,0:T(8,128)(2,1)S(1)} %get-tuple-element.39), channel_id=1, source_target_pairs={{0,1},{1,0},{2,3},{3,2},{4,5},{5,4},{6,7},{7,6},{8,9},{9,8},{10,11... | collective-permute-start | bytes 1572872 | tf_op jit(solution)/shard_map/ppermute | solution.py:58
  206.8 2.2 copy-start.3
  218.4 2.7 collective-permute-start.5
  222.8 20.7 %all-to-all-start.3 = ((bf16[256,16,64]{0,2,1:T(8,128)(2,1)}), bf16[256,16,64]{0,2,1:T(8,128)(2,1)S(1)}, u32[]{:S(2)}, u32[]{:S(2)}) async-start(bf16[256,16,64]{0,2,1:T(8,128)(2,1)} %bitcast.25), calls=%async_computation.4 | async-start | bytes 1048576 | tf_op jit(solution)/shard_map/all_to_all | solution.py:115
  244.1 11.3 %copy-start.4 = (bf16[256,64]{0,1:T(8,128)(2,1)S(1)}, bf16[256,64]{0,1:T(8,128)(2,1)}, u32[]{:S(2)}) copy-start(bf16[256,64]{0,1:T(8,128)(2,1)} %param.5) | copy-start | bytes 98308
  248.5 14.7 %all-to-all-start.4 = ((f32[16,16,68]{2,1,0:T(8,128)}), f32[16,16,68]{2,1,0:T(8,128)S(1)}, u32[]{:S(2)}, u32[]{:S(2)}) async-start(f32[16,16,68]{2,1,0:T(8,128)} %pad_maximum_fusion), calls=%async_computation.5 | async-start | bytes 262144 | tf_op jit(solution)/shard_map/all_to_all | solution.py:43
  263.9 11.4 %all-to-all-start.5 = ((f32[16,16,68]{2,1,0:T(8,128)}), f32[16,16,68]{2,1,0:T(8,128)S(1)}, u32[]{:S(2)}, u32[]{:S(2)}) async-start(f32[16,16,68]{2,1,0:T(8,128)} %broadcast_in_dim.7), calls=%async_computation.6 | async-start | bytes 262144 | tf_op jit(solution)/shard_map/all_to_all | solution.py:46
Sparse Core Ops, SparseCore 0:
  34.1 58.0 reduce-scatter.1
  123.2 41.7 all-gather.1

commit v6 on v4

--- a/solution.py
+++ b/solution.py
@@ -64,15 +64,14 @@
     gram_cross = bdot(own_half, z_other_half, ((1,), (1,)))
     gram_other = partner(gram_own.astype(jnp.bfloat16))
     own_block, cross_block = gram_own.astype(jnp.bfloat16), gram_cross.astype(jnp.bfloat16)
-    quartic_left = bdot(own_block, own_block, ((1,), (0,))) + bdot(cross_block, cross_block, ((1,), (1,)))
+    gram_rows = jnp.concatenate([own_block, cross_block], axis=1)
+    quartic_left = bdot(gram_rows, gram_rows, ((1,), (1,)))
     quartic_right = bdot(own_block, cross_block, ((1,), (0,))) + bdot(cross_block, gram_other, ((1,), (0,)))
-    mixer_left = coef_b * gram_own + coef_c * quartic_left
-    mixer_right = coef_b * gram_cross + coef_c * quartic_right
-    return (
-        coef_a * z_own
-        + bdot(mixer_left, own_half, ((1,), (0,)))
-        + bdot(mixer_right, z_other_half, ((1,), (0,)))
+    mixer = jnp.concatenate(
+        [coef_b * gram_own + coef_c * quartic_left, coef_b * gram_cross + coef_c * quartic_right], axis=1
     )
+    local_rows = jnp.concatenate([own_half, z_other_half], axis=0)
+    return coef_a * z_own + bdot(mixer, local_rows, ((1,), (0,)))
 
 
 def body(embeddings, codes, codebook):

time: 286 us -> 258 us (0.902)
  matrix products: 57.4 us -> 27.5 us
  waiting for transfers between devices: 109 us -> 112 us
    dot_general x18, matrix products: 44.6 us -> 14.7 us  [bdot(): lax.dot_general(left.astype(jnp.bfloat16), right.astype(jnp.bfloat16), (d...]
    ppermute x6, waiting for transfers between devices: 2.37 us -> 5.37 us  [partner(): return lax.ppermute(x, 'sub', [(i, i ^ 1) for i in range(count)])]
  transfers between devices with their start and end apart: 11 -> 11, of which waited for: 6 -> 9; matrix products, arithmetic and copies ran while one was open for 14% -> 7% of each run, Pallas kernels for 0% -> 0%
where the time goes in v6:
time: 258 us; the launch traced here: 255 us
  waiting for transfers between devices  112 us (43%)
  blocking collectives  58.2 us (23%)
  matrix products  27.5 us (11%)
  starting transfers between devices  18.6 us (7%)
  between operations  15.1 us (6%)
  other arithmetic  14.8 us (6%)
  local copies, waits for them, and re-layouts  9.55 us (4%)
    all_gather x1, waiting for transfers between devices, body(): cross = lax.all_gather(cross_panel, 'sub', axis=0, tiled=True)  41.1 us
    reduce_scatter x1, waiting for transfers between devices, body(): lax.psum_scatter(partial_t, 'sub', scatter_dimension=1, tiled=True)  38.6 us
    all_gather x1, blocking collectives, body(): table = lax.all_gather(codebook, 'sub', axis=1, tiled=True)  18.8 us
    all_to_all x1, blocking collectives, rows_sum(): lax.all_to_all(x, 'rows', split_axis=0, concat_axis=0, tiled=True)  15.1 us
    all_to_all x1, waiting for transfers between devices, body(): lax.all_to_all(rotated, 'sub', split_axis=1, concat_axis=0, tiled=True)  14.8 us
    dot_general x18, matrix products, bdot(): lax.dot_general(left.astype(jnp.bfloat16), right.astype(jnp.bfloat16), (d...  14.7 us
    all_to_all x1, blocking collectives, rows_sum(): lax.all_to_all(spread, 'rows', split_axis=0, concat_axis=0, tiled=True)  12.4 us
    all_to_all x1, blocking collectives, body(): lax.all_to_all(codes, 'sub', split_axis=0, concat_axis=1, tiled=True)  11.9 us
  transfers between devices with their start and end apart: 11, of which 9 were waited for; matrix products, arithmetic and copies ran while one was open for 7% of the time, Pallas kernels for 0%

profile of v6, /device:TPU:64, one launch (start us, length us, event | category | flops | bytes accessed | tf_op | source)
XLA Modules:
  0.0 255.4 jit_solution(3494341977541362424)
XLA Ops:
  7.2 18.8 %all_gather.6 = bf16[256,1024]{0,1:T(8,128)(2,1)S(1)} all-gather(bf16[256,64]{0,1:T(8,128)(2,1)} %param.5), channel_id=1, replica_groups=mesh['rows'=16,'sub'=16] {'sub'}, dimensions={1}, use_global_device_ids=true | all-gather | bytes 557056 | tf_op jit(solution)/shard_map/all_gather | solution.py:79
  26.0 5.3 %fusion.28 = bf16[64,256,16]{1,2,0:T(8,128)(2,1)S(1)} fusion(bf16[256,64,16]{0,2,1:T(8,128)(2,1)S(1)} %bitcast.85, s32[64,256]{1,0:T(8,128)} %param.4), kind=kOutput, calls=%fused_computation.43 | convolution fusion | flops 138674176 | bytes 1114112 | tf_op jit(solution)/shard_map/mnk,kmj->nmj/dot_general | solution.py:26
  31.3 2.7 %fusion.72 = f32[1024,1024]{0,1:T(8,128)} fusion(bf16[256,1024]{0,1:T(8,128)(2,1)S(1)} %bitcast.80, bf16[256,1024]{1,0:T(8,128)(2,1)S(1)} %copy-done), kind=kOutput, calls=%fused_computation.90 | convolution fusion | flops 536870912 | bytes 5242880 | tf_op jit(solution)/shard_map/dot_general | solution.py:81
  34.1 0.8 copy-done.2
  34.9 11.9 %all_to_all.68 = s32[16,4,256]{2,1,0:T(4,128)S(1)} all-to-all(s32[16,4,256]{2,1,0:T(4,128)S(1)} %all_to_all.48), channel_id=1, replica_groups=mesh['rows'=16,'sub'=16] {'sub'}, dimensions={0} | all-to-all | bytes 131072 | tf_op jit(solution)/shard_map/all_to_all | solution.py:78
  46.7 6.9 %convert_reduce_fusion = f32[4,256]{1,0:T(4,128)S(1)} fusion(s32[4,4096]{1,0:T(4,128)S(1)} %bitcast.88), kind=kLoop, calls=%fused_computation.1 | loop fusion | flops 16776192 | bytes 69632 | tf_op jit(solution)/shard_map/reduce_sum | solution.py:86
  53.6 38.6 %reduce-scatter.2.cloned.1.call-done = f32[1024,64]{0,1:T(8,128)} async-done(((f32[1024,1024]{0,1:T(8,128)}), f32[1024,64]{0,1:T(8,128)}) %reduce-scatter.2.cloned.1.call-update) | async-done | bytes 262160 | tf_op jit(solution)/shard_map/reduce_scatter | solution.py:84
  92.2 1.0 all_to_all.52
  93.3 15.1 %all_to_all.69 = f32[16,4,1024]{2,1,0:T(4,128)S(1)} all-to-all(f32[16,4,1024]{2,1,0:T(4,128)S(1)} %all_to_all.52), channel_id=1, replica_groups=mesh['rows'=16,'sub'=16] {'rows'}, dimensions={0} | all-to-all | bytes 524288 | tf_op jit(solution)/shard_map/all_to_all | solution.py:43
  108.5 12.4 %all_to_all.70 = f32[16,4,1024]{2,1,0:T(4,128)S(1)} all-to-all(f32[16,4,1024]{2,1,0:T(4,128)S(1)} %broadcast_in_dim.6), channel_id=1, replica_groups=mesh['rows'=16,'sub'=16] {'rows'}, dimensions={0} | all-to-all | bytes 524288 | tf_op jit(solution)/shard_map/all_to_all | solution.py:46
  120.9 0.8 all_to_all.55
  121.7 41.1 %all-gather.2.cloned.1.call-done = f32[1024,1024]{1,0:T(8,128)} async-done(((f32[64,1024]{1,0:T(8,128)}), f32[1024,1024]{1,0:T(8,128)}) %all-gather.2.cloned.1.call-update) | async-done | bytes 4194320 | tf_op jit(solution)/shard_map/all_gather | solution.py:89
  162.9 3.9 %multiply_reduce_fusion = f32[]{:T(128)} fusion(f32[1024,1024]{1,0:T(8,128)} %all-gather.2.cloned.1.call-done), kind=kLoop, calls=%fused_computation.9 | loop fusion | flops 2097151 | bytes 4194308 | tf_op jit(solution)/shard_map/reduce_sum | solution.py:90
  167.4 2.6 %broadcast_divide_fusion = f32[1024,1024]{1,0:T(8,128)S(1)} fusion(f32[1024,1024]{1,0:T(8,128)} %all-gather.2.cloned.1.call-done, f32[]{:T(128)S(6)} %add.71), kind=kLoop, calls=%fused_computation.27 | loop fusion | flops 1048576 | bytes 8388612 | tf_op jit(solution)/shard_map/div | solution.py:91
  170.8 0.7 fusion.64
  171.5 0.7 fusion.63
  172.6 0.8 fusion.29
  173.8 0.5 collective-permute-done
  174.3 0.5 fusion.32
  174.8 1.3 fusion.65
  176.4 0.7 fusion.67
  177.1 0.6 collective-permute-start.2
  177.7 1.1 collective-permute-done.1
  178.8 0.7 fusion.66
  179.6 0.8 fusion.30
  180.3 0.4 fusion.74
  180.8 0.5 add_convert_fusion.1
  181.3 1.3 fusion.68
  182.9 0.7 fusion.70
  184.0 1.3 collective-permute-done.3
  185.3 0.7 fusion.69
  186.1 0.8 fusion.31
  187.3 0.5 add_convert_fusion
  187.8 2.6 %fusion.71 = (bf16[512,1024]{1,0:T(8,128)(2,1)S(1)}, f32[512,1024]{1,0:T(8,128)}) fusion(bf16[512,1024]{1,0:T(8,128)(2,1)S(1)} %collective-permute-done.3, bf16[512,1024]{1,0:T(8,128)(2,1)S(1)} %get-tuple-element.39, bf16[512,512]{0,1:T(8,128)(2,1)S(1)} %add_convert_fusion, bf16[512,512]{0,1:T(8,128)(2,1)S(1)} %fusion.31, f32[512,1024]{1,0:T(8,128)S(1)} %get-tuple-element.40), kind=kOutput, calls=%fused_computation.89 | convolution fusion | flops 1081606144 | bytes 8388608 | tf_op jit(solution)/shard_map/dot_general | solution.py:50
  190.6 2.4 collective-permute-done.5
  193.3 1.6 convolution_convert_fusion
  194.9 6.0 %all-to-all-start.3 = ((bf16[256,16,64]{0,2,1:T(8,128)(2,1)}), bf16[256,16,64]{0,2,1:T(8,128)(2,1)S(1)}, u32[]{:S(2)}, u32[]{:S(2)}) async-start(bf16[256,16,64]{0,2,1:T(8,128)(2,1)} %bitcast.22), calls=%async_computation.4 | async-start | bytes 1048576 | tf_op jit(solution)/shard_map/all_to_all | solution.py:111
  201.0 14.8 %all-to-all-done.3 = bf16[256,16,64]{0,2,1:T(8,128)(2,1)S(1)} async-done(((bf16[256,16,64]{0,2,1:T(8,128)(2,1)}), bf16[256,16,64]{0,2,1:T(8,128)(2,1)S(1)}, u32[]{:S(2)}, u32[]{:S(2)}) %all-to-all-start.3) | async-done | bytes 524320 | tf_op jit(solution)/shard_map/all_to_all | solution.py:111
  216.3 3.2 %fusion.33 = f32[256,4,16]{0,2,1:T(8,128)S(1)} fusion(bf16[4096,4,16]{0,2,1:T(8,128)(2,1)S(1)} %reshape.76, s32[4,4096]{1,0:T(4,128)S(1)} %bitcast.89), kind=kOutput, calls=%fused_computation.49 | convolution fusion | flops 138412032 | bytes 655360 | tf_op jit(solution)/shard_map/mnk,nmj->kmj/dot_general | solution.py:36
  220.0 0.8 pad_maximum_fusion
  220.8 6.8 %all-to-all-start.4 = ((f32[16,16,68]{2,1,0:T(8,128)}), f32[16,16,68]{2,1,0:T(8,128)S(1)}, u32[]{:S(2)}, u32[]{:S(2)}) async-start(f32[16,16,68]{2,1,0:T(8,128)} %pad_maximum_fusion), calls=%async_computation.5 | async-start | bytes 262144 | tf_op jit(solution)/shard_map/all_to_all | solution.py:43
  227.7 7.7 %all-to-all-done.4 = f32[16,16,68]{2,1,0:T(8,128)S(1)} async-done(((f32[16,16,68]{2,1,0:T(8,128)}), f32[16,16,68]{2,1,0:T(8,128)S(1)}, u32[]{:S(2)}, u32[]{:S(2)}) %all-to-all-start.4) | async-done | bytes 69664 | tf_op jit(solution)/shard_map/all_to_all | solution.py:43
  235.4 0.7 broadcast_in_dim.7
  236.1 3.6 %all-to-all-start.5 = ((f32[16,16,68]{2,1,0:T(8,128)}), f32[16,16,68]{2,1,0:T(8,128)S(1)}, u32[]{:S(2)}, u32[]{:S(2)}) async-start(f32[16,16,68]{2,1,0:T(8,128)} %broadcast_in_dim.7), calls=%async_computation.6 | async-start | bytes 262144 | tf_op jit(solution)/shard_map/all_to_all | solution.py:46
  239.7 1.7 dynamic-slice_bitcast_fusion
  241.4 2.0 copy.65
  243.4 4.1 %all-to-all-done.5 = f32[16,16,68]{2,1,0:T(8,128)S(1)} async-done(((f32[16,16,68]{2,1,0:T(8,128)}), f32[16,16,68]{2,1,0:T(8,128)S(1)}, u32[]{:S(2)}, u32[]{:S(2)}) %all-to-all-start.5) | async-done | bytes 69664 | tf_op jit(solution)/shard_map/all_to_all | solution.py:46
  247.9 0.7 copy.66
  (37 shorter events, 5.1 us)
Async XLA Ops:
  7.2 24.1 %copy-start = (bf16[256,1024]{1,0:T(8,128)(2,1)S(1)}, bf16[256,1024]{1,0:T(8,128)(2,1)}, u32[]{:S(2)}) copy-start(bf16[256,1024]{1,0:T(8,128)(2,1)} %param.3) | copy-start | bytes 1572868
  7.2 85.1 %reduce-scatter.2.cloned.1.call-start = ((), (), s32[]{:S(2)}) async-start(), calls=%async_computation.7 | async-start | bytes 4456448 | tf_op jit(solution)/shard_map/reduce_scatter | solution.py:84
  34.0 0.8 copy-start.2
  34.0 128.8 %all-gather.2.cloned.1.call-start = ((), (), s32[]{:S(2)}) async-start(), calls=%async_computation.8 | async-start | bytes 4456448 | tf_op jit(solution)/shard_map/all_gather | solution.py:89
  172.3 2.0 collective-permute-start
  176.1 2.7 %collective-permute-start.1 = (bf16[512,1024]{1,0:T(8,128)(2,1)S(1)}, bf16[512,1024]{1,0:T(8,128)(2,1)S(1)}, u32[]{:S(2)}, u32[]{:S(2)}) collective-permute-start(bf16[512,1024]{1,0:T(8,128)(2,1)S(1)} %get-tuple-element.33), channel_id=1, source_target_pairs={{0,1},{1,0},{2,3},{3,2},{4,5},{5,4},{6,7},{7,6},{8,9},{9,8},{10,11... | collective-permute-start | bytes 3145736 | tf_op jit(solution)/shard_map/ppermute | solution.py:58
  177.1 3.6 %collective-permute-start.2 = (bf16[512,512]{0,1:T(8,128)(2,1)S(1)}, bf16[512,512]{0,1:T(8,128)(2,1)S(1)}, u32[]{:S(2)}, u32[]{:S(2)}) collective-permute-start(bf16[512,512]{0,1:T(8,128)(2,1)S(1)} %get-tuple-element.37), channel_id=1, source_target_pairs={{0,1},{1,0},{2,3},{3,2},{4,5},{5,4},{6,7},{7,6},{8,9},{9,8},{10,11... | collective-permute-start | bytes 1572872 | tf_op jit(solution)/shard_map/ppermute | solution.py:58
  182.6 2.7 %collective-permute-start.3 = (bf16[512,1024]{1,0:T(8,128)(2,1)S(1)}, bf16[512,1024]{1,0:T(8,128)(2,1)S(1)}, u32[]{:S(2)}, u32[]{:S(2)}) collective-permute-start(bf16[512,1024]{1,0:T(8,128)(2,1)S(1)} %get-tuple-element.39), channel_id=1, source_target_pairs={{0,1},{1,0},{2,3},{3,2},{4,5},{5,4},{6,7},{7,6},{8,9},{9,8},{10,11... | collective-permute-start | bytes 3145736 | tf_op jit(solution)/shard_map/ppermute | solution.py:58
  183.6 3.6 %collective-permute-start.4 = (bf16[512,512]{0,1:T(8,128)(2,1)S(1)}, bf16[512,512]{0,1:T(8,128)(2,1)S(1)}, u32[]{:S(2)}, u32[]{:S(2)}) collective-permute-start(bf16[512,512]{0,1:T(8,128)(2,1)S(1)} %get-tuple-element.43), channel_id=1, source_target_pairs={{0,1},{1,0},{2,3},{3,2},{4,5},{5,4},{6,7},{7,6},{8,9},{9,8},{10,11... | collective-permute-start | bytes 1572872 | tf_op jit(solution)/shard_map/ppermute | solution.py:58
  190.4 2.7 %collective-permute-start.5 = (bf16[512,1024]{1,0:T(8,128)(2,1)S(1)}, bf16[512,1024]{1,0:T(8,128)(2,1)S(1)}, u32[]{:S(2)}, u32[]{:S(2)}) collective-permute-start(bf16[512,1024]{1,0:T(8,128)(2,1)S(1)} %get-tuple-element.45), channel_id=1, source_target_pairs={{0,1},{1,0},{2,3},{3,2},{4,5},{5,4},{6,7},{7,6},{8,9},{9,8},{10,11... | collective-permute-start | bytes 3145736 | tf_op jit(solution)/shard_map/ppermute | solution.py:58
  194.9 20.9 %all-to-all-start.3 = ((bf16[256,16,64]{0,2,1:T(8,128)(2,1)}), bf16[256,16,64]{0,2,1:T(8,128)(2,1)S(1)}, u32[]{:S(2)}, u32[]{:S(2)}) async-start(bf16[256,16,64]{0,2,1:T(8,128)(2,1)} %bitcast.22), calls=%async_computation.4 | async-start | bytes 1048576 | tf_op jit(solution)/shard_map/all_to_all | solution.py:111
  216.3 11.3 %copy-start.1 = (bf16[256,64]{0,1:T(8,128)(2,1)S(1)}, bf16[256,64]{0,1:T(8,128)(2,1)}, u32[]{:S(2)}) copy-start(bf16[256,64]{0,1:T(8,128)(2,1)} %param.5) | copy-start | bytes 98308
  220.8 14.7 %all-to-all-start.4 = ((f32[16,16,68]{2,1,0:T(8,128)}), f32[16,16,68]{2,1,0:T(8,128)S(1)}, u32[]{:S(2)}, u32[]{:S(2)}) async-start(f32[16,16,68]{2,1,0:T(8,128)} %pad_maximum_fusion), calls=%async_computation.5 | async-start | bytes 262144 | tf_op jit(solution)/shard_map/all_to_all | solution.py:43
  236.1 11.4 %all-to-all-start.5 = ((f32[16,16,68]{2,1,0:T(8,128)}), f32[16,16,68]{2,1,0:T(8,128)S(1)}, u32[]{:S(2)}, u32[]{:S(2)}) async-start(f32[16,16,68]{2,1,0:T(8,128)} %broadcast_in_dim.7), calls=%async_computation.6 | async-start | bytes 262144 | tf_op jit(solution)/shard_map/all_to_all | solution.py:46
Sparse Core Ops, SparseCore 0:
  34.2 58.0 reduce-scatter.1
  121.8 41.0 all-gather.1

commit v7 on v6

--- a/solution.py
+++ b/solution.py
@@ -87,24 +87,25 @@
     partial_panel, moved_codes, counts = lax.optimization_barrier((partial_panel, moved_codes, counts))
     cross_panel = rows_sum(partial_panel)
     cross = lax.all_gather(cross_panel, "sub", axis=0, tiled=True)
-    frob_scale = jnp.sqrt(jnp.sum(cross * cross)) + frob_eps
-    z = cross / frob_scale
+    width = cross.shape[1]
+    square_rows = jnp.sum((cross * cross).reshape(-1, 8, width), axis=1)
+    frob_scale = jnp.sqrt(jnp.sum(lax.optimization_barrier(square_rows))) + frob_eps
     core = lax.axis_index("sub") % 2
-    panel_rows = z.shape[0] // lax.axis_size("sub")
-    by_parity = z.reshape(-1, 2, panel_rows, z.shape[1])
-    z_own = lax.dynamic_index_in_dim(by_parity, core, axis=1, keepdims=False).reshape(-1, z.shape[1])
-    z_other = lax.dynamic_index_in_dim(by_parity, 1 - core, axis=1, keepdims=False).reshape(-1, z.shape[1])
+    panel_rows = cross.shape[0] // lax.axis_size("sub")
+    by_parity = cross.reshape(-1, 2, panel_rows, width)
+    z_own = lax.dynamic_index_in_dim(by_parity, core, axis=1, keepdims=False).reshape(-1, width) / frob_scale
+    z_other = lax.dynamic_index_in_dim(by_parity, 1 - core, axis=1, keepdims=False).reshape(-1, width) / frob_scale
     z_other_half = z_other.astype(jnp.bfloat16)
     for newton_step_index in range(NS_STEPS):
         z_own = newton_half(z_own, z_other_half)
         z_other_half = partner(z_own.astype(jnp.bfloat16))
-    own_panels = z_own.astype(jnp.bfloat16).reshape(-1, panel_rows, z.shape[1])
-    other_panels = z_other_half.reshape(-1, panel_rows, z.shape[1])
+    own_panels = z_own.astype(jnp.bfloat16).reshape(-1, panel_rows, width)
+    other_panels = z_other_half.reshape(-1, panel_rows, width)
     rotation_half = jnp.where(
         core == 0,
         jnp.stack([own_panels, other_panels], axis=1),
         jnp.stack([other_panels, own_panels], axis=1),
-    ).reshape(z.shape)
+    ).reshape(-1, width)
     rotated = jnp.dot(embeddings, rotation_half, preferred_element_type=jnp.float32).astype(
         jnp.bfloat16
     )
@@ -117,7 +118,7 @@
     spread = jnp.repeat(counts, own_codebook.shape[1] // counts.shape[1], axis=1)
     new_codebook = (code_sums + own_codebook) / (spread + 1.0)
     me = lax.axis_index("sub")
-    panel = lax.dynamic_index_in_dim(z_own.reshape(-1, panel_rows, z.shape[1]), me // 2, axis=0, keepdims=False)
+    panel = lax.dynamic_index_in_dim(z_own.reshape(-1, panel_rows, width), me // 2, axis=0, keepdims=False)
     return (panel, rotated, new_codebook)
 
 

time: 258 us -> 258 us (level)
    convert_element_type x0 -> x1, other arithmetic: none -> 2.85 us  [newton_half(): own_half = z_own.astype(jnp.bfloat16)]
    div x1 -> x0, other arithmetic: 2.62 us -> none  [body(): z = cross / frob_scale]
where the time goes in v7:
time: 258 us; the launch traced here: 255 us
  waiting for transfers between devices  112 us (43%)
  blocking collectives  58.2 us (23%)
  matrix products  27.5 us (11%)
  starting transfers between devices  18.6 us (7%)
  other arithmetic  15.1 us (6%)
  between operations  15.1 us (6%)
  local copies, waits for them, and re-layouts  9.24 us (4%)
    all_gather x1, waiting for transfers between devices, body(): cross = lax.all_gather(cross_panel, 'sub', axis=0, tiled=True)  41.1 us
    reduce_scatter x1, waiting for transfers between devices, body(): lax.psum_scatter(partial_t, 'sub', scatter_dimension=1, tiled=True)  38.6 us
    all_gather x1, blocking collectives, body(): table = lax.all_gather(codebook, 'sub', axis=1, tiled=True)  18.8 us
    all_to_all x1, blocking collectives, rows_sum(): lax.all_to_all(x, 'rows', split_axis=0, concat_axis=0, tiled=True)  15.1 us
    all_to_all x1, waiting for transfers between devices, body(): lax.all_to_all(rotated, 'sub', split_axis=1, concat_axis=0, tiled=True)  14.8 us
    dot_general x18, matrix products, bdot(): lax.dot_general(left.astype(jnp.bfloat16), right.astype(jnp.bfloat16), (d...  14.7 us
    all_to_all x1, blocking collectives, rows_sum(): lax.all_to_all(spread, 'rows', split_axis=0, concat_axis=0, tiled=True)  12.4 us
    all_to_all x1, blocking collectives, body(): lax.all_to_all(codes, 'sub', split_axis=0, concat_axis=1, tiled=True)  11.9 us
  transfers between devices with their start and end apart: 11, of which 9 were waited for; matrix products, arithmetic and copies ran while one was open for 7% of the time, Pallas kernels for 0%

profile of v7, /device:TPU:64, one launch (start us, length us, event | category | flops | bytes accessed | tf_op | source)
XLA Modules:
  0.0 255.3 jit_solution(3129097919419118259)
XLA Ops:
  7.2 18.8 %all_gather.6 = bf16[256,1024]{0,1:T(8,128)(2,1)S(1)} all-gather(bf16[256,64]{0,1:T(8,128)(2,1)} %param.5), channel_id=1, replica_groups=mesh['rows'=16,'sub'=16] {'sub'}, dimensions={1}, use_global_device_ids=true | all-gather | bytes 557056 | tf_op jit(solution)/shard_map/all_gather | solution.py:79
  26.0 5.3 %fusion.28 = bf16[64,256,16]{1,2,0:T(8,128)(2,1)S(1)} fusion(bf16[256,64,16]{0,2,1:T(8,128)(2,1)S(1)} %bitcast.86, s32[64,256]{1,0:T(8,128)} %param.4), kind=kOutput, calls=%fused_computation.41 | convolution fusion | flops 138674176 | bytes 1114112 | tf_op jit(solution)/shard_map/mnk,kmj->nmj/dot_general | solution.py:26
  31.3 2.7 %fusion.73 = f32[1024,1024]{0,1:T(8,128)} fusion(bf16[256,1024]{0,1:T(8,128)(2,1)S(1)} %bitcast.81, bf16[256,1024]{1,0:T(8,128)(2,1)S(1)} %copy-done), kind=kOutput, calls=%fused_computation.90 | convolution fusion | flops 536870912 | bytes 5242880 | tf_op jit(solution)/shard_map/dot_general | solution.py:81
  34.1 0.8 copy-done.2
  34.8 11.9 %all_to_all.68 = s32[16,4,256]{2,1,0:T(4,128)S(1)} all-to-all(s32[16,4,256]{2,1,0:T(4,128)S(1)} %all_to_all.48), channel_id=1, replica_groups=mesh['rows'=16,'sub'=16] {'sub'}, dimensions={0} | all-to-all | bytes 131072 | tf_op jit(solution)/shard_map/all_to_all | solution.py:78
  46.7 6.9 %convert_reduce_fusion = f32[4,256]{1,0:T(4,128)S(1)} fusion(s32[4,4096]{1,0:T(4,128)S(1)} %bitcast.89), kind=kLoop, calls=%fused_computation.1 | loop fusion | flops 16776192 | bytes 69632 | tf_op jit(solution)/shard_map/reduce_sum | solution.py:86
  53.6 38.6 %reduce-scatter.2.cloned.1.call-done = f32[1024,64]{0,1:T(8,128)} async-done(((f32[1024,1024]{0,1:T(8,128)}), f32[1024,64]{0,1:T(8,128)}) %reduce-scatter.2.cloned.1.call-update) | async-done | bytes 262160 | tf_op jit(solution)/shard_map/reduce_scatter | solution.py:84
  92.2 1.0 all_to_all.52
  93.2 15.1 %all_to_all.69 = f32[16,4,1024]{2,1,0:T(4,128)S(1)} all-to-all(f32[16,4,1024]{2,1,0:T(4,128)S(1)} %all_to_all.52), channel_id=1, replica_groups=mesh['rows'=16,'sub'=16] {'rows'}, dimensions={0} | all-to-all | bytes 524288 | tf_op jit(solution)/shard_map/all_to_all | solution.py:43
  108.4 12.4 %all_to_all.70 = f32[16,4,1024]{2,1,0:T(4,128)S(1)} all-to-all(f32[16,4,1024]{2,1,0:T(4,128)S(1)} %broadcast_in_dim.6), channel_id=1, replica_groups=mesh['rows'=16,'sub'=16] {'rows'}, dimensions={0} | all-to-all | bytes 524288 | tf_op jit(solution)/shard_map/all_to_all | solution.py:46
  120.9 0.8 all_to_all.55
  121.7 41.1 %all-gather.2.cloned.1.call-done = f32[1024,1024]{1,0:T(8,128)} async-done(((f32[64,1024]{1,0:T(8,128)}), f32[1024,1024]{1,0:T(8,128)}) %all-gather.2.cloned.1.call-update) | async-done | bytes 4194320 | tf_op jit(solution)/shard_map/all_gather | solution.py:89
  162.9 3.5 %bitcast_reduce_fusion = f32[128,1024]{1,0:T(8,128)S(1)} fusion(f32[1024,1024]{1,0:T(8,128)} %all-gather.2.cloned.1.call-done), kind=kLoop, calls=%fused_computation.9 | loop fusion | flops 1966080 | bytes 4718592 | tf_op jit(solution)/shard_map/reduce_sum | solution.py:91
  166.4 0.7 reduce_sum.48
  167.8 2.9 %fusion.56 = (bf16[8,1,64,1024]{3,2,1,0:T(8,128)(2,1)S(1)}, bf16[8,1,64,1024]{3,2,1,0:T(8,128)(2,1)S(1)}, f32[8,1,64,1024]{3,2,1,0:T(8,128)S(1)}) fusion(f32[]{:T(128)S(6)} %add.73, f32[8,2,64,1024]{3,2,1,0:T(8,128)} %bitcast.74, s32[]{:T(128)S(6)} %select_n.35, s32[]{:T(128)S(6)} %select_n.36), kind=kLoop, calls=%fused_computation.69 | loop fusion | flops 2621440 | bytes 8388620 | tf_op jit(solution)/shard_map/convert_element_type | solution.py:62
  170.7 0.7 fusion.65
  171.4 0.7 fusion.64
  172.5 0.8 fusion.29
  173.7 0.5 collective-permute-done
  174.2 0.5 fusion.32
  174.7 1.3 fusion.66
  176.3 0.7 fusion.68
  177.1 0.6 collective-permute-start.2
  177.6 1.1 collective-permute-done.1
  178.7 0.7 fusion.67
  179.5 0.8 fusion.30
  180.7 0.5 add_convert_fusion.1
  181.2 1.3 fusion.69
  182.8 0.7 fusion.71
  183.9 1.3 collective-permute-done.3
  185.3 0.7 fusion.70
  186.0 0.8 fusion.31
  187.2 0.5 add_convert_fusion
  187.7 2.6 %fusion.72 = (bf16[512,1024]{1,0:T(8,128)(2,1)S(1)}, f32[512,1024]{1,0:T(8,128)}) fusion(bf16[512,1024]{1,0:T(8,128)(2,1)S(1)} %collective-permute-done.3, bf16[512,1024]{1,0:T(8,128)(2,1)S(1)} %get-tuple-element.40, bf16[512,512]{0,1:T(8,128)(2,1)S(1)} %add_convert_fusion, bf16[512,512]{0,1:T(8,128)(2,1)S(1)} %fusion.31, f32[512,1024]{1,0:T(8,128)S(1)} %get-tuple-element.41), kind=kOutput, calls=%fused_computation.89 | convolution fusion | flops 1081606144 | bytes 8388608 | tf_op jit(solution)/shard_map/dot_general | solution.py:50
  190.6 2.4 collective-permute-done.5
  193.2 1.6 convolution_convert_fusion
  194.8 6.0 %all-to-all-start.3 = ((bf16[256,16,64]{0,2,1:T(8,128)(2,1)}), bf16[256,16,64]{0,2,1:T(8,128)(2,1)S(1)}, u32[]{:S(2)}, u32[]{:S(2)}) async-start(bf16[256,16,64]{0,2,1:T(8,128)(2,1)} %bitcast.23), calls=%async_computation.4 | async-start | bytes 1048576 | tf_op jit(solution)/shard_map/all_to_all | solution.py:112
  200.9 14.8 %all-to-all-done.3 = bf16[256,16,64]{0,2,1:T(8,128)(2,1)S(1)} async-done(((bf16[256,16,64]{0,2,1:T(8,128)(2,1)}), bf16[256,16,64]{0,2,1:T(8,128)(2,1)S(1)}, u32[]{:S(2)}, u32[]{:S(2)}) %all-to-all-start.3) | async-done | bytes 524320 | tf_op jit(solution)/shard_map/all_to_all | solution.py:112
  216.2 3.2 %fusion.33 = f32[256,4,16]{0,2,1:T(8,128)S(1)} fusion(bf16[4096,4,16]{0,2,1:T(8,128)(2,1)S(1)} %reshape.84, s32[4,4096]{1,0:T(4,128)S(1)} %bitcast.90), kind=kOutput, calls=%fused_computation.47 | convolution fusion | flops 138412032 | bytes 655360 | tf_op jit(solution)/shard_map/mnk,nmj->kmj/dot_general | solution.py:36
  219.9 0.8 pad_maximum_fusion
  220.7 6.8 %all-to-all-start.4 = ((f32[16,16,68]{2,1,0:T(8,128)}), f32[16,16,68]{2,1,0:T(8,128)S(1)}, u32[]{:S(2)}, u32[]{:S(2)}) async-start(f32[16,16,68]{2,1,0:T(8,128)} %pad_maximum_fusion), calls=%async_computation.5 | async-start | bytes 262144 | tf_op jit(solution)/shard_map/all_to_all | solution.py:43
  227.6 7.7 %all-to-all-done.4 = f32[16,16,68]{2,1,0:T(8,128)S(1)} async-done(((f32[16,16,68]{2,1,0:T(8,128)}), f32[16,16,68]{2,1,0:T(8,128)S(1)}, u32[]{:S(2)}, u32[]{:S(2)}) %all-to-all-start.4) | async-done | bytes 69664 | tf_op jit(solution)/shard_map/all_to_all | solution.py:43
  235.3 0.6 broadcast_in_dim.7
  236.0 3.6 %all-to-all-start.5 = ((f32[16,16,68]{2,1,0:T(8,128)}), f32[16,16,68]{2,1,0:T(8,128)S(1)}, u32[]{:S(2)}, u32[]{:S(2)}) async-start(f32[16,16,68]{2,1,0:T(8,128)} %broadcast_in_dim.7), calls=%async_computation.6 | async-start | bytes 262144 | tf_op jit(solution)/shard_map/all_to_all | solution.py:46
  239.6 1.7 dynamic-slice_bitcast_fusion
  241.3 2.0 copy.65
  243.3 4.1 %all-to-all-done.5 = f32[16,16,68]{2,1,0:T(8,128)S(1)} async-done(((f32[16,16,68]{2,1,0:T(8,128)}), f32[16,16,68]{2,1,0:T(8,128)S(1)}, u32[]{:S(2)}, u32[]{:S(2)}) %all-to-all-start.5) | async-done | bytes 69664 | tf_op jit(solution)/shard_map/all_to_all | solution.py:46
  247.8 0.7 copy.66
  (36 shorter events, 4.8 us)
Async XLA Ops:
  7.2 24.1 %copy-start = (bf16[256,1024]{1,0:T(8,128)(2,1)S(1)}, bf16[256,1024]{1,0:T(8,128)(2,1)}, u32[]{:S(2)}) copy-start(bf16[256,1024]{1,0:T(8,128)(2,1)} %param.3) | copy-start | bytes 1572868
  7.2 85.0 %reduce-scatter.2.cloned.1.call-start = ((), (), s32[]{:S(2)}) async-start(), calls=%async_computation.7 | async-start | bytes 4456448 | tf_op jit(solution)/shard_map/reduce_scatter | solution.py:84
  34.0 0.8 copy-start.2
  34.0 128.8 %all-gather.2.cloned.1.call-start = ((), (), s32[]{:S(2)}) async-start(), calls=%async_computation.8 | async-start | bytes 4456448 | tf_op jit(solution)/shard_map/all_gather | solution.py:89
  172.2 2.0 collective-permute-start
  176.0 2.7 %collective-permute-start.1 = (bf16[512,1024]{1,0:T(8,128)(2,1)S(1)}, bf16[512,1024]{1,0:T(8,128)(2,1)S(1)}, u32[]{:S(2)}, u32[]{:S(2)}) collective-permute-start(bf16[512,1024]{1,0:T(8,128)(2,1)S(1)} %get-tuple-element.34), channel_id=1, source_target_pairs={{0,1},{1,0},{2,3},{3,2},{4,5},{5,4},{6,7},{7,6},{8,9},{9,8},{10,11... | collective-permute-start | bytes 3145736 | tf_op jit(solution)/shard_map/ppermute | solution.py:58
  177.1 3.6 %collective-permute-start.2 = (bf16[512,512]{0,1:T(8,128)(2,1)S(1)}, bf16[512,512]{0,1:T(8,128)(2,1)S(1)}, u32[]{:S(2)}, u32[]{:S(2)}) collective-permute-start(bf16[512,512]{0,1:T(8,128)(2,1)S(1)} %get-tuple-element.38), channel_id=1, source_target_pairs={{0,1},{1,0},{2,3},{3,2},{4,5},{5,4},{6,7},{7,6},{8,9},{9,8},{10,11... | collective-permute-start | bytes 1572872 | tf_op jit(solution)/shard_map/ppermute | solution.py:58
  182.5 2.7 %collective-permute-start.3 = (bf16[512,1024]{1,0:T(8,128)(2,1)S(1)}, bf16[512,1024]{1,0:T(8,128)(2,1)S(1)}, u32[]{:S(2)}, u32[]{:S(2)}) collective-permute-start(bf16[512,1024]{1,0:T(8,128)(2,1)S(1)} %get-tuple-element.40), channel_id=1, source_target_pairs={{0,1},{1,0},{2,3},{3,2},{4,5},{5,4},{6,7},{7,6},{8,9},{9,8},{10,11... | collective-permute-start | bytes 3145736 | tf_op jit(solution)/shard_map/ppermute | solution.py:58
  183.6 3.6 %collective-permute-start.4 = (bf16[512,512]{0,1:T(8,128)(2,1)S(1)}, bf16[512,512]{0,1:T(8,128)(2,1)S(1)}, u32[]{:S(2)}, u32[]{:S(2)}) collective-permute-start(bf16[512,512]{0,1:T(8,128)(2,1)S(1)} %get-tuple-element.44), channel_id=1, source_target_pairs={{0,1},{1,0},{2,3},{3,2},{4,5},{5,4},{6,7},{7,6},{8,9},{9,8},{10,11... | collective-permute-start | bytes 1572872 | tf_op jit(solution)/shard_map/ppermute | solution.py:58
  190.3 2.7 %collective-permute-start.5 = (bf16[512,1024]{1,0:T(8,128)(2,1)S(1)}, bf16[512,1024]{1,0:T(8,128)(2,1)S(1)}, u32[]{:S(2)}, u32[]{:S(2)}) collective-permute-start(bf16[512,1024]{1,0:T(8,128)(2,1)S(1)} %get-tuple-element.46), channel_id=1, source_target_pairs={{0,1},{1,0},{2,3},{3,2},{4,5},{5,4},{6,7},{7,6},{8,9},{9,8},{10,11... | collective-permute-start | bytes 3145736 | tf_op jit(solution)/shard_map/ppermute | solution.py:58
  194.8 20.9 %all-to-all-start.3 = ((bf16[256,16,64]{0,2,1:T(8,128)(2,1)}), bf16[256,16,64]{0,2,1:T(8,128)(2,1)S(1)}, u32[]{:S(2)}, u32[]{:S(2)}) async-start(bf16[256,16,64]{0,2,1:T(8,128)(2,1)} %bitcast.23), calls=%async_computation.4 | async-start | bytes 1048576 | tf_op jit(solution)/shard_map/all_to_all | solution.py:112
  216.2 11.3 %copy-start.1 = (bf16[256,64]{0,1:T(8,128)(2,1)S(1)}, bf16[256,64]{0,1:T(8,128)(2,1)}, u32[]{:S(2)}) copy-start(bf16[256,64]{0,1:T(8,128)(2,1)} %param.5) | copy-start | bytes 98308
  220.7 14.7 %all-to-all-start.4 = ((f32[16,16,68]{2,1,0:T(8,128)}), f32[16,16,68]{2,1,0:T(8,128)S(1)}, u32[]{:S(2)}, u32[]{:S(2)}) async-start(f32[16,16,68]{2,1,0:T(8,128)} %pad_maximum_fusion), calls=%async_computation.5 | async-start | bytes 262144 | tf_op jit(solution)/shard_map/all_to_all | solution.py:43
  236.0 11.4 %all-to-all-start.5 = ((f32[16,16,68]{2,1,0:T(8,128)}), f32[16,16,68]{2,1,0:T(8,128)S(1)}, u32[]{:S(2)}, u32[]{:S(2)}) async-start(f32[16,16,68]{2,1,0:T(8,128)} %broadcast_in_dim.7), calls=%async_computation.6 | async-start | bytes 262144 | tf_op jit(solution)/shard_map/all_to_all | solution.py:46
Sparse Core Ops, SparseCore 0:
  34.1 58.0 reduce-scatter.1
  121.8 41.0 all-gather.1

commit v8 on v7

--- a/solution.py
+++ b/solution.py
@@ -88,27 +88,26 @@
     cross_panel = rows_sum(partial_panel)
     cross = lax.all_gather(cross_panel, "sub", axis=0, tiled=True)
     width = cross.shape[1]
-    square_rows = jnp.sum((cross * cross).reshape(-1, 8, width), axis=1)
-    frob_scale = jnp.sqrt(jnp.sum(lax.optimization_barrier(square_rows))) + frob_eps
+    frob_scale = jnp.sqrt(jnp.sum(cross * cross)) + frob_eps
     core = lax.axis_index("sub") % 2
     panel_rows = cross.shape[0] // lax.axis_size("sub")
     by_parity = cross.reshape(-1, 2, panel_rows, width)
     z_own = lax.dynamic_index_in_dim(by_parity, core, axis=1, keepdims=False).reshape(-1, width) / frob_scale
     z_other = lax.dynamic_index_in_dim(by_parity, 1 - core, axis=1, keepdims=False).reshape(-1, width) / frob_scale
     z_other_half = z_other.astype(jnp.bfloat16)
-    for newton_step_index in range(NS_STEPS):
+    for newton_step_index in range(NS_STEPS - 1):
         z_own = newton_half(z_own, z_other_half)
         z_other_half = partner(z_own.astype(jnp.bfloat16))
-    own_panels = z_own.astype(jnp.bfloat16).reshape(-1, panel_rows, width)
-    other_panels = z_other_half.reshape(-1, panel_rows, width)
-    rotation_half = jnp.where(
-        core == 0,
-        jnp.stack([own_panels, other_panels], axis=1),
-        jnp.stack([other_panels, own_panels], axis=1),
-    ).reshape(-1, width)
-    rotated = jnp.dot(embeddings, rotation_half, preferred_element_type=jnp.float32).astype(
-        jnp.bfloat16
-    )
+    z_own = newton_half(z_own, z_other_half)
+    own_half = z_own.astype(jnp.bfloat16)
+    z_other_half = partner(own_half)
+    columns = embeddings.reshape(embeddings.shape[0], -1, 2, panel_rows)
+    own_columns = lax.dynamic_index_in_dim(columns, core, axis=2, keepdims=False).reshape(embeddings.shape[0], -1)
+    other_columns = lax.dynamic_index_in_dim(columns, 1 - core, axis=2, keepdims=False).reshape(embeddings.shape[0], -1)
+    rotated = (
+        jnp.dot(own_columns, own_half, preferred_element_type=jnp.float32)
+        + jnp.dot(other_columns, z_other_half, preferred_element_type=jnp.float32)
+    ).astype(jnp.bfloat16)
     moved_rows = lax.all_to_all(rotated, "sub", split_axis=1, concat_axis=0, tiled=True)
     code_sums = codeword_sums(moved_codes, moved_rows, table.shape[0])
     sums_width = code_sums.shape[1]

time: 258 us -> 259 us (level)
    all_to_all x1, waiting for transfers between devices: 4.12 us -> 7.11 us  [rows_sum(): lax.all_to_all(spread, 'rows', split_axis=0, concat_axis=0, tiled=True)]
  transfers between devices with their start and end apart: 11 -> 11, of which waited for: 9 -> 8; matrix products, arithmetic and copies ran while one was open for 7% -> 7% of each run, Pallas kernels for 0% -> 0%
where the time goes in v8:
time: 259 us; the launch traced here: 256 us
  waiting for transfers between devices  112 us (43%)
  blocking collectives  58.1 us (22%)
  matrix products  26.9 us (10%)
  starting transfers between devices  18.7 us (7%)
  between operations  15.1 us (6%)
  other arithmetic  14.5 us (6%)
  local copies, waits for them, and re-layouts  10.4 us (4%)
    all_gather x1, waiting for transfers between devices, body(): cross = lax.all_gather(cross_panel, 'sub', axis=0, tiled=True)  41.1 us
    reduce_scatter x1, waiting for transfers between devices, body(): lax.psum_scatter(partial_t, 'sub', scatter_dimension=1, tiled=True)  38.6 us
    all_gather x1, blocking collectives, body(): table = lax.all_gather(codebook, 'sub', axis=1, tiled=True)  18.6 us
    all_to_all x1, blocking collectives, rows_sum(): lax.all_to_all(x, 'rows', split_axis=0, concat_axis=0, tiled=True)  15.1 us
    all_to_all x1, waiting for transfers between devices, body(): lax.all_to_all(rotated, 'sub', split_axis=1, concat_axis=0, tiled=True)  14.8 us
    dot_general x18, matrix products, bdot(): lax.dot_general(left.astype(jnp.bfloat16), right.astype(jnp.bfloat16), (d...  13.4 us
    all_to_all x1, blocking collectives, rows_sum(): lax.all_to_all(spread, 'rows', split_axis=0, concat_axis=0, tiled=True)  12.5 us
    all_to_all x1, blocking collectives, body(): lax.all_to_all(codes, 'sub', split_axis=0, concat_axis=1, tiled=True)  11.9 us
  transfers between devices with their start and end apart: 11, of which 8 were waited for; matrix products, arithmetic and copies ran while one was open for 7% of the time, Pallas kernels for 0%

profile of v8, /device:TPU:64, one launch (start us, length us, event | category | flops | bytes accessed | tf_op | source)
XLA Modules:
  0.0 255.8 jit_solution(1178929608850901659)
XLA Ops:
  7.2 18.6 %all_gather.6 = bf16[256,1024]{0,1:T(8,128)(2,1)S(1)} all-gather(bf16[256,64]{0,1:T(8,128)(2,1)} %param.5), channel_id=1, replica_groups=mesh['rows'=16,'sub'=16] {'sub'}, dimensions={1}, use_global_device_ids=true | all-gather | bytes 557056 | tf_op jit(solution)/shard_map/all_gather | solution.py:79
  25.9 5.3 %fusion.29 = bf16[64,256,16]{1,2,0:T(8,128)(2,1)S(1)} fusion(bf16[256,64,16]{0,2,1:T(8,128)(2,1)S(1)} %bitcast.78, s32[64,256]{1,0:T(8,128)} %param.4), kind=kOutput, calls=%fused_computation.42 | convolution fusion | flops 138674176 | bytes 1114112 | tf_op jit(solution)/shard_map/mnk,kmj->nmj/dot_general | solution.py:26
  31.2 2.7 %fusion.74 = f32[1024,1024]{0,1:T(8,128)} fusion(bf16[256,1024]{0,1:T(8,128)(2,1)S(1)} %bitcast.72, bf16[256,1024]{1,0:T(8,128)(2,1)S(1)} %copy-done), kind=kOutput, calls=%fused_computation.92 | convolution fusion | flops 536870912 | bytes 5242880 | tf_op jit(solution)/shard_map/dot_general | solution.py:81
  34.0 0.8 copy-done.3
  34.8 11.9 %all_to_all.68 = s32[16,4,256]{2,1,0:T(4,128)S(1)} all-to-all(s32[16,4,256]{2,1,0:T(4,128)S(1)} %all_to_all.48), channel_id=1, replica_groups=mesh['rows'=16,'sub'=16] {'sub'}, dimensions={0} | all-to-all | bytes 131072 | tf_op jit(solution)/shard_map/all_to_all | solution.py:78
  46.6 6.9 %convert_reduce_fusion = f32[4,256]{1,0:T(4,128)S(1)} fusion(s32[4,4096]{1,0:T(4,128)S(1)} %bitcast.81), kind=kLoop, calls=%fused_computation.1 | loop fusion | flops 16776192 | bytes 69632 | tf_op jit(solution)/shard_map/reduce_sum | solution.py:86
  53.5 38.6 %reduce-scatter.2.cloned.1.call-done = f32[1024,64]{0,1:T(8,128)} async-done(((f32[1024,1024]{0,1:T(8,128)}), f32[1024,64]{0,1:T(8,128)}) %reduce-scatter.2.cloned.1.call-update) | async-done | bytes 262160 | tf_op jit(solution)/shard_map/reduce_scatter | solution.py:84
  92.1 1.0 all_to_all.52
  93.2 15.1 %all_to_all.69 = f32[16,4,1024]{2,1,0:T(4,128)S(1)} all-to-all(f32[16,4,1024]{2,1,0:T(4,128)S(1)} %all_to_all.52), channel_id=1, replica_groups=mesh['rows'=16,'sub'=16] {'rows'}, dimensions={0} | all-to-all | bytes 524288 | tf_op jit(solution)/shard_map/all_to_all | solution.py:43
  108.3 12.5 %all_to_all.70 = f32[16,4,1024]{2,1,0:T(4,128)S(1)} all-to-all(f32[16,4,1024]{2,1,0:T(4,128)S(1)} %broadcast_in_dim.6), channel_id=1, replica_groups=mesh['rows'=16,'sub'=16] {'rows'}, dimensions={0} | all-to-all | bytes 524288 | tf_op jit(solution)/shard_map/all_to_all | solution.py:46
  120.8 0.8 all_to_all.55
  121.7 41.1 %all-gather.2.cloned.1.call-done = f32[1024,1024]{1,0:T(8,128)} async-done(((f32[64,1024]{1,0:T(8,128)}), f32[1024,1024]{1,0:T(8,128)}) %all-gather.2.cloned.1.call-update) | async-done | bytes 4194320 | tf_op jit(solution)/shard_map/all_gather | solution.py:89
  162.8 3.9 %multiply_reduce_fusion = f32[]{:T(128)} fusion(f32[1024,1024]{1,0:T(8,128)} %all-gather.2.cloned.1.call-done), kind=kLoop, calls=%fused_computation.9 | loop fusion | flops 2097151 | bytes 4194308 | tf_op jit(solution)/shard_map/reduce_sum | solution.py:91
  167.3 2.9 %fusion.57 = (bf16[8,1,64,1024]{3,2,1,0:T(8,128)(2,1)S(1)}, bf16[8,1,64,1024]{3,2,1,0:T(8,128)(2,1)S(1)}, f32[8,1,64,1024]{3,2,1,0:T(8,128)S(1)}) fusion(f32[]{:T(128)S(6)} %add.79, f32[8,2,64,1024]{3,2,1,0:T(8,128)} %bitcast.66, s32[]{:T(128)S(6)} %select_n.26, s32[]{:T(128)S(6)} %select_n.27), kind=kLoop, calls=%fused_computation.69 | loop fusion | flops 2621440 | bytes 8388620 | tf_op jit(solution)/shard_map/convert_element_type | solution.py:62
  170.2 0.7 fusion.66
  171.0 0.7 fusion.65
  172.0 0.8 fusion.30
  173.2 0.5 collective-permute-done
  173.7 0.5 fusion.33
  174.2 1.3 fusion.67
  175.8 0.7 fusion.69
  176.6 0.6 collective-permute-start.2
  177.1 1.1 collective-permute-done.1
  178.3 0.8 fusion.68
  179.1 0.8 fusion.31
  180.3 0.5 add_convert_fusion.1
  180.8 1.3 fusion.70
  182.4 0.7 fusion.72
  183.5 1.3 collective-permute-done.3
  184.8 0.7 fusion.71
  185.6 0.8 fusion.32
  186.8 0.5 add_convert_fusion
  187.3 1.3 fusion.73
  188.9 2.0 copy.40
  190.9 1.1 constant_dynamic-slice_fusion
  192.5 1.7 fusion.28
  194.2 1.0 copy.41
  195.2 6.0 %all-to-all-start.3 = ((bf16[256,16,64]{0,2,1:T(8,128)(2,1)}), bf16[256,16,64]{0,2,1:T(8,128)(2,1)S(1)}, u32[]{:S(2)}, u32[]{:S(2)}) async-start(bf16[256,16,64]{0,2,1:T(8,128)(2,1)} %bitcast.17), calls=%async_computation.4 | async-start | bytes 1048576 | tf_op jit(solution)/shard_map/all_to_all | solution.py:111
  201.4 14.8 %all-to-all-done.3 = bf16[256,16,64]{0,2,1:T(8,128)(2,1)S(1)} async-done(((bf16[256,16,64]{0,2,1:T(8,128)(2,1)}), bf16[256,16,64]{0,2,1:T(8,128)(2,1)S(1)}, u32[]{:S(2)}, u32[]{:S(2)}) %all-to-all-start.3) | async-done | bytes 524320 | tf_op jit(solution)/shard_map/all_to_all | solution.py:111
  216.7 3.2 %fusion.34 = f32[256,4,16]{0,2,1:T(8,128)S(1)} fusion(bf16[4096,4,16]{0,2,1:T(8,128)(2,1)S(1)} %reshape.89, s32[4,4096]{1,0:T(4,128)S(1)} %bitcast.82), kind=kOutput, calls=%fused_computation.47 | convolution fusion | flops 138412032 | bytes 655360 | tf_op jit(solution)/shard_map/mnk,nmj->kmj/dot_general | solution.py:36
  220.4 0.8 pad_maximum_fusion
  221.1 6.8 %all-to-all-start.4 = ((f32[16,16,68]{2,1,0:T(8,128)}), f32[16,16,68]{2,1,0:T(8,128)S(1)}, u32[]{:S(2)}, u32[]{:S(2)}) async-start(f32[16,16,68]{2,1,0:T(8,128)} %pad_maximum_fusion), calls=%async_computation.5 | async-start | bytes 262144 | tf_op jit(solution)/shard_map/all_to_all | solution.py:43
  228.1 7.7 %all-to-all-done.4 = f32[16,16,68]{2,1,0:T(8,128)S(1)} async-done(((f32[16,16,68]{2,1,0:T(8,128)}), f32[16,16,68]{2,1,0:T(8,128)S(1)}, u32[]{:S(2)}, u32[]{:S(2)}) %all-to-all-start.4) | async-done | bytes 69664 | tf_op jit(solution)/shard_map/all_to_all | solution.py:43
  235.8 0.7 broadcast_in_dim.7
  236.5 3.6 %all-to-all-start.5 = ((f32[16,16,68]{2,1,0:T(8,128)}), f32[16,16,68]{2,1,0:T(8,128)S(1)}, u32[]{:S(2)}, u32[]{:S(2)}) async-start(f32[16,16,68]{2,1,0:T(8,128)} %broadcast_in_dim.7), calls=%async_computation.6 | async-start | bytes 262144 | tf_op jit(solution)/shard_map/all_to_all | solution.py:46
  240.1 0.7 dynamic-slice_bitcast_fusion
  240.8 7.1 %all-to-all-done.5 = f32[16,16,68]{2,1,0:T(8,128)S(1)} async-done(((f32[16,16,68]{2,1,0:T(8,128)}), f32[16,16,68]{2,1,0:T(8,128)S(1)}, u32[]{:S(2)}, u32[]{:S(2)}) %all-to-all-start.5) | async-done | bytes 69664 | tf_op jit(solution)/shard_map/all_to_all | solution.py:46
  248.3 0.7 copy.50
  (39 shorter events, 5.2 us)
Async XLA Ops:
  7.2 85.0 %reduce-scatter.2.cloned.1.call-start = ((), (), s32[]{:S(2)}) async-start(), calls=%async_computation.7 | async-start | bytes 4456448 | tf_op jit(solution)/shard_map/reduce_scatter | solution.py:84
  25.8 5.3 %copy-start = (bf16[256,1024]{1,0:T(8,128)(2,1)S(1)}, bf16[256,1024]{1,0:T(8,128)(2,1)}, u32[]{:S(2)}) copy-start(bf16[256,1024]{1,0:T(8,128)(2,1)} %param.3) | copy-start | bytes 1572868
  33.9 0.8 copy-start.3
  33.9 128.8 %all-gather.2.cloned.1.call-start = ((), (), s32[]{:S(2)}) async-start(), calls=%async_computation.8 | async-start | bytes 4456448 | tf_op jit(solution)/shard_map/all_gather | solution.py:89
  171.7 2.0 collective-permute-start
  175.5 2.7 %collective-permute-start.1 = (bf16[512,1024]{1,0:T(8,128)(2,1)S(1)}, bf16[512,1024]{1,0:T(8,128)(2,1)S(1)}, u32[]{:S(2)}, u32[]{:S(2)}) collective-permute-start(bf16[512,1024]{1,0:T(8,128)(2,1)S(1)} %get-tuple-element.33), channel_id=1, source_target_pairs={{0,1},{1,0},{2,3},{3,2},{4,5},{5,4},{6,7},{7,6},{8,9},{9,8},{10,11... | collective-permute-start | bytes 3145736 | tf_op jit(solution)/shard_map/ppermute | solution.py:58
  176.6 3.7 %collective-permute-start.2 = (bf16[512,512]{0,1:T(8,128)(2,1)S(1)}, bf16[512,512]{0,1:T(8,128)(2,1)S(1)}, u32[]{:S(2)}, u32[]{:S(2)}) collective-permute-start(bf16[512,512]{0,1:T(8,128)(2,1)S(1)} %get-tuple-element.37), channel_id=1, source_target_pairs={{0,1},{1,0},{2,3},{3,2},{4,5},{5,4},{6,7},{7,6},{8,9},{9,8},{10,11... | collective-permute-start | bytes 1572872 | tf_op jit(solution)/shard_map/ppermute | solution.py:58
  182.1 2.7 %collective-permute-start.3 = (bf16[512,1024]{1,0:T(8,128)(2,1)S(1)}, bf16[512,1024]{1,0:T(8,128)(2,1)S(1)}, u32[]{:S(2)}, u32[]{:S(2)}) collective-permute-start(bf16[512,1024]{1,0:T(8,128)(2,1)S(1)} %get-tuple-element.39), channel_id=1, source_target_pairs={{0,1},{1,0},{2,3},{3,2},{4,5},{5,4},{6,7},{7,6},{8,9},{9,8},{10,11... | collective-permute-start | bytes 3145736 | tf_op jit(solution)/shard_map/ppermute | solution.py:58
  183.1 3.7 %collective-permute-start.4 = (bf16[512,512]{0,1:T(8,128)(2,1)S(1)}, bf16[512,512]{0,1:T(8,128)(2,1)S(1)}, u32[]{:S(2)}, u32[]{:S(2)}) collective-permute-start(bf16[512,512]{0,1:T(8,128)(2,1)S(1)} %get-tuple-element.43), channel_id=1, source_target_pairs={{0,1},{1,0},{2,3},{3,2},{4,5},{5,4},{6,7},{7,6},{8,9},{9,8},{10,11... | collective-permute-start | bytes 1572872 | tf_op jit(solution)/shard_map/ppermute | solution.py:58
  188.6 3.9 %collective-permute-start.5 = (bf16[512,1024]{1,0:T(8,128)(2,1)S(1)}, bf16[512,1024]{1,0:T(8,128)(2,1)}, u32[]{:S(2)}, u32[]{:S(2)}) collective-permute-start(bf16[512,1024]{1,0:T(8,128)(2,1)S(1)} %get-tuple-element.45), channel_id=1, source_target_pairs={{0,1},{1,0},{2,3},{3,2},{4,5},{5,4},{6,7},{7,6},{8,9},{9,8},{10,11... | collective-permute-start | bytes 3145736 | tf_op jit(solution)/shard_map/ppermute | solution.py:58
  194.2 1.0 copy-start.1
  195.2 20.9 %all-to-all-start.3 = ((bf16[256,16,64]{0,2,1:T(8,128)(2,1)}), bf16[256,16,64]{0,2,1:T(8,128)(2,1)S(1)}, u32[]{:S(2)}, u32[]{:S(2)}) async-start(bf16[256,16,64]{0,2,1:T(8,128)(2,1)} %bitcast.17), calls=%async_computation.4 | async-start | bytes 1048576 | tf_op jit(solution)/shard_map/all_to_all | solution.py:111
  216.7 11.3 %copy-start.2 = (bf16[256,64]{0,1:T(8,128)(2,1)S(1)}, bf16[256,64]{0,1:T(8,128)(2,1)}, u32[]{:S(2)}) copy-start(bf16[256,64]{0,1:T(8,128)(2,1)} %param.5) | copy-start | bytes 98308
  221.1 14.7 %all-to-all-start.4 = ((f32[16,16,68]{2,1,0:T(8,128)}), f32[16,16,68]{2,1,0:T(8,128)S(1)}, u32[]{:S(2)}, u32[]{:S(2)}) async-start(f32[16,16,68]{2,1,0:T(8,128)} %pad_maximum_fusion), calls=%async_computation.5 | async-start | bytes 262144 | tf_op jit(solution)/shard_map/all_to_all | solution.py:43
  236.5 11.4 %all-to-all-start.5 = ((f32[16,16,68]{2,1,0:T(8,128)}), f32[16,16,68]{2,1,0:T(8,128)S(1)}, u32[]{:S(2)}, u32[]{:S(2)}) async-start(f32[16,16,68]{2,1,0:T(8,128)} %broadcast_in_dim.7), calls=%async_computation.6 | async-start | bytes 262144 | tf_op jit(solution)/shard_map/all_to_all | solution.py:46
Sparse Core Ops, SparseCore 0:
  34.1 58.0 reduce-scatter.1
  121.8 40.9 all-gather.1

commit v9 on v8

--- a/solution.py
+++ b/solution.py
@@ -84,7 +84,14 @@
     partial_panel = lax.psum_scatter(partial_t, "sub", scatter_dimension=1, tiled=True).T
     code_one_hot = one_hot_codes(moved_codes, table.shape[0])
     counts = jnp.sum(code_one_hot, axis=1, dtype=jnp.float32).T
-    partial_panel, moved_codes, counts = lax.optimization_barrier((partial_panel, moved_codes, counts))
+    core = lax.axis_index("sub") % 2
+    panel_rows = partial_panel.shape[0]
+    columns = embeddings.reshape(embeddings.shape[0], -1, 2, panel_rows)
+    own_columns = lax.dynamic_index_in_dim(columns, core, axis=2, keepdims=False).reshape(embeddings.shape[0], -1)
+    other_columns = lax.dynamic_index_in_dim(columns, 1 - core, axis=2, keepdims=False).reshape(embeddings.shape[0], -1)
+    partial_panel, moved_codes, counts, own_columns, other_columns = lax.optimization_barrier(
+        (partial_panel, moved_codes, counts, own_columns, other_columns)
+    )
     cross_panel = rows_sum(partial_panel)
     cross = lax.all_gather(cross_panel, "sub", axis=0, tiled=True)
     width = cross.shape[1]
@@ -101,9 +108,6 @@
     z_own = newton_half(z_own, z_other_half)
     own_half = z_own.astype(jnp.bfloat16)
     z_other_half = partner(own_half)
-    columns = embeddings.reshape(embeddings.shape[0], -1, 2, panel_rows)
-    own_columns = lax.dynamic_index_in_dim(columns, core, axis=2, keepdims=False).reshape(embeddings.shape[0], -1)
-    other_columns = lax.dynamic_index_in_dim(columns, 1 - core, axis=2, keepdims=False).reshape(embeddings.shape[0], -1)
     rotated = (
         jnp.dot(own_columns, own_half, preferred_element_type=jnp.float32)
         + jnp.dot(other_columns, z_other_half, preferred_element_type=jnp.float32)

time: 259 us -> 256 us (0.988)
  blocking collectives: 58.1 us -> 46.2 us
  waiting for transfers between devices: 112 us -> 119 us
  starting transfers between devices: 18.7 us -> 25 us
    all_to_all x1 -> x0, blocking collectives: 11.9 us -> none  [body(): lax.all_to_all(codes, 'sub', split_axis=0, concat_axis=1, tiled=True)]
    all_to_all x0 -> x1, starting transfers between devices: none -> 6.32 us  [body(): lax.all_to_all(codes, 'sub', split_axis=0, concat_axis=1, tiled=True)]
    all_to_all x0 -> x1, waiting for transfers between devices: none -> 5.41 us  [body(): lax.all_to_all(codes, 'sub', split_axis=0, concat_axis=1, tiled=True)]
  transfers between devices with their start and end apart: 11 -> 12, of which waited for: 8 -> 10; matrix products, arithmetic and copies ran while one was open for 7% -> 6% of each run, Pallas kernels for 0% -> 0%
where the time goes in v9:
time: 256 us; the launch traced here: 253 us
  waiting for transfers between devices  119 us (46%)
  blocking collectives  46.2 us (18%)
  matrix products  25.6 us (10%)
  starting transfers between devices  25 us (10%)
  between operations  15.1 us (6%)
  other arithmetic  14.5 us (6%)
  local copies, waits for them, and re-layouts  8.2 us (3%)
    all_gather x1, waiting for transfers between devices, body(): cross = lax.all_gather(cross_panel, 'sub', axis=0, tiled=True)  41.2 us
    reduce_scatter x1, waiting for transfers between devices, body(): lax.psum_scatter(partial_t, 'sub', scatter_dimension=1, tiled=True)  37.8 us
    all_gather x1, blocking collectives, body(): table = lax.all_gather(codebook, 'sub', axis=1, tiled=True)  18.6 us
    all_to_all x1, blocking collectives, rows_sum(): lax.all_to_all(x, 'rows', split_axis=0, concat_axis=0, tiled=True)  15.1 us
    all_to_all x1, waiting for transfers between devices, body(): lax.all_to_all(rotated, 'sub', split_axis=1, concat_axis=0, tiled=True)  14.8 us
    dot_general x18, matrix products, bdot(): lax.dot_general(left.astype(jnp.bfloat16), right.astype(jnp.bfloat16), (d...  13.4 us
    all_to_all x1, blocking collectives, rows_sum(): lax.all_to_all(spread, 'rows', split_axis=0, concat_axis=0, tiled=True)  12.4 us
    all_to_all x1, waiting for transfers between devices, rows_sum(): lax.all_to_all(x, 'rows', split_axis=0, concat_axis=0, tiled=True)  7.7 us
  transfers between devices with their start and end apart: 12, of which 10 were waited for; matrix products, arithmetic and copies ran while one was open for 6% of the time, Pallas kernels for 0%

profile of v9, /device:TPU:64, one launch (start us, length us, event | category | flops | bytes accessed | tf_op | source)
XLA Modules:
  0.0 253.4 jit_solution(15722012978009492368)
XLA Ops:
  7.2 18.6 %all_gather.6 = bf16[256,1024]{0,1:T(8,128)(2,1)S(1)} all-gather(bf16[256,64]{0,1:T(8,128)(2,1)} %param.5), channel_id=1, replica_groups=mesh['rows'=16,'sub'=16] {'sub'}, dimensions={1}, use_global_device_ids=true | all-gather | bytes 557056 | tf_op jit(solution)/shard_map/all_gather | solution.py:79
  25.8 5.3 %fusion.29 = bf16[64,256,16]{1,2,0:T(8,128)(2,1)S(1)} fusion(bf16[256,64,16]{0,2,1:T(8,128)(2,1)S(1)} %bitcast.78, s32[64,256]{1,0:T(8,128)} %param.4), kind=kOutput, calls=%fused_computation.42 | convolution fusion | flops 138674176 | bytes 1114112 | tf_op jit(solution)/shard_map/mnk,kmj->nmj/dot_general | solution.py:26
  31.2 2.7 %fusion.74 = f32[1024,1024]{0,1:T(8,128)} fusion(bf16[256,1024]{0,1:T(8,128)(2,1)S(1)} %bitcast.72, bf16[256,1024]{1,0:T(8,128)(2,1)S(1)} %copy-done), kind=kOutput, calls=%fused_computation.92 | convolution fusion | flops 536870912 | bytes 5242880 | tf_op jit(solution)/shard_map/dot_general | solution.py:81
  33.9 0.8 copy-done.3
  34.7 0.6 all_to_all.48
  35.4 6.3 %all-to-all-start = ((s32[16,4,256]{2,1,0:T(4,128)}), s32[16,4,256]{2,1,0:T(4,128)S(1)}, u32[]{:S(2)}, u32[]{:S(2)}) async-start(s32[16,4,256]{2,1,0:T(4,128)} %all_to_all.48), calls=%async_computation.1 | async-start | bytes 131072 | tf_op jit(solution)/shard_map/all_to_all | solution.py:78
  42.0 5.4 %all-to-all-done = s32[16,4,256]{2,1,0:T(4,128)S(1)} async-done(((s32[16,4,256]{2,1,0:T(4,128)}), s32[16,4,256]{2,1,0:T(4,128)S(1)}, u32[]{:S(2)}, u32[]{:S(2)}) %all-to-all-start) | async-done | bytes 65568 | tf_op jit(solution)/shard_map/all_to_all | solution.py:78
  47.5 6.9 %convert_reduce_fusion = f32[4,256]{1,0:T(4,128)S(1)} fusion(s32[4,4096]{1,0:T(4,128)S(1)} %bitcast.81), kind=kLoop, calls=%fused_computation.1 | loop fusion | flops 16776192 | bytes 69632 | tf_op jit(solution)/shard_map/reduce_sum | solution.py:86
  54.4 37.8 %reduce-scatter.2.cloned.1.call-done = f32[1024,64]{0,1:T(8,128)} async-done(((f32[1024,1024]{0,1:T(8,128)}), f32[1024,64]{0,1:T(8,128)}) %reduce-scatter.2.cloned.1.call-update) | async-done | bytes 262160 | tf_op jit(solution)/shard_map/reduce_scatter | solution.py:84
  92.1 1.0 all_to_all.52
  93.2 15.1 %all_to_all.68 = f32[16,4,1024]{2,1,0:T(4,128)S(1)} all-to-all(f32[16,4,1024]{2,1,0:T(4,128)S(1)} %all_to_all.52), channel_id=1, replica_groups=mesh['rows'=16,'sub'=16] {'rows'}, dimensions={0} | all-to-all | bytes 524288 | tf_op jit(solution)/shard_map/all_to_all | solution.py:43
  108.3 12.4 %all_to_all.69 = f32[16,4,1024]{2,1,0:T(4,128)S(1)} all-to-all(f32[16,4,1024]{2,1,0:T(4,128)S(1)} %broadcast_in_dim.6), channel_id=1, replica_groups=mesh['rows'=16,'sub'=16] {'rows'}, dimensions={0} | all-to-all | bytes 524288 | tf_op jit(solution)/shard_map/all_to_all | solution.py:46
  120.8 0.8 all_to_all.55
  121.6 41.2 %all-gather.2.cloned.1.call-done = f32[1024,1024]{1,0:T(8,128)} async-done(((f32[64,1024]{1,0:T(8,128)}), f32[1024,1024]{1,0:T(8,128)}) %all-gather.2.cloned.1.call-update) | async-done | bytes 4194320 | tf_op jit(solution)/shard_map/all_gather | solution.py:96
  162.8 3.9 %multiply_reduce_fusion = f32[]{:T(128)} fusion(f32[1024,1024]{1,0:T(8,128)} %all-gather.2.cloned.1.call-done), kind=kLoop, calls=%fused_computation.9 | loop fusion | flops 2097151 | bytes 4194308 | tf_op jit(solution)/shard_map/reduce_sum | solution.py:98
  167.3 2.9 %fusion.57 = (bf16[8,1,64,1024]{3,2,1,0:T(8,128)(2,1)S(1)}, bf16[8,1,64,1024]{3,2,1,0:T(8,128)(2,1)S(1)}, f32[8,1,64,1024]{3,2,1,0:T(8,128)S(1)}) fusion(f32[]{:T(128)S(6)} %add.81, f32[8,2,64,1024]{3,2,1,0:T(8,128)} %bitcast.66, s32[]{:T(128)S(6)} %select_n.28, s32[]{:T(128)S(6)} %select_n.29), kind=kLoop, calls=%fused_computation.69 | loop fusion | flops 2621440 | bytes 8388620 | tf_op jit(solution)/shard_map/convert_element_type | solution.py:62
  170.2 0.7 fusion.66
  170.9 0.7 fusion.65
  172.0 0.8 fusion.30
  173.2 0.5 collective-permute-done
  173.7 0.5 fusion.33
  174.2 1.3 fusion.67
  175.8 0.7 fusion.69
  176.6 0.6 collective-permute-start.2
  177.1 1.1 collective-permute-done.1
  178.3 0.7 fusion.68
  179.0 0.8 fusion.31
  180.2 0.5 add_convert_fusion.1
  180.7 1.3 fusion.70
  182.3 0.7 fusion.72
  183.4 1.3 collective-permute-done.3
  184.8 0.7 fusion.71
  185.5 0.8 fusion.32
  186.7 0.5 add_convert_fusion
  187.2 1.3 fusion.73
  189.3 2.0 collective-permute-done.5
  191.7 1.0 copy.41
  192.7 6.0 %all-to-all-start.3 = ((bf16[256,16,64]{0,2,1:T(8,128)(2,1)}), bf16[256,16,64]{0,2,1:T(8,128)(2,1)S(1)}, u32[]{:S(2)}, u32[]{:S(2)}) async-start(bf16[256,16,64]{0,2,1:T(8,128)(2,1)} %bitcast.17), calls=%async_computation.4 | async-start | bytes 1048576 | tf_op jit(solution)/shard_map/all_to_all | solution.py:115
  198.9 14.8 %all-to-all-done.3 = bf16[256,16,64]{0,2,1:T(8,128)(2,1)S(1)} async-done(((bf16[256,16,64]{0,2,1:T(8,128)(2,1)}), bf16[256,16,64]{0,2,1:T(8,128)(2,1)S(1)}, u32[]{:S(2)}, u32[]{:S(2)}) %all-to-all-start.3) | async-done | bytes 524320 | tf_op jit(solution)/shard_map/all_to_all | solution.py:115
  214.2 3.2 %fusion.34 = f32[256,4,16]{0,2,1:T(8,128)S(1)} fusion(bf16[4096,4,16]{0,2,1:T(8,128)(2,1)S(1)} %reshape.89, s32[4,4096]{1,0:T(4,128)S(1)} %bitcast.82), kind=kOutput, calls=%fused_computation.47 | convolution fusion | flops 138412032 | bytes 655360 | tf_op jit(solution)/shard_map/mnk,nmj->kmj/dot_general | solution.py:36
  217.9 0.8 pad_maximum_fusion
  218.7 6.8 %all-to-all-start.4 = ((f32[16,16,68]{2,1,0:T(8,128)}), f32[16,16,68]{2,1,0:T(8,128)S(1)}, u32[]{:S(2)}, u32[]{:S(2)}) async-start(f32[16,16,68]{2,1,0:T(8,128)} %pad_maximum_fusion), calls=%async_computation.5 | async-start | bytes 262144 | tf_op jit(solution)/shard_map/all_to_all | solution.py:43
  225.6 7.7 %all-to-all-done.4 = f32[16,16,68]{2,1,0:T(8,128)S(1)} async-done(((f32[16,16,68]{2,1,0:T(8,128)}), f32[16,16,68]{2,1,0:T(8,128)S(1)}, u32[]{:S(2)}, u32[]{:S(2)}) %all-to-all-start.4) | async-done | bytes 69664 | tf_op jit(solution)/shard_map/all_to_all | solution.py:43
  233.3 0.7 broadcast_in_dim.7
  234.0 3.6 %all-to-all-start.5 = ((f32[16,16,68]{2,1,0:T(8,128)}), f32[16,16,68]{2,1,0:T(8,128)S(1)}, u32[]{:S(2)}, u32[]{:S(2)}) async-start(f32[16,16,68]{2,1,0:T(8,128)} %broadcast_in_dim.7), calls=%async_computation.6 | async-start | bytes 262144 | tf_op jit(solution)/shard_map/all_to_all | solution.py:46
  237.6 0.7 dynamic-slice_bitcast_fusion
  238.3 7.1 %all-to-all-done.5 = f32[16,16,68]{2,1,0:T(8,128)S(1)} async-done(((f32[16,16,68]{2,1,0:T(8,128)}), f32[16,16,68]{2,1,0:T(8,128)S(1)}, u32[]{:S(2)}, u32[]{:S(2)}) %all-to-all-start.5) | async-done | bytes 69664 | tf_op jit(solution)/shard_map/all_to_all | solution.py:46
  245.8 0.7 copy.50
  (40 shorter events, 5.9 us)
Async XLA Ops:
  7.2 85.0 %reduce-scatter.2.cloned.1.call-start = ((), (), s32[]{:S(2)}) async-start(), calls=%async_computation.7 | async-start | bytes 4456448 | tf_op jit(solution)/shard_map/reduce_scatter | solution.py:84
  25.8 5.3 %copy-start = (bf16[256,1024]{1,0:T(8,128)(2,1)S(1)}, bf16[256,1024]{1,0:T(8,128)(2,1)}, u32[]{:S(2)}) copy-start(bf16[256,1024]{1,0:T(8,128)(2,1)} %param.3) | copy-start | bytes 1572868
  33.9 0.8 copy-start.3
  35.4 12.1 %all-to-all-start = ((s32[16,4,256]{2,1,0:T(4,128)}), s32[16,4,256]{2,1,0:T(4,128)S(1)}, u32[]{:S(2)}, u32[]{:S(2)}) async-start(s32[16,4,256]{2,1,0:T(4,128)} %all_to_all.48), calls=%async_computation.1 | async-start | bytes 131072 | tf_op jit(solution)/shard_map/all_to_all | solution.py:78
  41.7 121.1 %all-gather.2.cloned.1.call-start = ((), (), s32[]{:S(2)}) async-start(), calls=%async_computation.8 | async-start | bytes 4456448 | tf_op jit(solution)/shard_map/all_gather | solution.py:96
  171.7 2.0 collective-permute-start
  175.5 2.7 %collective-permute-start.1 = (bf16[512,1024]{1,0:T(8,128)(2,1)S(1)}, bf16[512,1024]{1,0:T(8,128)(2,1)S(1)}, u32[]{:S(2)}, u32[]{:S(2)}) collective-permute-start(bf16[512,1024]{1,0:T(8,128)(2,1)S(1)} %get-tuple-element.37), channel_id=1, source_target_pairs={{0,1},{1,0},{2,3},{3,2},{4,5},{5,4},{6,7},{7,6},{8,9},{9,8},{10,11... | collective-permute-start | bytes 3145736 | tf_op jit(solution)/shard_map/ppermute | solution.py:58
  176.6 3.6 %collective-permute-start.2 = (bf16[512,512]{0,1:T(8,128)(2,1)S(1)}, bf16[512,512]{0,1:T(8,128)(2,1)S(1)}, u32[]{:S(2)}, u32[]{:S(2)}) collective-permute-start(bf16[512,512]{0,1:T(8,128)(2,1)S(1)} %get-tuple-element.41), channel_id=1, source_target_pairs={{0,1},{1,0},{2,3},{3,2},{4,5},{5,4},{6,7},{7,6},{8,9},{9,8},{10,11... | collective-permute-start | bytes 1572872 | tf_op jit(solution)/shard_map/ppermute | solution.py:58
  182.0 2.7 %collective-permute-start.3 = (bf16[512,1024]{1,0:T(8,128)(2,1)S(1)}, bf16[512,1024]{1,0:T(8,128)(2,1)S(1)}, u32[]{:S(2)}, u32[]{:S(2)}) collective-permute-start(bf16[512,1024]{1,0:T(8,128)(2,1)S(1)} %get-tuple-element.43), channel_id=1, source_target_pairs={{0,1},{1,0},{2,3},{3,2},{4,5},{5,4},{6,7},{7,6},{8,9},{9,8},{10,11... | collective-permute-start | bytes 3145736 | tf_op jit(solution)/shard_map/ppermute | solution.py:58
  183.1 3.6 %collective-permute-start.4 = (bf16[512,512]{0,1:T(8,128)(2,1)S(1)}, bf16[512,512]{0,1:T(8,128)(2,1)S(1)}, u32[]{:S(2)}, u32[]{:S(2)}) collective-permute-start(bf16[512,512]{0,1:T(8,128)(2,1)S(1)} %get-tuple-element.47), channel_id=1, source_target_pairs={{0,1},{1,0},{2,3},{3,2},{4,5},{5,4},{6,7},{7,6},{8,9},{9,8},{10,11... | collective-permute-start | bytes 1572872 | tf_op jit(solution)/shard_map/ppermute | solution.py:58
  188.5 2.7 %collective-permute-start.5 = (bf16[512,1024]{1,0:T(8,128)(2,1)S(1)}, bf16[512,1024]{1,0:T(8,128)(2,1)S(1)}, u32[]{:S(2)}, u32[]{:S(2)}) collective-permute-start(bf16[512,1024]{1,0:T(8,128)(2,1)S(1)} %get-tuple-element.49), channel_id=1, source_target_pairs={{0,1},{1,0},{2,3},{3,2},{4,5},{5,4},{6,7},{7,6},{8,9},{9,8},{10,11... | collective-permute-start | bytes 3145736 | tf_op jit(solution)/shard_map/ppermute | solution.py:58
  191.7 1.0 copy-start.1
  192.7 20.9 %all-to-all-start.3 = ((bf16[256,16,64]{0,2,1:T(8,128)(2,1)}), bf16[256,16,64]{0,2,1:T(8,128)(2,1)S(1)}, u32[]{:S(2)}, u32[]{:S(2)}) async-start(bf16[256,16,64]{0,2,1:T(8,128)(2,1)} %bitcast.17), calls=%async_computation.4 | async-start | bytes 1048576 | tf_op jit(solution)/shard_map/all_to_all | solution.py:115
  214.2 11.3 %copy-start.2 = (bf16[256,64]{0,1:T(8,128)(2,1)S(1)}, bf16[256,64]{0,1:T(8,128)(2,1)}, u32[]{:S(2)}) copy-start(bf16[256,64]{0,1:T(8,128)(2,1)} %param.5) | copy-start | bytes 98308
  218.7 14.7 %all-to-all-start.4 = ((f32[16,16,68]{2,1,0:T(8,128)}), f32[16,16,68]{2,1,0:T(8,128)S(1)}, u32[]{:S(2)}, u32[]{:S(2)}) async-start(f32[16,16,68]{2,1,0:T(8,128)} %pad_maximum_fusion), calls=%async_computation.5 | async-start | bytes 262144 | tf_op jit(solution)/shard_map/all_to_all | solution.py:43
  234.0 11.4 %all-to-all-start.5 = ((f32[16,16,68]{2,1,0:T(8,128)}), f32[16,16,68]{2,1,0:T(8,128)S(1)}, u32[]{:S(2)}, u32[]{:S(2)}) async-start(f32[16,16,68]{2,1,0:T(8,128)} %broadcast_in_dim.7), calls=%async_computation.6 | async-start | bytes 262144 | tf_op jit(solution)/shard_map/all_to_all | solution.py:46
Sparse Core Ops, SparseCore 0:
  34.0 58.0 reduce-scatter.1
  121.7 41.0 all-gather.1

commit v10 on v9

--- a/solution.py
+++ b/solution.py
@@ -46,6 +46,17 @@
     return lax.all_to_all(spread, "rows", split_axis=0, concat_axis=0, tiled=True)
 
 
+def panel_rows_sum(x):
+    groups = lax.axis_size("rows")
+    height, width = x.shape
+    tiles = x.reshape(height // 8, 8, 2, width // 2).transpose(0, 2, 1, 3).reshape(groups, 8, width // 2)
+    scattered = lax.all_to_all(tiles, "rows", split_axis=0, concat_axis=0, tiled=True)
+    own = jnp.sum(scattered, axis=0)
+    spread = jnp.broadcast_to(own[None], scattered.shape)
+    gathered = lax.all_to_all(spread, "rows", split_axis=0, concat_axis=0, tiled=True)
+    return gathered.reshape(height // 8, 2, 8, width // 2).transpose(0, 2, 1, 3).reshape(height, width)
+
+
 def bdot(left, right, dims):
     return lax.dot_general(
         left.astype(jnp.bfloat16), right.astype(jnp.bfloat16), (dims, ((), ())),
@@ -92,7 +103,7 @@
     partial_panel, moved_codes, counts, own_columns, other_columns = lax.optimization_barrier(
         (partial_panel, moved_codes, counts, own_columns, other_columns)
     )
-    cross_panel = rows_sum(partial_panel)
+    cross_panel = panel_rows_sum(partial_panel)
     cross = lax.all_gather(cross_panel, "sub", axis=0, tiled=True)
     width = cross.shape[1]
     frob_scale = jnp.sqrt(jnp.sum(cross * cross)) + frob_eps

time: 256 us -> 254 us (level)
  no operation moved by 1% of the time
where the time goes in v10:
time: 254 us; the launch traced here: 252 us
  waiting for transfers between devices  119 us (47%)
  blocking collectives  46.5 us (18%)
  matrix products  25.6 us (10%)
  starting transfers between devices  25 us (10%)
  between operations  15.1 us (6%)
  other arithmetic  14.5 us (6%)
  local copies, waits for them, and re-layouts  6.36 us (3%)
    all_gather x1, waiting for transfers between devices, body(): cross = lax.all_gather(cross_panel, 'sub', axis=0, tiled=True)  41.2 us
    reduce_scatter x1, waiting for transfers between devices, body(): lax.psum_scatter(partial_t, 'sub', scatter_dimension=1, tiled=True)  37.8 us
    all_gather x1, blocking collectives, body(): table = lax.all_gather(codebook, 'sub', axis=1, tiled=True)  18.6 us
    all_to_all x1, blocking collectives, panel_rows_sum(): lax.all_to_all(tiles, 'rows', split_axis=0, concat_axis=0, tiled=True)  15.3 us
    all_to_all x1, waiting for transfers between devices, body(): lax.all_to_all(rotated, 'sub', split_axis=1, concat_axis=0, tiled=True)  14.8 us
    dot_general x18, matrix products, bdot(): lax.dot_general(left.astype(jnp.bfloat16), right.astype(jnp.bfloat16), (d...  13.4 us
    all_to_all x1, blocking collectives, panel_rows_sum(): lax.all_to_all(spread, 'rows', split_axis=0, concat_axis=0, tiled=True)  12.5 us
    all_to_all x1, waiting for transfers between devices, rows_sum(): lax.all_to_all(x, 'rows', split_axis=0, concat_axis=0, tiled=True)  7.7 us
  transfers between devices with their start and end apart: 12, of which 10 were waited for; matrix products, arithmetic and copies ran while one was open for 6% of the time, Pallas kernels for 0%

profile of v10, /device:TPU:64, one launch (start us, length us, event | category | flops | bytes accessed | tf_op | source)
XLA Modules:
  0.0 251.8 jit_solution(15213216096596442487)
XLA Ops:
  7.2 18.6 %all_gather.6 = bf16[256,1024]{0,1:T(8,128)(2,1)S(1)} all-gather(bf16[256,64]{0,1:T(8,128)(2,1)} %param.5), channel_id=1, replica_groups=mesh['rows'=16,'sub'=16] {'sub'}, dimensions={1}, use_global_device_ids=true | all-gather | bytes 557056 | tf_op jit(solution)/shard_map/all_gather | solution.py:90
  25.8 5.3 %fusion.29 = bf16[64,256,16]{1,2,0:T(8,128)(2,1)S(1)} fusion(bf16[256,64,16]{0,2,1:T(8,128)(2,1)S(1)} %bitcast.89, s32[64,256]{1,0:T(8,128)} %param.4), kind=kOutput, calls=%fused_computation.42 | convolution fusion | flops 138674176 | bytes 1114112 | tf_op jit(solution)/shard_map/mnk,kmj->nmj/dot_general | solution.py:26
  31.2 2.7 %fusion.74 = f32[1024,1024]{0,1:T(8,128)} fusion(bf16[256,1024]{0,1:T(8,128)(2,1)S(1)} %bitcast.82, bf16[256,1024]{1,0:T(8,128)(2,1)S(1)} %copy-done), kind=kOutput, calls=%fused_computation.92 | convolution fusion | flops 536870912 | bytes 5242880 | tf_op jit(solution)/shard_map/dot_general | solution.py:92
  33.9 0.8 copy-done.3
  34.7 0.6 all_to_all.42
  35.4 6.3 %all-to-all-start = ((s32[16,4,256]{2,1,0:T(4,128)}), s32[16,4,256]{2,1,0:T(4,128)S(1)}, u32[]{:S(2)}, u32[]{:S(2)}) async-start(s32[16,4,256]{2,1,0:T(4,128)} %all_to_all.42), calls=%async_computation.1 | async-start | bytes 131072 | tf_op jit(solution)/shard_map/all_to_all | solution.py:89
  42.0 5.4 %all-to-all-done = s32[16,4,256]{2,1,0:T(4,128)S(1)} async-done(((s32[16,4,256]{2,1,0:T(4,128)}), s32[16,4,256]{2,1,0:T(4,128)S(1)}, u32[]{:S(2)}, u32[]{:S(2)}) %all-to-all-start) | async-done | bytes 65568 | tf_op jit(solution)/shard_map/all_to_all | solution.py:89
  47.5 6.9 %convert_reduce_fusion = f32[4,256]{1,0:T(4,128)S(1)} fusion(s32[4,4096]{1,0:T(4,128)S(1)} %bitcast.92), kind=kLoop, calls=%fused_computation.1 | loop fusion | flops 16776192 | bytes 69632 | tf_op jit(solution)/shard_map/reduce_sum | solution.py:97
  54.4 37.8 %reduce-scatter.2.cloned.1.call-done = f32[1024,64]{0,1:T(8,128)} async-done(((f32[1024,1024]{0,1:T(8,128)}), f32[1024,64]{0,1:T(8,128)}) %reduce-scatter.2.cloned.1.call-update) | async-done | bytes 262160 | tf_op jit(solution)/shard_map/reduce_scatter | solution.py:95
  92.1 15.3 %all_to_all.60 = f32[16,8,512]{2,1,0:T(8,128)S(1)} all-to-all(f32[16,8,512]{2,1,0:T(8,128)} %bitcast.91), channel_id=1, replica_groups=mesh['rows'=16,'sub'=16] {'rows'}, dimensions={0} | all-to-all | bytes 524288 | tf_op jit(solution)/shard_map/all_to_all | solution.py:53
  107.5 12.5 %all_to_all.61 = f32[16,8,512]{2,1,0:T(8,128)} all-to-all(f32[16,8,512]{2,1,0:T(8,128)S(1)} %broadcast_in_dim.6), channel_id=1, replica_groups=mesh['rows'=16,'sub'=16] {'rows'}, dimensions={0} | all-to-all | bytes 524288 | tf_op jit(solution)/shard_map/all_to_all | solution.py:56
  120.0 41.2 %all-gather.2.cloned.1.call-done = f32[1024,1024]{1,0:T(8,128)} async-done(((f32[64,1024]{1,0:T(8,128)}), f32[1024,1024]{1,0:T(8,128)}) %all-gather.2.cloned.1.call-update) | async-done | bytes 4194320 | tf_op jit(solution)/shard_map/all_gather | solution.py:107
  161.2 3.9 %multiply_reduce_fusion = f32[]{:T(128)} fusion(f32[1024,1024]{1,0:T(8,128)} %all-gather.2.cloned.1.call-done), kind=kLoop, calls=%fused_computation.9 | loop fusion | flops 2097151 | bytes 4194308 | tf_op jit(solution)/shard_map/reduce_sum | solution.py:109
  165.8 2.9 %fusion.57 = (bf16[8,1,64,1024]{3,2,1,0:T(8,128)(2,1)S(1)}, bf16[8,1,64,1024]{3,2,1,0:T(8,128)(2,1)S(1)}, f32[8,1,64,1024]{3,2,1,0:T(8,128)S(1)}) fusion(f32[]{:T(128)S(6)} %add.81, f32[8,2,64,1024]{3,2,1,0:T(8,128)} %bitcast.76, s32[]{:T(128)S(6)} %select_n.28, s32[]{:T(128)S(6)} %select_n.29), kind=kLoop, calls=%fused_computation.69 | loop fusion | flops 2621440 | bytes 8388620 | tf_op jit(solution)/shard_map/convert_element_type | solution.py:73
  168.6 0.7 fusion.66
  169.4 0.7 fusion.65
  170.4 0.8 fusion.30
  171.6 0.5 collective-permute-done
  172.1 0.5 fusion.33
  172.6 1.3 fusion.67
  174.2 0.7 fusion.69
  175.0 0.6 collective-permute-start.2
  175.5 1.1 collective-permute-done.1
  176.7 0.7 fusion.68
  177.4 0.8 fusion.31
  178.6 0.5 add_convert_fusion.1
  179.2 1.3 fusion.70
  180.8 0.7 fusion.72
  181.9 1.3 collective-permute-done.3
  183.2 0.7 fusion.71
  183.9 0.8 fusion.32
  185.1 0.5 add_convert_fusion
  185.7 1.3 fusion.73
  187.3 0.5 fusion.75
  187.7 2.0 collective-permute-done.5
  189.7 0.5 fusion.28
  190.2 1.0 copy.41
  191.2 6.0 %all-to-all-start.3 = ((bf16[256,16,64]{0,2,1:T(8,128)(2,1)}), bf16[256,16,64]{0,2,1:T(8,128)(2,1)S(1)}, u32[]{:S(2)}, u32[]{:S(2)}) async-start(bf16[256,16,64]{0,2,1:T(8,128)(2,1)} %bitcast.23), calls=%async_computation.4 | async-start | bytes 1048576 | tf_op jit(solution)/shard_map/all_to_all | solution.py:126
  197.3 14.8 %all-to-all-done.3 = bf16[256,16,64]{0,2,1:T(8,128)(2,1)S(1)} async-done(((bf16[256,16,64]{0,2,1:T(8,128)(2,1)}), bf16[256,16,64]{0,2,1:T(8,128)(2,1)S(1)}, u32[]{:S(2)}, u32[]{:S(2)}) %all-to-all-start.3) | async-done | bytes 524320 | tf_op jit(solution)/shard_map/all_to_all | solution.py:126
  212.7 3.2 %fusion.34 = f32[256,4,16]{0,2,1:T(8,128)S(1)} fusion(bf16[4096,4,16]{0,2,1:T(8,128)(2,1)S(1)} %reshape.97, s32[4,4096]{1,0:T(4,128)S(1)} %bitcast.93), kind=kOutput, calls=%fused_computation.47 | convolution fusion | flops 138412032 | bytes 655360 | tf_op jit(solution)/shard_map/mnk,nmj->kmj/dot_general | solution.py:36
  216.3 0.8 pad_maximum_fusion
  217.1 6.8 %all-to-all-start.4 = ((f32[16,16,68]{2,1,0:T(8,128)}), f32[16,16,68]{2,1,0:T(8,128)S(1)}, u32[]{:S(2)}, u32[]{:S(2)}) async-start(f32[16,16,68]{2,1,0:T(8,128)} %pad_maximum_fusion), calls=%async_computation.5 | async-start | bytes 262144 | tf_op jit(solution)/shard_map/all_to_all | solution.py:43
  224.1 7.7 %all-to-all-done.4 = f32[16,16,68]{2,1,0:T(8,128)S(1)} async-done(((f32[16,16,68]{2,1,0:T(8,128)}), f32[16,16,68]{2,1,0:T(8,128)S(1)}, u32[]{:S(2)}, u32[]{:S(2)}) %all-to-all-start.4) | async-done | bytes 69664 | tf_op jit(solution)/shard_map/all_to_all | solution.py:43
  231.8 0.7 broadcast_in_dim.7
  232.4 3.6 %all-to-all-start.5 = ((f32[16,16,68]{2,1,0:T(8,128)}), f32[16,16,68]{2,1,0:T(8,128)S(1)}, u32[]{:S(2)}, u32[]{:S(2)}) async-start(f32[16,16,68]{2,1,0:T(8,128)} %broadcast_in_dim.7), calls=%async_computation.6 | async-start | bytes 262144 | tf_op jit(solution)/shard_map/all_to_all | solution.py:46
  236.0 0.7 dynamic-slice_bitcast_fusion
  236.8 7.1 %all-to-all-done.5 = f32[16,16,68]{2,1,0:T(8,128)S(1)} async-done(((f32[16,16,68]{2,1,0:T(8,128)}), f32[16,16,68]{2,1,0:T(8,128)S(1)}, u32[]{:S(2)}, u32[]{:S(2)}) %all-to-all-start.5) | async-done | bytes 69664 | tf_op jit(solution)/shard_map/all_to_all | solution.py:46
  244.2 0.7 copy.50
  (38 shorter events, 4.9 us)
Async XLA Ops:
  7.2 85.0 %reduce-scatter.2.cloned.1.call-start = ((), (), s32[]{:S(2)}) async-start(), calls=%async_computation.7 | async-start | bytes 4456448 | tf_op jit(solution)/shard_map/reduce_scatter | solution.py:95
  25.8 5.3 %copy-start = (bf16[256,1024]{1,0:T(8,128)(2,1)S(1)}, bf16[256,1024]{1,0:T(8,128)(2,1)}, u32[]{:S(2)}) copy-start(bf16[256,1024]{1,0:T(8,128)(2,1)} %param.3) | copy-start | bytes 1572868
  33.9 0.8 copy-start.3
  35.4 12.1 %all-to-all-start = ((s32[16,4,256]{2,1,0:T(4,128)}), s32[16,4,256]{2,1,0:T(4,128)S(1)}, u32[]{:S(2)}, u32[]{:S(2)}) async-start(s32[16,4,256]{2,1,0:T(4,128)} %all_to_all.42), calls=%async_computation.1 | async-start | bytes 131072 | tf_op jit(solution)/shard_map/all_to_all | solution.py:89
  41.7 119.5 %all-gather.2.cloned.1.call-start = ((), (), s32[]{:S(2)}) async-start(), calls=%async_computation.8 | async-start | bytes 4456448 | tf_op jit(solution)/shard_map/all_gather | solution.py:107
  170.1 2.0 collective-permute-start
  173.9 2.7 %collective-permute-start.1 = (bf16[512,1024]{1,0:T(8,128)(2,1)S(1)}, bf16[512,1024]{1,0:T(8,128)(2,1)S(1)}, u32[]{:S(2)}, u32[]{:S(2)}) collective-permute-start(bf16[512,1024]{1,0:T(8,128)(2,1)S(1)} %get-tuple-element.37), channel_id=1, source_target_pairs={{0,1},{1,0},{2,3},{3,2},{4,5},{5,4},{6,7},{7,6},{8,9},{9,8},{10,11... | collective-permute-start | bytes 3145736 | tf_op jit(solution)/shard_map/ppermute | solution.py:69
  175.0 3.6 %collective-permute-start.2 = (bf16[512,512]{0,1:T(8,128)(2,1)S(1)}, bf16[512,512]{0,1:T(8,128)(2,1)S(1)}, u32[]{:S(2)}, u32[]{:S(2)}) collective-permute-start(bf16[512,512]{0,1:T(8,128)(2,1)S(1)} %get-tuple-element.41), channel_id=1, source_target_pairs={{0,1},{1,0},{2,3},{3,2},{4,5},{5,4},{6,7},{7,6},{8,9},{9,8},{10,11... | collective-permute-start | bytes 1572872 | tf_op jit(solution)/shard_map/ppermute | solution.py:69
  180.4 2.7 %collective-permute-start.3 = (bf16[512,1024]{1,0:T(8,128)(2,1)S(1)}, bf16[512,1024]{1,0:T(8,128)(2,1)S(1)}, u32[]{:S(2)}, u32[]{:S(2)}) collective-permute-start(bf16[512,1024]{1,0:T(8,128)(2,1)S(1)} %get-tuple-element.43), channel_id=1, source_target_pairs={{0,1},{1,0},{2,3},{3,2},{4,5},{5,4},{6,7},{7,6},{8,9},{9,8},{10,11... | collective-permute-start | bytes 3145736 | tf_op jit(solution)/shard_map/ppermute | solution.py:69
  181.5 3.6 %collective-permute-start.4 = (bf16[512,512]{0,1:T(8,128)(2,1)S(1)}, bf16[512,512]{0,1:T(8,128)(2,1)S(1)}, u32[]{:S(2)}, u32[]{:S(2)}) collective-permute-start(bf16[512,512]{0,1:T(8,128)(2,1)S(1)} %get-tuple-element.47), channel_id=1, source_target_pairs={{0,1},{1,0},{2,3},{3,2},{4,5},{5,4},{6,7},{7,6},{8,9},{9,8},{10,11... | collective-permute-start | bytes 1572872 | tf_op jit(solution)/shard_map/ppermute | solution.py:69
  186.9 2.7 %collective-permute-start.5 = (bf16[512,1024]{1,0:T(8,128)(2,1)S(1)}, bf16[512,1024]{1,0:T(8,128)(2,1)S(1)}, u32[]{:S(2)}, u32[]{:S(2)}) collective-permute-start(bf16[512,1024]{1,0:T(8,128)(2,1)S(1)} %get-tuple-element.49), channel_id=1, source_target_pairs={{0,1},{1,0},{2,3},{3,2},{4,5},{5,4},{6,7},{7,6},{8,9},{9,8},{10,11... | collective-permute-start | bytes 3145736 | tf_op jit(solution)/shard_map/ppermute | solution.py:69
  190.1 1.0 copy-start.1
  191.2 20.9 %all-to-all-start.3 = ((bf16[256,16,64]{0,2,1:T(8,128)(2,1)}), bf16[256,16,64]{0,2,1:T(8,128)(2,1)S(1)}, u32[]{:S(2)}, u32[]{:S(2)}) async-start(bf16[256,16,64]{0,2,1:T(8,128)(2,1)} %bitcast.23), calls=%async_computation.4 | async-start | bytes 1048576 | tf_op jit(solution)/shard_map/all_to_all | solution.py:126
  212.6 11.3 %copy-start.2 = (bf16[256,64]{0,1:T(8,128)(2,1)S(1)}, bf16[256,64]{0,1:T(8,128)(2,1)}, u32[]{:S(2)}) copy-start(bf16[256,64]{0,1:T(8,128)(2,1)} %param.5) | copy-start | bytes 98308
  217.1 14.7 %all-to-all-start.4 = ((f32[16,16,68]{2,1,0:T(8,128)}), f32[16,16,68]{2,1,0:T(8,128)S(1)}, u32[]{:S(2)}, u32[]{:S(2)}) async-start(f32[16,16,68]{2,1,0:T(8,128)} %pad_maximum_fusion), calls=%async_computation.5 | async-start | bytes 262144 | tf_op jit(solution)/shard_map/all_to_all | solution.py:43
  232.4 11.4 %all-to-all-start.5 = ((f32[16,16,68]{2,1,0:T(8,128)}), f32[16,16,68]{2,1,0:T(8,128)S(1)}, u32[]{:S(2)}, u32[]{:S(2)}) async-start(f32[16,16,68]{2,1,0:T(8,128)} %broadcast_in_dim.7), calls=%async_computation.6 | async-start | bytes 262144 | tf_op jit(solution)/shard_map/all_to_all | solution.py:46
Sparse Core Ops, SparseCore 0:
  34.0 58.0 reduce-scatter.1
  120.1 41.0 all-gather.1

commit v11 on v10

--- a/solution.py
+++ b/solution.py
@@ -126,8 +126,9 @@
     moved_rows = lax.all_to_all(rotated, "sub", split_axis=1, concat_axis=0, tiled=True)
     code_sums = codeword_sums(moved_codes, moved_rows, table.shape[0])
     sums_width = code_sums.shape[1]
-    totals = rows_sum(jnp.concatenate([code_sums, counts], axis=1))
-    code_sums, counts = totals[:, :sums_width], totals[:, sums_width:]
+    padded_counts = jnp.pad(counts, ((0, 0), (0, sums_width - counts.shape[1])))
+    totals = rows_sum(jnp.concatenate([code_sums, padded_counts], axis=1))
+    code_sums, counts = totals[:, :sums_width], totals[:, sums_width:sums_width + counts.shape[1]]
     own_codebook = codebook.astype(jnp.float32)
     spread = jnp.repeat(counts, own_codebook.shape[1] // counts.shape[1], axis=1)
     new_codebook = (code_sums + own_codebook) / (spread + 1.0)

time: 254 us -> 254 us (level)
  blocking collectives: 46.5 us -> 60.9 us
  waiting for transfers between devices: 119 us -> 111 us
  starting transfers between devices: 25 us -> 18.2 us
    all_to_all x0 -> x1, blocking collectives: none -> 14.4 us  [rows_sum(): lax.all_to_all(x, 'rows', split_axis=0, concat_axis=0, tiled=True)]
    all_to_all x1 -> x0, waiting for transfers between devices: 7.7 us -> none  [rows_sum(): lax.all_to_all(x, 'rows', split_axis=0, concat_axis=0, tiled=True)]
    all_to_all x1 -> x0, starting transfers between devices: 6.81 us -> none  [rows_sum(): lax.all_to_all(x, 'rows', split_axis=0, concat_axis=0, tiled=True)]
  transfers between devices with their start and end apart: 12 -> 11, of which waited for: 10 -> 9; matrix products, arithmetic and copies ran while one was open for 6% -> 6% of each run, Pallas kernels for 0% -> 0%
where the time goes in v11:
time: 254 us; the launch traced here: 251 us
  waiting for transfers between devices  111 us (44%)
  blocking collectives  60.9 us (24%)
  matrix products  25.6 us (10%)
  starting transfers between devices  18.2 us (7%)
  between operations  15.1 us (6%)
  other arithmetic  13.8 us (5%)
  local copies, waits for them, and re-layouts  6.4 us (3%)
    all_gather x1, waiting for transfers between devices, body(): cross = lax.all_gather(cross_panel, 'sub', axis=0, tiled=True)  41.2 us
    reduce_scatter x1, waiting for transfers between devices, body(): lax.psum_scatter(partial_t, 'sub', scatter_dimension=1, tiled=True)  37.8 us
    all_gather x1, blocking collectives, body(): table = lax.all_gather(codebook, 'sub', axis=1, tiled=True)  18.6 us
    all_to_all x1, blocking collectives, panel_rows_sum(): lax.all_to_all(tiles, 'rows', split_axis=0, concat_axis=0, tiled=True)  15.3 us
    all_to_all x1, waiting for transfers between devices, body(): lax.all_to_all(rotated, 'sub', split_axis=1, concat_axis=0, tiled=True)  14.7 us
    all_to_all x1, blocking collectives, rows_sum(): lax.all_to_all(x, 'rows', split_axis=0, concat_axis=0, tiled=True)  14.4 us
    dot_general x18, matrix products, bdot(): lax.dot_general(left.astype(jnp.bfloat16), right.astype(jnp.bfloat16), (d...  13.4 us
    all_to_all x1, blocking collectives, panel_rows_sum(): lax.all_to_all(spread, 'rows', split_axis=0, concat_axis=0, tiled=True)  12.5 us
  transfers between devices with their start and end apart: 11, of which 9 were waited for; matrix products, arithmetic and copies ran while one was open for 6% of the time, Pallas kernels for 0%

profile of v11, /device:TPU:64, one launch (start us, length us, event | category | flops | bytes accessed | tf_op | source)
XLA Modules:
  0.0 250.9 jit_solution(4950489378078883166)
XLA Ops:
  7.2 18.6 %all_gather.6 = bf16[256,1024]{0,1:T(8,128)(2,1)S(1)} all-gather(bf16[256,64]{0,1:T(8,128)(2,1)} %param.5), channel_id=1, replica_groups=mesh['rows'=16,'sub'=16] {'sub'}, dimensions={1}, use_global_device_ids=true | all-gather | bytes 557056 | tf_op jit(solution)/shard_map/all_gather | solution.py:90
  25.8 5.3 %fusion.29 = bf16[64,256,16]{1,2,0:T(8,128)(2,1)S(1)} fusion(bf16[256,64,16]{0,2,1:T(8,128)(2,1)S(1)} %bitcast.89, s32[64,256]{1,0:T(8,128)} %param.4), kind=kOutput, calls=%fused_computation.42 | convolution fusion | flops 138674176 | bytes 1114112 | tf_op jit(solution)/shard_map/mnk,kmj->nmj/dot_general | solution.py:26
  31.2 2.7 %fusion.74 = f32[1024,1024]{0,1:T(8,128)} fusion(bf16[256,1024]{0,1:T(8,128)(2,1)S(1)} %bitcast.82, bf16[256,1024]{1,0:T(8,128)(2,1)S(1)} %copy-done), kind=kOutput, calls=%fused_computation.92 | convolution fusion | flops 536870912 | bytes 5242880 | tf_op jit(solution)/shard_map/dot_general | solution.py:92
  33.9 0.8 copy-done.3
  34.8 0.6 all_to_all.42
  35.4 6.3 %all-to-all-start = ((s32[16,4,256]{2,1,0:T(4,128)}), s32[16,4,256]{2,1,0:T(4,128)S(1)}, u32[]{:S(2)}, u32[]{:S(2)}) async-start(s32[16,4,256]{2,1,0:T(4,128)} %all_to_all.42), calls=%async_computation.1 | async-start | bytes 131072 | tf_op jit(solution)/shard_map/all_to_all | solution.py:89
  42.1 5.4 %all-to-all-done = s32[16,4,256]{2,1,0:T(4,128)S(1)} async-done(((s32[16,4,256]{2,1,0:T(4,128)}), s32[16,4,256]{2,1,0:T(4,128)S(1)}, u32[]{:S(2)}, u32[]{:S(2)}) %all-to-all-start) | async-done | bytes 65568 | tf_op jit(solution)/shard_map/all_to_all | solution.py:89
  47.5 6.9 %convert_reduce_fusion = f32[4,256]{1,0:T(4,128)S(1)} fusion(s32[4,4096]{1,0:T(4,128)S(1)} %bitcast.92), kind=kLoop, calls=%fused_computation.1 | loop fusion | flops 16776192 | bytes 69632 | tf_op jit(solution)/shard_map/reduce_sum | solution.py:97
  54.4 37.8 %reduce-scatter.2.cloned.1.call-done = f32[1024,64]{0,1:T(8,128)} async-done(((f32[1024,1024]{0,1:T(8,128)}), f32[1024,64]{0,1:T(8,128)}) %reduce-scatter.2.cloned.1.call-update) | async-done | bytes 262160 | tf_op jit(solution)/shard_map/reduce_scatter | solution.py:95
  92.1 15.3 %all_to_all.60 = f32[16,8,512]{2,1,0:T(8,128)S(1)} all-to-all(f32[16,8,512]{2,1,0:T(8,128)} %bitcast.91), channel_id=1, replica_groups=mesh['rows'=16,'sub'=16] {'rows'}, dimensions={0} | all-to-all | bytes 524288 | tf_op jit(solution)/shard_map/all_to_all | solution.py:53
  107.5 12.5 %all_to_all.61 = f32[16,8,512]{2,1,0:T(8,128)} all-to-all(f32[16,8,512]{2,1,0:T(8,128)S(1)} %broadcast_in_dim.6), channel_id=1, replica_groups=mesh['rows'=16,'sub'=16] {'rows'}, dimensions={0} | all-to-all | bytes 524288 | tf_op jit(solution)/shard_map/all_to_all | solution.py:56
  120.0 41.2 %all-gather.2.cloned.1.call-done = f32[1024,1024]{1,0:T(8,128)} async-done(((f32[64,1024]{1,0:T(8,128)}), f32[1024,1024]{1,0:T(8,128)}) %all-gather.2.cloned.1.call-update) | async-done | bytes 4194320 | tf_op jit(solution)/shard_map/all_gather | solution.py:107
  161.2 3.9 %multiply_reduce_fusion = f32[]{:T(128)} fusion(f32[1024,1024]{1,0:T(8,128)} %all-gather.2.cloned.1.call-done), kind=kLoop, calls=%fused_computation.9 | loop fusion | flops 2097151 | bytes 4194308 | tf_op jit(solution)/shard_map/reduce_sum | solution.py:109
  165.8 2.9 %fusion.57 = (bf16[8,1,64,1024]{3,2,1,0:T(8,128)(2,1)S(1)}, bf16[8,1,64,1024]{3,2,1,0:T(8,128)(2,1)S(1)}, f32[8,1,64,1024]{3,2,1,0:T(8,128)S(1)}) fusion(f32[]{:T(128)S(6)} %add.83, f32[8,2,64,1024]{3,2,1,0:T(8,128)} %bitcast.76, s32[]{:T(128)S(6)} %select_n.28, s32[]{:T(128)S(6)} %select_n.29), kind=kLoop, calls=%fused_computation.69 | loop fusion | flops 2621440 | bytes 8388620 | tf_op jit(solution)/shard_map/convert_element_type | solution.py:73
  168.6 0.7 fusion.66
  169.4 0.7 fusion.65
  170.4 0.8 fusion.30
  171.2 0.4 fusion.76
  171.7 0.5 collective-permute-done
  172.1 0.5 fusion.33
  172.6 1.3 fusion.67
  174.3 0.7 fusion.69
  175.0 0.6 collective-permute-start.2
  175.6 1.1 collective-permute-done.1
  176.7 0.7 fusion.68
  177.4 0.8 fusion.31
  178.7 0.5 add_convert_fusion.1
  179.2 1.3 fusion.70
  180.8 0.7 fusion.72
  181.9 1.3 collective-permute-done.3
  183.2 0.7 fusion.71
  183.9 0.8 fusion.32
  184.7 0.4 fusion.78
  185.2 0.5 add_convert_fusion
  185.7 1.3 fusion.73
  187.3 0.5 fusion.75
  187.7 2.0 collective-permute-done.5
  189.7 0.5 fusion.28
  190.2 1.0 copy.43
  191.2 6.0 %all-to-all-start.3 = ((bf16[256,16,64]{0,2,1:T(8,128)(2,1)}), bf16[256,16,64]{0,2,1:T(8,128)(2,1)S(1)}, u32[]{:S(2)}, u32[]{:S(2)}) async-start(bf16[256,16,64]{0,2,1:T(8,128)(2,1)} %bitcast.23), calls=%async_computation.4 | async-start | bytes 1048576 | tf_op jit(solution)/shard_map/all_to_all | solution.py:126
  197.4 14.7 %all-to-all-done.3 = bf16[256,16,64]{0,2,1:T(8,128)(2,1)S(1)} async-done(((bf16[256,16,64]{0,2,1:T(8,128)(2,1)}), bf16[256,16,64]{0,2,1:T(8,128)(2,1)S(1)}, u32[]{:S(2)}, u32[]{:S(2)}) %all-to-all-start.3) | async-done | bytes 524320 | tf_op jit(solution)/shard_map/all_to_all | solution.py:126
  212.7 3.2 %fusion.34 = f32[256,4,16]{0,2,1:T(8,128)S(1)} fusion(bf16[4096,4,16]{0,2,1:T(8,128)(2,1)S(1)} %reshape.97, s32[4,4096]{1,0:T(4,128)S(1)} %bitcast.93), kind=kOutput, calls=%fused_computation.47 | convolution fusion | flops 138412032 | bytes 655360 | tf_op jit(solution)/shard_map/mnk,nmj->kmj/dot_general | solution.py:36
  216.4 14.4 %all_to_all.62 = f32[16,16,128]{2,1,0:T(8,128)S(1)} all-to-all(f32[16,16,128]{2,1,0:T(8,128)S(1)} %pad_maximum_fusion), channel_id=1, replica_groups=mesh['rows'=16,'sub'=16] {'rows'}, dimensions={0} | all-to-all | bytes 262144 | tf_op jit(solution)/shard_map/all_to_all | solution.py:43
  230.9 0.7 broadcast_in_dim.7
  231.6 3.6 %all-to-all-start.5 = ((f32[16,16,128]{2,1,0:T(8,128)}), f32[16,16,128]{2,1,0:T(8,128)S(1)}, u32[]{:S(2)}, u32[]{:S(2)}) async-start(f32[16,16,128]{2,1,0:T(8,128)} %broadcast_in_dim.7), calls=%async_computation.6 | async-start | bytes 262144 | tf_op jit(solution)/shard_map/all_to_all | solution.py:46
  235.3 0.7 dynamic-slice_bitcast_fusion
  236.1 7.0 %all-to-all-done.5 = f32[16,16,128]{2,1,0:T(8,128)S(1)} async-done(((f32[16,16,128]{2,1,0:T(8,128)}), f32[16,16,128]{2,1,0:T(8,128)S(1)}, u32[]{:S(2)}, u32[]{:S(2)}) %all-to-all-start.5) | async-done | bytes 131104 | tf_op jit(solution)/shard_map/all_to_all | solution.py:46
  243.4 0.7 copy.52
  (38 shorter events, 4.1 us)
Async XLA Ops:
  7.2 85.0 %reduce-scatter.2.cloned.1.call-start = ((), (), s32[]{:S(2)}) async-start(), calls=%async_computation.7 | async-start | bytes 4456448 | tf_op jit(solution)/shard_map/reduce_scatter | solution.py:95
  25.8 5.3 %copy-start = (bf16[256,1024]{1,0:T(8,128)(2,1)S(1)}, bf16[256,1024]{1,0:T(8,128)(2,1)}, u32[]{:S(2)}) copy-start(bf16[256,1024]{1,0:T(8,128)(2,1)} %param.3) | copy-start | bytes 1572868
  33.9 0.8 copy-start.3
  35.4 12.1 %all-to-all-start = ((s32[16,4,256]{2,1,0:T(4,128)}), s32[16,4,256]{2,1,0:T(4,128)S(1)}, u32[]{:S(2)}, u32[]{:S(2)}) async-start(s32[16,4,256]{2,1,0:T(4,128)} %all_to_all.42), calls=%async_computation.1 | async-start | bytes 131072 | tf_op jit(solution)/shard_map/all_to_all | solution.py:89
  41.7 119.5 %all-gather.2.cloned.1.call-start = ((), (), s32[]{:S(2)}) async-start(), calls=%async_computation.8 | async-start | bytes 4456448 | tf_op jit(solution)/shard_map/all_gather | solution.py:107
  170.1 2.0 collective-permute-start
  173.9 2.7 %collective-permute-start.1 = (bf16[512,1024]{1,0:T(8,128)(2,1)S(1)}, bf16[512,1024]{1,0:T(8,128)(2,1)S(1)}, u32[]{:S(2)}, u32[]{:S(2)}) collective-permute-start(bf16[512,1024]{1,0:T(8,128)(2,1)S(1)} %get-tuple-element.37), channel_id=1, source_target_pairs={{0,1},{1,0},{2,3},{3,2},{4,5},{5,4},{6,7},{7,6},{8,9},{9,8},{10,11... | collective-permute-start | bytes 3145736 | tf_op jit(solution)/shard_map/ppermute | solution.py:69
  175.0 3.6 %collective-permute-start.2 = (bf16[512,512]{0,1:T(8,128)(2,1)S(1)}, bf16[512,512]{0,1:T(8,128)(2,1)S(1)}, u32[]{:S(2)}, u32[]{:S(2)}) collective-permute-start(bf16[512,512]{0,1:T(8,128)(2,1)S(1)} %get-tuple-element.41), channel_id=1, source_target_pairs={{0,1},{1,0},{2,3},{3,2},{4,5},{5,4},{6,7},{7,6},{8,9},{9,8},{10,11... | collective-permute-start | bytes 1572872 | tf_op jit(solution)/shard_map/ppermute | solution.py:69
  180.5 2.7 %collective-permute-start.3 = (bf16[512,1024]{1,0:T(8,128)(2,1)S(1)}, bf16[512,1024]{1,0:T(8,128)(2,1)S(1)}, u32[]{:S(2)}, u32[]{:S(2)}) collective-permute-start(bf16[512,1024]{1,0:T(8,128)(2,1)S(1)} %get-tuple-element.43), channel_id=1, source_target_pairs={{0,1},{1,0},{2,3},{3,2},{4,5},{5,4},{6,7},{7,6},{8,9},{9,8},{10,11... | collective-permute-start | bytes 3145736 | tf_op jit(solution)/shard_map/ppermute | solution.py:69
  181.5 3.6 %collective-permute-start.4 = (bf16[512,512]{0,1:T(8,128)(2,1)S(1)}, bf16[512,512]{0,1:T(8,128)(2,1)S(1)}, u32[]{:S(2)}, u32[]{:S(2)}) collective-permute-start(bf16[512,512]{0,1:T(8,128)(2,1)S(1)} %get-tuple-element.47), channel_id=1, source_target_pairs={{0,1},{1,0},{2,3},{3,2},{4,5},{5,4},{6,7},{7,6},{8,9},{9,8},{10,11... | collective-permute-start | bytes 1572872 | tf_op jit(solution)/shard_map/ppermute | solution.py:69
  187.0 2.7 %collective-permute-start.5 = (bf16[512,1024]{1,0:T(8,128)(2,1)S(1)}, bf16[512,1024]{1,0:T(8,128)(2,1)S(1)}, u32[]{:S(2)}, u32[]{:S(2)}) collective-permute-start(bf16[512,1024]{1,0:T(8,128)(2,1)S(1)} %get-tuple-element.49), channel_id=1, source_target_pairs={{0,1},{1,0},{2,3},{3,2},{4,5},{5,4},{6,7},{7,6},{8,9},{9,8},{10,11... | collective-permute-start | bytes 3145736 | tf_op jit(solution)/shard_map/ppermute | solution.py:69
  190.2 1.0 copy-start.1
  191.2 20.9 %all-to-all-start.3 = ((bf16[256,16,64]{0,2,1:T(8,128)(2,1)}), bf16[256,16,64]{0,2,1:T(8,128)(2,1)S(1)}, u32[]{:S(2)}, u32[]{:S(2)}) async-start(bf16[256,16,64]{0,2,1:T(8,128)(2,1)} %bitcast.23), calls=%async_computation.4 | async-start | bytes 1048576 | tf_op jit(solution)/shard_map/all_to_all | solution.py:126
  215.9 19.3 %copy-start.2 = (bf16[256,64]{0,1:T(8,128)(2,1)S(1)}, bf16[256,64]{0,1:T(8,128)(2,1)}, u32[]{:S(2)}) copy-start(bf16[256,64]{0,1:T(8,128)(2,1)} %param.5) | copy-start | bytes 98308
  231.6 11.4 %all-to-all-start.5 = ((f32[16,16,128]{2,1,0:T(8,128)}), f32[16,16,128]{2,1,0:T(8,128)S(1)}, u32[]{:S(2)}, u32[]{:S(2)}) async-start(f32[16,16,128]{2,1,0:T(8,128)} %broadcast_in_dim.7), calls=%async_computation.6 | async-start | bytes 262144 | tf_op jit(solution)/shard_map/all_to_all | solution.py:46
Sparse Core Ops, SparseCore 0:
  34.1 58.0 reduce-scatter.1
  120.2 41.0 all-gather.1
